TPU v7x, 32 devices: a whole 2x2x4 slice. The times are simulated.
32 devices in a mesh: dp: 4 (over y, x), seq: 8 (over z, core).
Axes of the slice: x: 2, y: 2, z: 4, core: 2. Of those that a mesh axis runs over, the one named last changes fastest.
Arguments:
- hidden_in: bfloat16 [8192, 2048], P(('dp', 'seq')), parts along dimension 0, may hold values from -6 to 6
- lin_query: bfloat16 [8192, 1024], P(('dp', 'seq')), parts along dimension 0, may hold values from -6 to 6
- lin_key: bfloat16 [8192, 256], P(('dp', 'seq')), parts along dimension 0, may hold values from -6 to 6
- lin_value: bfloat16 [8192, 256], P(('dp', 'seq')), parts along dimension 0, may hold values from -6 to 6
- lin_gain: float32 [1024], replicated, may hold values from 0.1 to 1.9
- lin_out_weight: bfloat16 [1024, 2048], replicated, may hold values from -0.1875 to 0.1875
- soft_gain: float32 [2048], replicated, may hold values from 0.1 to 1.9
- soft_wq: bfloat16 [2048, 1024], replicated, may hold values from -4 to 4
- soft_wk: bfloat16 [2048, 256], replicated, may hold values from -4 to 4
- soft_wv: bfloat16 [2048, 256], replicated, may hold values from -0.125 to 0.125
- pattern: int32 [2, 16, 18], replicated, may hold values from 0 to 15, as said below
Outputs:
- attended: bfloat16 [8192, 1024], P(('dp', 'seq')), parts along dimension 0
There are 4 independent parts, one for each index of `dp`. A program takes and returns all parts, laid end to end along the dimension named above; an argument that names none is the same for every part. Nothing has to cross between parts.
Inputs may be any that keep to these rules, and one draw needn't show every extreme that they name: pattern[g, b, 0] = b and pattern[g, b, 1] = max(b - 1, 0); every entry of row b lies between 0 and b; for each key-value head and the 2 query blocks held by one device, the entries in slots 2 to 17 of those rows that lie in another device's tokens all name the same key block of that device.
All inputs are finite; a program needn't handle non-finite values.
Results may differ from a plain program's by a relative error of at most 0.035.
Values may be sent and summed in bfloat16 or wider, within the bound.
No kernel may reach another device: no remote copies, remote signals or barrier semaphores. Data moves between devices by JAX's collectives and lax.ppermute only.
A program may use at most 128 MiB of HBM per device.

v0:
```python
import jax
import jax.numpy as jnp
from jax import lax
from jax.sharding import PartitionSpec as P

HEAD_DIM = 128
HEADS = 8
KV_HEADS = 2
BLOCK = 128


EPSILON = 1e-06


def carried_in(shard, axis, combine, identity):
    devices, position = (lax.axis_size(axis), lax.axis_index(axis))
    everything = lax.all_gather(shard, axis)
    start = jnp.broadcast_to(jnp.asarray(identity, shard.dtype), shard.shape)

    def lap(k, before):
        reached = k < position
        new = combine(before, everything[k])
        return jnp.where(reached, new, before)

    return lax.fori_loop(0, devices, lap, start)


def add_states(earlier, later):
    return earlier + later


def local(
    hidden_in,
    lin_query,
    lin_key,
    lin_value,
    lin_gain,
    lin_out_weight,
    soft_gain,
    soft_wq,
    soft_wk,
    soft_wv,
    pattern,
):
    tok_count = hidden_in.shape[0]
    local_blocks = tok_count // BLOCK
    per_group = HEADS // KV_HEADS
    listed = pattern.shape[2]
    position = lax.axis_index("seq")
    query_blocks = lin_query.reshape(local_blocks, BLOCK, KV_HEADS, per_group, HEAD_DIM)
    key_blocks = lin_key.reshape(local_blocks, BLOCK, KV_HEADS, HEAD_DIM)
    value_blocks = lin_value.reshape(local_blocks, BLOCK, KV_HEADS, HEAD_DIM)
    block_states = jnp.einsum(
        "ntgd,ntge->ngde", key_blocks, value_blocks, preferred_element_type=jnp.float32
    )
    device_state = jnp.sum(block_states, axis=0)
    carried = carried_in(device_state, "seq", add_states, jnp.zeros_like(device_state))
    running = jnp.concatenate(
        [jnp.zeros_like(block_states[:1]), jnp.cumsum(block_states[:-1], axis=0)], axis=0
    )
    before = carried[None] + running
    inter = jnp.einsum(
        "ntgpd,ngde->ntgpe",
        query_blocks.astype(jnp.float32),
        before,
        precision=lax.Precision.HIGHEST,
    )
    rows_here = jnp.arange(BLOCK)
    causal = rows_here[:, None] >= rows_here[None, :]
    local_scores = jnp.einsum(
        "ntgpd,nsgd->ngpts", query_blocks, key_blocks, preferred_element_type=jnp.float32
    )
    local_scores = jnp.where(causal, local_scores, 0.0).astype(jnp.bfloat16)
    intra = jnp.einsum(
        "ngpts,nsge->ntgpe", local_scores, value_blocks, preferred_element_type=jnp.float32
    )
    mixed = (inter + intra).reshape(tok_count, HEADS, HEAD_DIM)
    normed = (
        mixed
        * lax.rsqrt(jnp.mean(mixed * mixed, axis=-1, keepdims=True) + EPSILON)
        * lin_gain.reshape(HEADS, HEAD_DIM)
    )
    normed = normed.reshape(tok_count, HEADS * HEAD_DIM).astype(jnp.bfloat16)
    branch = jnp.dot(normed, lin_out_weight, preferred_element_type=jnp.float32)
    residual = (hidden_in.astype(jnp.float32) + branch).astype(jnp.bfloat16)
    widened = residual.astype(jnp.float32)
    layer_in = (
        widened
        * lax.rsqrt(jnp.mean(widened * widened, axis=-1, keepdims=True) + EPSILON)
        * soft_gain
    ).astype(jnp.bfloat16)
    soft_query = jnp.dot(layer_in, soft_wq, preferred_element_type=jnp.float32).astype(jnp.bfloat16)
    soft_key = jnp.dot(layer_in, soft_wk, preferred_element_type=jnp.float32).astype(jnp.bfloat16)
    soft_value = jnp.dot(layer_in, soft_wv, preferred_element_type=jnp.float32).astype(jnp.bfloat16)
    packed = jnp.concatenate(
        [
            soft_key.reshape(tok_count, KV_HEADS, HEAD_DIM),
            soft_value.reshape(tok_count, KV_HEADS, HEAD_DIM),
        ],
        axis=-1,
    )
    mine = lax.dynamic_slice_in_dim(pattern, position * local_blocks, local_blocks, 1)
    whole = lax.all_gather(packed, "seq", axis=0, tiled=True)
    table = whole.reshape(-1, BLOCK, KV_HEADS, 2 * HEAD_DIM)
    group_ids = jnp.arange(KV_HEADS)[:, None, None]
    tiles = table[mine, :, group_ids, :]
    tiles = tiles.reshape(KV_HEADS, local_blocks, listed * BLOCK, 2 * HEAD_DIM)
    keys_tile = tiles[..., :HEAD_DIM]
    values_tile = tiles[..., HEAD_DIM:]
    soft_blocks = soft_query.reshape(local_blocks, BLOCK, KV_HEADS, per_group, HEAD_DIM)
    scores = jnp.einsum(
        "ntgpd,gnkd->gnptk", soft_blocks, keys_tile, preferred_element_type=jnp.float32
    ) * HEAD_DIM ** (-0.5)
    same = mine[..., :, None] == mine[..., None, :]
    earlier = jnp.arange(listed)[None, :] < jnp.arange(listed)[:, None]
    repeated = jnp.any(same & earlier, axis=-1)
    live = jnp.repeat(jnp.logical_not(repeated), BLOCK, axis=-1)
    columns = jnp.arange(listed * BLOCK)
    causal_keys = (columns[None, :] >= BLOCK) | (columns[None, :] <= rows_here[:, None])
    allowed = live[:, :, None, None, :] & causal_keys[None, None, None]
    highest = jnp.max(jnp.where(allowed, scores, -jnp.inf), axis=-1, keepdims=True)
    weights = jnp.where(allowed, jnp.exp(scores - highest), 0.0)
    total = jnp.sum(weights, axis=-1, keepdims=True)
    probs = (weights / total).astype(jnp.bfloat16)
    attended = jnp.einsum(
        "gnptk,gnke->ntgpe", probs, values_tile, preferred_element_type=jnp.float32
    )
    return attended.reshape(tok_count, HEADS * HEAD_DIM).astype(jnp.bfloat16)


def solution(mesh):
    in_specs = (
        P(("dp", "seq"), None),
        P(("dp", "seq"), None),
        P(("dp", "seq"), None),
        P(("dp", "seq"), None),
        P(),
        P(),
        P(),
        P(),
        P(),
        P(),
        P(),
    )
    out_specs = P(("dp", "seq"), None)
    return jax.shard_map(local, mesh=mesh, in_specs=in_specs, out_specs=out_specs, check_vma=False)
```

profile of v0, /device:TPU:0, one launch (start us, length us, event | category | flops | bytes accessed | tf_op | source)
XLA Modules:
  0.0 125.7 jit_solution(3397042050817061094)
XLA Ops:
  6.5 0.0 copy-start
  6.5 0.0 all-gather.6.cloned.1.call-start
  6.5 1.0 reshape.120
  7.6 0.9 reshape.121
  8.5 0.9 fusion.61
  9.4 0.0 all-gather.6.cloned.1.call-update
  9.4 0.0 all-gather.4.cloned.1.call-start
  9.5 1.4 %reshape.122 = bf16[2,128,2,4,128]{4,3,2,1,0:T(4,128)(2,1)S(1)} reshape(bf16[256,1024]{1,0:T(8,128)(2,1)} %param.14) | data formatting | bytes 1048576 | tf_op jit(solution)/shard_map/reshape | solution.py:50
  10.9 23.6 %all-gather.6.cloned.1.call-done = f32[16,128,128]{2,1,0:T(8,128)} async-done(((f32[2,128,128]{2,1,0:T(8,128)}), f32[16,128,128]{2,1,0:T(8,128)}) %all-gather.6.cloned.1.call-update) | async-done | bytes 1048592 | tf_op jit(solution)/shard_map/all_gather | solution.py:17
  34.5 7.8 %while.14 = (s32[]{:T(128)}, f32[2,128,128]{2,1,0:T(8,128)S(1)}, s32[]{:T(128)}, f32[8,2,128,128]{3,2,1,0:T(8,128)}, s32[]{:T(128)}, /*index=5*/s32[]{:T(128)}) while((s32[]{:T(128)}, f32[2,128,128]{2,1,0:T(8,128)S(1)}, s32[]{:T(128)}, f32[8,2,128,128]{3,2,1,0:T(8,128)}, s32[]{:T(128)}, /*index=5*/s32[]{:T(128)}) %tuple.44), condition=%wide.region_2.3_spmd.clone, body=%wide.region_1.2_spmd.clone.sunk | while | flops 98308 | bytes 393317 | solution.py:25
  34.5 0.9 add_select_fusion.2
  35.5 0.9 add_select_fusion.2
  36.5 0.9 add_select_fusion.2
  37.5 0.9 add_select_fusion.2
  38.4 0.9 add_select_fusion.2
  39.4 0.9 add_select_fusion.2
  40.4 0.9 add_select_fusion.2
  41.4 0.9 add_select_fusion.2
  42.3 0.6 convolution_bitcast_fusion.2
  42.9 0.0 copy-start.5
  43.0 1.5 %multiply_reduce_fusion = (f32[2,128,2,4]{1,3,2,0:T(4,128)S(1)}, f32[2,128,2,4,128]{1,4,3,2,0:T(8,128)}) fusion(f32[2,128,2,4,128]{1,4,3,2,0:T(8,128)S(1)} %convolution_bitcast_fusion.2, pred[128,128]{0,1:T(8,128)(4,1)S(1)} %iota_compare_fusion.1, bf16[2,128,2,4,128]{4,3,2,1,0:T(4,128)(2,1)S(1)} %reshape.122, bf16[2,128,2,128,1]{3,2,1,0,4:T(2,128)(2,1)S(1)} %bitcast.81, ...), kind=kOutput, calls=%fused_computation.43 | convolution fusion | flops 135526400 | bytes 2908160 | tf_op jit(solution)/shard_map/ngpts,nsge->ntgpe/dot_general | solution.py:74
  44.4 0.1 copy.74
  44.6 1.7 %copy.73 = f32[2,128,2,4,128]{4,3,2,1,0:T(4,128)S(1)} copy(f32[2,128,2,4,128]{1,4,3,2,0:T(8,128)} %get-tuple-element.113) | data formatting | bytes 2097152 | tf_op jit(solution)/shard_map/add | solution.py:77
  46.2 0.4 reshape.123
  46.7 0.3 mul.56
  47.0 0.0 copy-done.5
  47.0 0.0 copy-start.4
  47.0 0.0 copy-start.3
  47.0 4.0 %fusion.13 = (f32[256]{0:T(256)S(1)}, bf16[256,2048]{1,0:T(8,128)(2,1)S(1)}) fusion(bf16[1024,2048]{1,0:T(8,128)(2,1)} %param.18, f32[256,1024]{1,0:T(8,128)S(1)} %reshape.123, f32[32,8,8,128]{3,2,1,0:T(8,128)S(1)} %bitcast.83, f32[1024]{0:T(1024)S(1)} %copy-done.5, bf16[256,2048]{1,0:T(8,128)(2,1)} %param.13), kind=kOutput, calls=%fused_computation.24 | convolution fusion | flops 1077673728 | bytes 8393728 | tf_op jit(solution)/shard_map/dot_general | solution.py:84
  51.0 0.0 copy-start.6
  51.1 0.0 copy-done
  51.1 0.0 copy-done.4
  51.1 0.7 convolution_convert_fusion.1
  51.8 0.3 copy-done.6
  52.0 0.0 copy-start.7
  52.0 0.1 copy.76
  52.2 0.0 copy-done.3
  52.2 2.0 %convolution_convert_fusion.2 = bf16[256,256]{0,1:T(8,128)(2,1)S(1)} fusion(bf16[2048,256]{1,0:T(8,128)(2,1)S(1)} %copy-done.3, bf16[256,2048]{1,0:T(8,128)(2,1)} %copy-done.6, f32[2048]{0:T(1024)S(1)} %copy-done.4, f32[256]{0:T(256)S(1)} %add_rsqrt_fusion.1), kind=kOutput, calls=%fused_computation.39 | convolution fusion | flops 270598144 | bytes 2237440 | tf_op jit(solution)/shard_map/dot_general | solution.py:93
  54.1 0.1 copy.75
  54.3 0.7 pad_maximum_fusion
  55.0 0.0 all-gather.4.cloned.1.call-update
  55.0 0.7 fusion.53
  55.7 0.1 reshape.129
  55.8 0.2 and_reduce_fusion
  56.1 0.1 broadcast_in_dim.64
  56.2 1.2 fusion.29
  57.5 3.2 %broadcast_and_fusion = pred[2,2,128,2304]{2,3,1,0:T(8,128)(4,1)} fusion(pred[128,2304]{0,1:T(8,128)(4,1)S(1)} %fusion.29, pred[2,2,2304]{2,1,0:T(4,128)(4,1)S(1)} %and.31), kind=kLoop, calls=%fused_computation.23 | loop fusion | flops 1179648 | bytes 1483776 | tf_op jit(solution)/shard_map/and | solution.py:120
  60.6 0.0 copy-done.7
  60.6 3.6 %convolution_convert_fusion = bf16[256,1024]{1,0:T(8,128)(2,1)S(1)} fusion(bf16[2048,1024]{1,0:T(8,128)(2,1)} %param.20, bf16[256,2048]{1,0:T(8,128)(2,1)S(1)} %copy-done.7, f32[2048]{0:T(1024)S(1)} %copy-done.4, f32[256]{0:T(256)S(1)} %add_rsqrt_fusion.1), kind=kOutput, calls=%fused_computation.34 | convolution fusion | flops 1076101120 | bytes 5776384 | tf_op jit(solution)/shard_map/dot_general | solution.py:92
  64.3 0.4 reshape.128
  64.6 19.3 %all-gather.4.cloned.1.call-done = bf16[2048,2,256]{2,0,1:T(8,128)(2,1)} async-done(((bf16[256,2,256]{2,0,1:T(8,128)(2,1)}), bf16[2048,2,256]{2,0,1:T(8,128)(2,1)}) %all-gather.4.cloned.1.call-update) | async-done | bytes 2097168 | tf_op jit(solution)/shard_map/all_gather | solution.py:103
  84.0 1.7 %copy.77 = bf16[16,128,2,256]{3,1,2,0:T(8,128)(2,1)S(1)} copy(bf16[16,128,2,256]{3,1,0,2:T(8,128)(2,1)} %bitcast.80) | data formatting | bytes 4194304 | tf_op jit(solution)/shard_map/reshape | solution.py:104
  85.7 7.0 %gather_fusion = bf16[72,128,256]{2,1,0:T(8,128)(2,1)} fusion(bf16[16,128,2,256]{3,1,2,0:T(8,128)(2,1)S(1)} %copy.77, s32[72]{0:T(128)S(1)} %reshape.129), kind=kCustom, calls=%fused_computation | custom fusion | bytes 9437760 | tf_op jit(solution)/shard_map/gather | solution.py:106
  92.7 0.0 copy-start.2
  92.7 4.4 %fusion.11 = f32[2,2,2304,128,4]{3,2,4,1,0:T(8,128)S(1)} fusion(bf16[2,2,2304,256]{3,2,1,0:T(8,128)(2,1)} %bitcast.78, bf16[2,128,2,4,128]{4,3,2,1,0:T(4,128)(2,1)S(1)} %reshape.128), kind=kOutput, calls=%fused_computation.20 | convolution fusion | flops 1207959552 | bytes 21757952 | tf_op jit(solution)/shard_map/ntgpd,gnkd->gnptk/dot_general | solution.py:111
  97.1 0.0 copy-done.2
  97.1 11.5 %fusion.66 = (f32[2,2,4,128]{3,2,1,0:T(4,128)S(1)}, f32[2,2,4,128,2304]{3,4,2,1,0:T(8,128)}) fusion(f32[2,2,2304,128,4]{3,2,4,1,0:T(8,128)S(1)} %fusion.11, pred[2,2,128,2304]{2,3,1,0:T(8,128)(4,1)S(1)} %copy-done.2), kind=kOutput, calls=%fused_computation.77 | output fusion | flops 28313856 | bytes 38936576 | tf_op jit(solution)/shard_map/sub | solution.py:122
  108.6 0.0 copy-start.1
  108.6 8.8 %fusion.24 = bf16[2,128,2,4,128]{1,4,3,2,0:T(8,128)(2,1)S(1)} fusion(f32[2,2,4,128,2304]{3,4,2,1,0:T(8,128)} %get-tuple-element.117, f32[2,2,4,128]{3,2,1,0:T(4,128)S(1)} %get-tuple-element.116, bf16[2,2,2304,256]{3,2,1,0:T(8,128)(2,1)} %bitcast.79), kind=kOutput, calls=%fused_computation.35 | convolution fusion | flops 1217658880 | bytes 21766144 | tf_op jit(solution)/shard_map/gnptk,gnke->ntgpe/dot_general | solution.py:125
  117.4 0.3 copy.81
  117.7 1.2 convert_element_type.52
  118.8 0.0 copy-done.1
  (9 shorter events, 0.1 us)
Async XLA Ops:
  6.5 44.5 %copy-start = (bf16[2048,256]{1,0:T(8,128)(2,1)S(1)}, bf16[2048,256]{1,0:T(8,128)(2,1)}, u32[]{:S(2)}) copy-start(bf16[2048,256]{1,0:T(8,128)(2,1)} %param.22) | copy-start | bytes 3145732
  6.5 28.0 %all-gather.6.cloned.1.call-start = ((), (), s32[]{:S(2)}) async-start(), calls=%async_computation.1 | async-start | bytes 1179648 | tf_op jit(solution)/shard_map/all_gather | solution.py:17
  9.4 74.5 %all-gather.4.cloned.1.call-start = ((), (), s32[]{:S(2)}) async-start(), calls=%async_computation | async-start | bytes 2359296 | tf_op jit(solution)/shard_map/all_gather | solution.py:103
  42.9 4.1 %copy-start.5 = (f32[1024]{0:T(1024)S(1)}, f32[1024]{0:T(1024)}, u32[]{:S(2)}) copy-start(f32[1024]{0:T(1024)} %param.17) | copy-start | bytes 12292
  47.0 4.1 %copy-start.4 = (f32[2048]{0:T(1024)S(1)}, f32[2048]{0:T(1024)}, u32[]{:S(2)}) copy-start(f32[2048]{0:T(1024)} %param.19) | copy-start | bytes 24580
  47.0 5.1 %copy-start.3 = (bf16[2048,256]{1,0:T(8,128)(2,1)S(1)}, bf16[2048,256]{1,0:T(8,128)(2,1)}, u32[]{:S(2)}) copy-start(bf16[2048,256]{1,0:T(8,128)(2,1)} %param.21) | copy-start | bytes 3145732
  51.0 1.0 copy-start.6
  52.0 8.6 %copy-start.7 = (bf16[256,2048]{1,0:T(8,128)(2,1)S(1)}, bf16[256,2048]{1,0:T(8,128)(2,1)}, u32[]{:S(2)}) copy-start(bf16[256,2048]{1,0:T(8,128)(2,1)} %copy-done.6) | copy-start | bytes 3145732
  92.7 4.4 %copy-start.2 = (pred[2,2,128,2304]{2,3,1,0:T(8,128)(4,1)S(1)}, pred[2,2,128,2304]{2,3,1,0:T(8,128)(4,1)}, u32[]{:S(2)}) copy-start(pred[2,2,128,2304]{2,3,1,0:T(8,128)(4,1)} %broadcast_and_fusion) | copy-start | bytes 3538948
  108.6 10.3 %copy-start.1 = (bf16[2048,256]{1,0:T(8,128)(2,1)S(1)}, bf16[2048,256]{1,0:T(8,128)(2,1)}, u32[]{:S(2)}) copy-start(bf16[2048,256]{1,0:T(8,128)(2,1)} %param.22) | copy-start | bytes 3145732
Sparse Core Ops, SparseCore 0:
  9.6 24.9 all-gather.5
  55.2 28.7 all-gather.3
where the time goes:
time: 126 us
  waiting for transfers between devices  43 us (34%)
  matrix products  26.4 us (21%)
  other arithmetic  25.2 us (20%)
  local copies, waits for them, and re-layouts  17.2 us (14%)
  between operations  13.7 us (11%)
    all_gather x1, waiting for transfers between devices, carried_in(): everything = lax.all_gather(shard, axis)  23.6 us
    all_gather x1, waiting for transfers between devices, local(): whole = lax.all_gather(packed, 'seq', axis=0, tiled=True)  19.3 us
    sub x1, other arithmetic, local(): weights = jnp.where(allowed, jnp.exp(scores - highest), 0.0)  11.5 us
    dot_general x1, matrix products, local(): jnp.einsum('gnptk,gnke->ntgpe', probs, values_tile, preferred_element_typ...  8.79 us
    select_n x8, other arithmetic, lap(): return jnp.where(reached, new, before)  7.6 us
    gather x1, local copies, waits for them, and re-layouts, local(): tiles = table[mine, :, group_ids, :]  6.99 us
    dot_general x1, matrix products, local(): jnp.einsum('ntgpd,gnkd->gnptk', soft_blocks, keys_tile, preferred_element...  4.37 us
    dot_general x1, matrix products, local(): branch = jnp.dot(normed, lin_out_weight, preferred_element_type=jnp.float32)  4 us
  transfers between devices with their start and end apart: 2, of which 2 were waited for; matrix products, arithmetic and copies ran while one was open for 9% of the time, Pallas kernels for 0%

commit v1 on v0

v1 whole, which is shorter than its diff:
```python
import functools

import jax
import jax.numpy as jnp
from jax import lax
from jax.experimental import pallas as pl
from jax.experimental.pallas import tpu as pltpu
from jax.sharding import PartitionSpec as P

HEAD_DIM = 128
HEADS = 8
KV_HEADS = 2
BLOCK = 128
DENSE_MAX_BLOCKS = 32


EPSILON = 1e-06


def exclusive_prefix(state, axis, devices):
    total = jnp.zeros_like(state)
    window = state
    shift = 1
    while shift < devices:
        pairs = [(i, i + shift) for i in range(devices - shift)]
        got = lax.ppermute(window, axis, pairs)
        total = total + got
        if shift * 2 < devices:
            window = window + got
        shift *= 2
    return total


def attention_kernel(q_ref, kv_ref, code_ref, o_ref, *, per_group):
    keys_total = kv_ref.shape[0]
    keys = kv_ref[:, :HEAD_DIM]
    values = kv_ref[:, HEAD_DIM:]
    code = code_ref[...]
    rows = lax.broadcasted_iota(jnp.int32, (BLOCK, keys_total), 0)
    cols = lax.broadcasted_iota(jnp.int32, (BLOCK, keys_total), 1)
    cols = jnp.bitwise_and(cols, BLOCK - 1)
    allowed = (code == 1) | ((code == 2) & (cols <= rows))
    scale = HEAD_DIM ** (-0.5)
    for p in range(per_group):
        qp = q_ref[:, p * HEAD_DIM:(p + 1) * HEAD_DIM]
        scores = lax.dot_general(
            qp, keys, (((1,), (1,)), ((), ())), preferred_element_type=jnp.float32
        ) * scale
        scores = jnp.where(allowed, scores, -jnp.inf)
        highest = jnp.max(scores, axis=-1, keepdims=True)
        weights = jnp.where(allowed, jnp.exp(scores - highest), 0.0)
        total = jnp.sum(weights, axis=-1, keepdims=True)
        probs = (weights * (1.0 / total)).astype(jnp.bfloat16)
        out = jnp.dot(probs, values, preferred_element_type=jnp.float32)
        o_ref[:, p * HEAD_DIM:(p + 1) * HEAD_DIM] = out.astype(o_ref.dtype)


def attention(soft_query, kv, code, dense):
    tok_count = soft_query.shape[0]
    local_blocks = tok_count // BLOCK
    per_group = HEADS // KV_HEADS
    keys_total = code.shape[-1]
    width = per_group * HEAD_DIM
    if dense:
        kv_spec = pl.BlockSpec((keys_total, 2 * HEAD_DIM), lambda g, n: (0, g))
    else:
        kv_spec = pl.BlockSpec((None, None, keys_total, 2 * HEAD_DIM), lambda g, n: (g, n, 0, 0))
    flops = 4 * tok_count * HEADS * keys_total * HEAD_DIM
    bytes_accessed = 2 * (2 * soft_query.size + KV_HEADS * local_blocks * keys_total * 2 * HEAD_DIM)
    return pl.pallas_call(
        functools.partial(attention_kernel, per_group=per_group),
        out_shape=jax.ShapeDtypeStruct(soft_query.shape, jnp.bfloat16),
        grid=(KV_HEADS, local_blocks),
        in_specs=[
            pl.BlockSpec((BLOCK, width), lambda g, n: (n, g)),
            kv_spec,
            pl.BlockSpec((None, None, 1, keys_total), lambda g, n: (g, n, 0, 0)),
        ],
        out_specs=pl.BlockSpec((BLOCK, width), lambda g, n: (n, g)),
        compiler_params=pltpu.CompilerParams(vmem_limit_bytes=48 * 1024 * 1024),
        cost_estimate=pl.CostEstimate(
            flops=flops, transcendentals=tok_count * HEADS * keys_total, bytes_accessed=bytes_accessed
        ),
    )(soft_query, kv, code)


def local(
    hidden_in,
    lin_query,
    lin_key,
    lin_value,
    lin_gain,
    lin_out_weight,
    soft_gain,
    soft_wq,
    soft_wk,
    soft_wv,
    pattern,
    *,
    devices,
):
    tok_count = hidden_in.shape[0]
    local_blocks = tok_count // BLOCK
    per_group = HEADS // KV_HEADS
    listed = pattern.shape[2]
    position = lax.axis_index("seq")
    query_blocks = lin_query.reshape(local_blocks, BLOCK, KV_HEADS, per_group, HEAD_DIM)
    key_blocks = lin_key.reshape(local_blocks, BLOCK, KV_HEADS, HEAD_DIM)
    value_blocks = lin_value.reshape(local_blocks, BLOCK, KV_HEADS, HEAD_DIM)
    block_states = jnp.einsum(
        "ntgd,ntge->ngde", key_blocks, value_blocks, preferred_element_type=jnp.float32
    )
    device_state = jnp.sum(block_states, axis=0)
    carried = exclusive_prefix(device_state, "seq", devices)
    running = jnp.concatenate(
        [jnp.zeros_like(block_states[:1]), jnp.cumsum(block_states[:-1], axis=0)], axis=0
    )
    before = carried[None] + running
    inter = jnp.einsum(
        "ntgpd,ngde->ntgpe",
        query_blocks.astype(jnp.float32),
        before,
        precision=lax.Precision.HIGHEST,
    )
    rows_here = jnp.arange(BLOCK)
    causal = rows_here[:, None] >= rows_here[None, :]
    local_scores = jnp.einsum(
        "ntgpd,nsgd->ngpts", query_blocks, key_blocks, preferred_element_type=jnp.float32
    )
    local_scores = jnp.where(causal, local_scores, 0.0).astype(jnp.bfloat16)
    intra = jnp.einsum(
        "ngpts,nsge->ntgpe", local_scores, value_blocks, preferred_element_type=jnp.float32
    )
    mixed = (inter + intra).reshape(tok_count, HEADS, HEAD_DIM)
    normed = (
        mixed
        * lax.rsqrt(jnp.mean(mixed * mixed, axis=-1, keepdims=True) + EPSILON)
        * lin_gain.reshape(HEADS, HEAD_DIM)
    )
    normed = normed.reshape(tok_count, HEADS * HEAD_DIM).astype(jnp.bfloat16)
    branch = jnp.dot(normed, lin_out_weight, preferred_element_type=jnp.float32)
    residual = (hidden_in.astype(jnp.float32) + branch).astype(jnp.bfloat16)
    widened = residual.astype(jnp.float32)
    layer_in = (
        widened
        * lax.rsqrt(jnp.mean(widened * widened, axis=-1, keepdims=True) + EPSILON)
        * soft_gain
    ).astype(jnp.bfloat16)
    soft_key = jnp.dot(layer_in, soft_wk, preferred_element_type=jnp.float32).astype(jnp.bfloat16)
    soft_value = jnp.dot(layer_in, soft_wv, preferred_element_type=jnp.float32).astype(jnp.bfloat16)
    packed = jnp.concatenate(
        [
            soft_key.reshape(tok_count, KV_HEADS, HEAD_DIM),
            soft_value.reshape(tok_count, KV_HEADS, HEAD_DIM),
        ],
        axis=-1,
    )
    whole = lax.all_gather(packed, "seq", axis=0, tiled=True)
    soft_query = jnp.dot(layer_in, soft_wq, preferred_element_type=jnp.float32).astype(jnp.bfloat16)

    mine = lax.dynamic_slice_in_dim(pattern, position * local_blocks, local_blocks, 1)
    total_blocks = devices * local_blocks
    dense = total_blocks <= DENSE_MAX_BLOCKS
    if dense:
        block_ids = jnp.arange(total_blocks, dtype=jnp.int32)
        present = jnp.any(mine[..., :, None] == block_ids, axis=-2)
        own = mine[..., :1] == block_ids
        code = jnp.where(own, 2, present.astype(jnp.int32))
        kv = whole.reshape(total_blocks * BLOCK, KV_HEADS * 2 * HEAD_DIM)
    else:
        same = mine[..., :, None] == mine[..., None, :]
        earlier = jnp.arange(listed)[None, :] < jnp.arange(listed)[:, None]
        repeated = jnp.any(same & earlier, axis=-1)
        first_slot = (jnp.arange(listed) == 0)[None, None, :]
        code = jnp.where(first_slot, 2, jnp.logical_not(repeated).astype(jnp.int32))
        table = whole.reshape(-1, BLOCK, KV_HEADS, 2 * HEAD_DIM)
        group_ids = jnp.arange(KV_HEADS)[:, None, None]
        tiles = table[mine, :, group_ids, :]
        kv = tiles.reshape(KV_HEADS, local_blocks, listed * BLOCK, 2 * HEAD_DIM)
    code = jnp.repeat(code, BLOCK, axis=-1)[:, :, None, :]
    return attention(soft_query, kv, code, dense)


def solution(mesh):
    in_specs = (
        P(("dp", "seq"), None),
        P(("dp", "seq"), None),
        P(("dp", "seq"), None),
        P(("dp", "seq"), None),
        P(),
        P(),
        P(),
        P(),
        P(),
        P(),
        P(),
    )
    out_specs = P(("dp", "seq"), None)
    body = functools.partial(local, devices=mesh.shape["seq"])
    return jax.shard_map(body, mesh=mesh, in_specs=in_specs, out_specs=out_specs, check_vma=False)
```

time: 126 us -> 101 us (0.80)
  other arithmetic: 25.2 us -> 1.28 us
  starting transfers between devices: 0.04 us -> 15.7 us
  Pallas kernels: 0 us -> 14.7 us
  matrix products: 26.4 us -> 12.7 us
  waiting for transfers between devices: 43 us -> 32.5 us
  local copies, waits for them, and re-layouts: 17.2 us -> 9.59 us
    all_gather x1 -> x0, waiting for transfers between devices: 23.6 us -> none  [carried_in(): everything = lax.all_gather(shard, axis)]
    ppermute x0 -> x3, starting transfers between devices: none -> 15.7 us  [exclusive_prefix(): got = lax.ppermute(window, axis, pairs)]
    pallas_call x0 -> x1, Pallas kernels: none -> 14.7 us  [attention(): pl.pallas_call(functools.partial(attention_kernel, per_group=per_group),...]
    dot_general x2 -> x0, matrix products: 13.2 us -> none  [the longest x1 8.79 us: local(): jnp.einsum('gnptk,gnke->ntgpe', probs, values_tile, preferred_element_typ...]
    sub x1 -> x0, other arithmetic: 11.5 us -> none  [local(): weights = jnp.where(allowed, jnp.exp(scores - highest), 0.0)]
    all_gather x1, waiting for transfers between devices: 19.3 us -> 27 us  [local(): whole = lax.all_gather(packed, 'seq', axis=0, tiled=True)]
    select_n x8 -> x1, other arithmetic: 7.6 us -> 0.07 us  [local(): code = jnp.where(own, 2, present.astype(jnp.int32))]
    gather x1 -> x0, local copies, waits for them, and re-layouts: 6.99 us -> none  [local(): tiles = table[mine, :, group_ids, :]]
  transfers between devices with their start and end apart: 2 -> 4, of which waited for: 2 -> 4; matrix products, arithmetic and copies ran while one was open for 9% -> 6% of each run, Pallas kernels for 0% -> 0%
where the time goes in v1:
time: 101 us; the launch traced here: 100 us
  waiting for transfers between devices  32.5 us (32%)
  starting transfers between devices  15.7 us (16%)
  Pallas kernels  14.7 us (15%)
  between operations  13.6 us (13%)
  matrix products  12.7 us (13%)
  local copies, waits for them, and re-layouts  9.59 us (9%)
  other arithmetic  1.28 us (1%)
    all_gather x1, waiting for transfers between devices, local(): whole = lax.all_gather(packed, 'seq', axis=0, tiled=True)  27 us
    ppermute x3, starting transfers between devices, exclusive_prefix(): got = lax.ppermute(window, axis, pairs)  15.7 us
    pallas_call x1, Pallas kernels, attention(): pl.pallas_call(functools.partial(attention_kernel, per_group=per_group),...  14.7 us
    ppermute x3, waiting for transfers between devices, exclusive_prefix(): got = lax.ppermute(window, axis, pairs)  5.53 us
    dot_general x1, matrix products, local(): branch = jnp.dot(normed, lin_out_weight, preferred_element_type=jnp.float32)  3.92 us
    dot_general x1, matrix products, local(): jnp.dot(layer_in, soft_wq, preferred_element_type=jnp.float32)  3.83 us
    unnamed x13, local copies, waits for them, and re-layouts  2.81 us
  transfers between devices with their start and end apart: 4, of which 4 were waited for; matrix products, arithmetic and copies ran while one was open for 6% of the time, Pallas kernels for 0%

profile of v1, /device:TPU:0, one launch (start us, length us, event | category | flops | bytes accessed | tf_op | source)
XLA Modules:
  0.0 100.1 jit_solution(15335357931664591681)
XLA Ops:
  6.5 0.0 copy-start
  6.5 0.0 copy-start.1
  6.5 0.0 all-gather.2.cloned.1.call-start
  6.5 1.1 %reshape.56 = bf16[2,128,2,128]{3,2,1,0:T(2,128)(2,1)S(1)} reshape(bf16[256,256]{1,0:T(8,128)(2,1)} %param.14) | data formatting | bytes 262144 | tf_op jit(solution)/shard_map/reshape | solution.py:109
  7.6 0.9 reshape.55
  8.5 0.2 fusion.32
  8.8 2.4 %collective-permute-start = (f32[2,128,128]{2,1,0:T(8,128)S(1)}, f32[2,128,128]{2,1,0:T(8,128)S(1)}, u32[]{:S(2)}, u32[]{:S(2)}) collective-permute-start(f32[2,128,128]{2,1,0:T(8,128)S(1)} %get-tuple-element.5), channel_id=1, source_target_pairs={{0,1},{1,2},{2,3},{3,4},{4,5},{5,6},{6,7},{8,9},{9,10},{10,11},{11... | collective-permute-start | bytes 393224 | tf_op jit(solution)/shard_map/ppermute | solution.py:26
  11.2 1.0 collective-permute-done
  12.2 7.9 %collective-permute-start.1 = (f32[2,128,128]{2,1,0:T(8,128)S(1)}, f32[2,128,128]{2,1,0:T(8,128)S(1)}, u32[]{:S(2)}, u32[]{:S(2)}) collective-permute-start(f32[2,128,128]{2,1,0:T(8,128)S(1)} %add.55), channel_id=1, source_target_pairs={{0,2},{1,3},{2,4},{3,5},{4,6},{5,7},{8,10},{9,11},{10,12},{11,13},... | collective-permute-start | bytes 393224 | tf_op jit(solution)/shard_map/ppermute | solution.py:26
  20.1 2.5 %collective-permute-done.1 = f32[2,128,128]{2,1,0:T(8,128)S(1)} collective-permute-done((f32[2,128,128]{2,1,0:T(8,128)S(1)}, f32[2,128,128]{2,1,0:T(8,128)S(1)}, u32[]{:S(2)}, u32[]{:S(2)}) %collective-permute-start.1) | collective-permute-done | bytes 131104 | tf_op jit(solution)/shard_map/ppermute | solution.py:26
  22.6 5.4 %collective-permute-start.2 = (f32[2,128,128]{2,1,0:T(8,128)S(1)}, f32[2,128,128]{2,1,0:T(8,128)S(1)}, u32[]{:S(2)}, u32[]{:S(2)}) collective-permute-start(f32[2,128,128]{2,1,0:T(8,128)S(1)} %add.57), channel_id=1, source_target_pairs={{0,4},{1,5},{2,6},{3,7},{8,12},{9,13},{10,14},{11,15},{16,20},{17,... | collective-permute-start | bytes 393224 | tf_op jit(solution)/shard_map/ppermute | solution.py:26
  28.0 0.0 copy-done.1
  28.0 0.4 reshape.57
  28.4 2.1 %collective-permute-done.2 = f32[2,128,128]{2,1,0:T(8,128)S(1)} collective-permute-done((f32[2,128,128]{2,1,0:T(8,128)S(1)}, f32[2,128,128]{2,1,0:T(8,128)S(1)}, u32[]{:S(2)}, u32[]{:S(2)}) %collective-permute-start.2) | collective-permute-done | bytes 131104 | tf_op jit(solution)/shard_map/ppermute | solution.py:26
  30.5 0.6 convolution_bitcast_fusion.2
  31.1 1.5 %multiply_reduce_fusion = (f32[2,128,2,4]{1,3,2,0:T(4,128)S(1)}, f32[2,128,2,4,128]{1,4,3,2,0:T(8,128)}) fusion(f32[2,128,2,4,128]{1,4,3,2,0:T(8,128)S(1)} %convolution_bitcast_fusion.2, pred[128,128]{0,1:T(8,128)(4,1)S(1)} %iota_compare_fusion, bf16[2,128,2,4,128]{4,3,2,1,0:T(4,128)(2,1)S(1)} %reshape.57, bf16[2,128,2,128,1]{3,2,1,0,4:T(2,128)(2,1)S(1)} %bitcast.47, ...), kind=kOutput, calls=%fused_computation.19 | convolution fusion | flops 135526400 | bytes 2908160 | tf_op jit(solution)/shard_map/ngpts,nsge->ntgpe/dot_general | solution.py:131
  32.6 1.7 %copy.48 = f32[2,128,2,4,128]{4,3,2,1,0:T(4,128)S(1)} copy(f32[2,128,2,4,128]{1,4,3,2,0:T(8,128)} %get-tuple-element.8) | data formatting | bytes 2097152 | tf_op jit(solution)/shard_map/add | solution.py:134
  34.3 0.0 copy-start.4
  34.3 0.4 reshape.58
  34.7 0.1 copy.49
  34.8 0.3 mul.47
  35.2 0.0 copy-done.4
  35.2 0.0 copy-start.3
  35.2 3.9 %fusion.1 = (f32[256]{0:T(256)S(1)}, bf16[256,2048]{1,0:T(8,128)(2,1)S(1)}) fusion(bf16[1024,2048]{1,0:T(8,128)(2,1)} %param.16, f32[256,1024]{1,0:T(8,128)S(1)} %reshape.58, f32[32,8,8,128]{3,2,1,0:T(8,128)S(1)} %bitcast.48, f32[1024]{0:T(1024)S(1)} %copy-done.4, bf16[256,2048]{1,0:T(8,128)(2,1)} %param.11), kind=kOutput, calls=%fused_computation.4 | convolution fusion | flops 1077673728 | bytes 8393728 | tf_op jit(solution)/shard_map/dot_general | solution.py:141
  39.1 0.0 copy-start.5
  39.1 0.0 copy-start.2
  39.2 0.0 copy-done
  39.2 0.0 copy-done.3
  39.2 0.7 convolution_convert_fusion.1
  39.9 0.3 copy-done.5
  40.1 0.1 copy.51
  40.3 0.5 copy-done.2
  40.7 1.9 %convolution_convert_fusion.2 = bf16[256,256]{0,1:T(8,128)(2,1)S(1)} fusion(bf16[2048,256]{1,0:T(8,128)(2,1)S(1)} %copy-done.2, bf16[256,2048]{1,0:T(8,128)(2,1)} %copy-done.5, f32[2048]{0:T(1024)S(1)} %copy-done.3, f32[256]{0:T(256)S(1)} %add_rsqrt_fusion.1), kind=kOutput, calls=%fused_computation.15 | convolution fusion | flops 270598144 | bytes 2237440 | tf_op jit(solution)/shard_map/dot_general | solution.py:149
  42.6 0.1 copy.50
  42.8 1.0 pad_maximum_fusion
  43.7 0.0 all-gather.2.cloned.1.call-update
  43.8 0.8 dynamic-slice_reduce_fusion
  44.6 0.7 constant_dynamic-slice_fusion
  45.3 0.1 fusion.26
  45.5 0.1 compare_select_fusion
  45.6 3.8 %convolution_convert_fusion.q_ref = bf16[256,1024]{1,0:T(8,128)(2,1)S(1)} fusion(bf16[2048,1024]{1,0:T(8,128)(2,1)} %param.18, bf16[256,2048]{1,0:T(8,128)(2,1)} %copy-done.5, f32[2048]{0:T(1024)S(1)} %copy-done.3, f32[256]{0:T(256)S(1)} %add_rsqrt_fusion.1), kind=kOutput, calls=%fused_computation.13 | convolution fusion | flops 1076101120 | bytes 5776384 | tf_op jit(solution)/shard_map/dot_general | solution.py:159
  49.4 27.0 %all-gather.2.cloned.1.call-done = bf16[2048,2,256]{2,1,0:T(2,128)(2,1)} async-done(((bf16[256,2,256]{2,1,0:T(2,128)(2,1)}), bf16[2048,2,256]{2,1,0:T(2,128)(2,1)}) %all-gather.2.cloned.1.call-update) | async-done | bytes 2097168 | tf_op jit(solution)/shard_map/all_gather | solution.py:158
  76.4 2.0 %copy.63 = bf16[256,8,2,256]{3,1,2,0:T(8,128)(2,1)S(1)} copy(bf16[256,8,2,256]{3,2,1,0:T(2,128)(2,1)} %bitcast.45) | data formatting | bytes 4194304
  78.4 0.1 broadcast_in_dim.28
  78.5 14.7 %shard_map.109 = bf16[256,1024]{1,0:T(8,128)(2,1)} custom-call(bf16[256,1024]{1,0:T(8,128)(2,1)S(1)} %convolution_convert_fusion.q_ref, bf16[2048,512]{1,0:T(8,128)(2,1)S(1)} %bitcast.43, s32[2,2,1,2048]{3,2,1,0:T(1,128)S(1)} %bitcast.44), custom_call_target="tpu_custom_call" | custom-call | flops 2147483648 | bytes 5242880 | tf_op jit(solution)/shard_map/pallas_call | solution.py:70
  (7 shorter events, 0.1 us)
Async XLA Ops:
  6.5 32.6 %copy-start = (bf16[2048,256]{1,0:T(8,128)(2,1)S(1)}, bf16[2048,256]{1,0:T(8,128)(2,1)}, u32[]{:S(2)}) copy-start(bf16[2048,256]{1,0:T(8,128)(2,1)} %param.20) | copy-start | bytes 3145732
  6.5 21.4 %copy-start.1 = (bf16[256,1024]{1,0:T(8,128)(2,1)S(1)}, bf16[256,1024]{1,0:T(8,128)(2,1)}, u32[]{:S(2)}) copy-start(bf16[256,1024]{1,0:T(8,128)(2,1)} %param.12) | copy-start | bytes 1572868
  6.5 69.8 %all-gather.2.cloned.1.call-start = ((), (), s32[]{:S(2)}) async-start(), calls=%async_computation | async-start | bytes 2359296 | tf_op jit(solution)/shard_map/all_gather | solution.py:158
  8.8 3.4 %collective-permute-start = (f32[2,128,128]{2,1,0:T(8,128)S(1)}, f32[2,128,128]{2,1,0:T(8,128)S(1)}, u32[]{:S(2)}, u32[]{:S(2)}) collective-permute-start(f32[2,128,128]{2,1,0:T(8,128)S(1)} %get-tuple-element.5), channel_id=1, source_target_pairs={{0,1},{1,2},{2,3},{3,4},{4,5},{5,6},{6,7},{8,9},{9,10},{10,11},{11... | collective-permute-start | bytes 393224 | tf_op jit(solution)/shard_map/ppermute | solution.py:26
  12.2 10.4 %collective-permute-start.1 = (f32[2,128,128]{2,1,0:T(8,128)S(1)}, f32[2,128,128]{2,1,0:T(8,128)S(1)}, u32[]{:S(2)}, u32[]{:S(2)}) collective-permute-start(f32[2,128,128]{2,1,0:T(8,128)S(1)} %add.55), channel_id=1, source_target_pairs={{0,2},{1,3},{2,4},{3,5},{4,6},{5,7},{8,10},{9,11},{10,12},{11,13},... | collective-permute-start | bytes 393224 | tf_op jit(solution)/shard_map/ppermute | solution.py:26
  22.6 7.9 %collective-permute-start.2 = (f32[2,128,128]{2,1,0:T(8,128)S(1)}, f32[2,128,128]{2,1,0:T(8,128)S(1)}, u32[]{:S(2)}, u32[]{:S(2)}) collective-permute-start(f32[2,128,128]{2,1,0:T(8,128)S(1)} %add.57), channel_id=1, source_target_pairs={{0,4},{1,5},{2,6},{3,7},{8,12},{9,13},{10,14},{11,15},{16,20},{17,... | collective-permute-start | bytes 393224 | tf_op jit(solution)/shard_map/ppermute | solution.py:26
  34.3 0.9 copy-start.4
  35.2 4.0 %copy-start.3 = (f32[2048]{0:T(1024)S(1)}, f32[2048]{0:T(1024)}, u32[]{:S(2)}) copy-start(f32[2048]{0:T(1024)} %param.17) | copy-start | bytes 24580
  39.1 1.0 %copy-start.5 = (bf16[256,2048]{1,0:T(8,128)(2,1)}, bf16[256,2048]{1,0:T(8,128)(2,1)S(1)}, u32[]{:S(2)}) copy-start(bf16[256,2048]{1,0:T(8,128)(2,1)S(1)} %get-tuple-element.10) | copy-start | bytes 3145732
  39.1 1.6 %copy-start.2 = (bf16[2048,256]{1,0:T(8,128)(2,1)S(1)}, bf16[2048,256]{1,0:T(8,128)(2,1)}, u32[]{:S(2)}) copy-start(bf16[2048,256]{1,0:T(8,128)(2,1)} %param.19) | copy-start | bytes 3145732
Sparse Core Ops, SparseCore 0:
  43.9 32.4 all-gather.1

commit v2 on v1

--- a/solution.py
+++ b/solution.py
@@ -11,7 +11,7 @@
 HEADS = 8
 KV_HEADS = 2
 BLOCK = 128
-DENSE_MAX_BLOCKS = 32
+EXCHANGE_MAX_DEVICES = 16
 
 
 EPSILON = 1e-06
@@ -55,14 +55,14 @@
         o_ref[:, p * HEAD_DIM:(p + 1) * HEAD_DIM] = out.astype(o_ref.dtype)
 
 
-def attention(soft_query, kv, code, dense):
+def attention(soft_query, kv, code):
     tok_count = soft_query.shape[0]
     local_blocks = tok_count // BLOCK
     per_group = HEADS // KV_HEADS
     keys_total = code.shape[-1]
     width = per_group * HEAD_DIM
-    if dense:
-        kv_spec = pl.BlockSpec((keys_total, 2 * HEAD_DIM), lambda g, n: (0, g))
+    if kv.ndim == 3:
+        kv_spec = pl.BlockSpec((None, keys_total, 2 * HEAD_DIM), lambda g, n: (g, 0, 0))
     else:
         kv_spec = pl.BlockSpec((None, None, keys_total, 2 * HEAD_DIM), lambda g, n: (g, n, 0, 0))
     flops = 4 * tok_count * HEADS * keys_total * HEAD_DIM
@@ -82,6 +82,44 @@
             flops=flops, transcendentals=tok_count * HEADS * keys_total, bytes_accessed=bytes_accessed
         ),
     )(soft_query, kv, code)
+
+
+def exchange_kv(packed, pattern, position, devices):
+    tok_count = packed.shape[0]
+    local_blocks = tok_count // BLOCK
+    blocks = packed.reshape(local_blocks, BLOCK, KV_HEADS, 2 * HEAD_DIM)
+    heads = jnp.arange(KV_HEADS)
+    per_head = jnp.transpose(blocks, (2, 0, 1, 3)).reshape(KV_HEADS, tok_count, 2 * HEAD_DIM)
+    pieces = [per_head]
+    own_ids = position * local_blocks + jnp.arange(local_blocks, dtype=jnp.int32)
+    ids = [jnp.broadcast_to(own_ids, (KV_HEADS, local_blocks))]
+    if devices > 1:
+        pairs = [(i, i + 1) for i in range(devices - 1)]
+        pieces.append(lax.ppermute(per_head, "seq", pairs))
+        near = own_ids - local_blocks
+        ids.append(jnp.broadcast_to(jnp.where(position >= 1, near, -1), (KV_HEADS, local_blocks)))
+    mine = lax.dynamic_slice_in_dim(pattern, position * local_blocks, local_blocks, 1)
+    my_far = mine[:, :, 2:].reshape(KV_HEADS, -1)
+    for shift in range(2, devices):
+        dest = jnp.minimum(position + shift, devices - 1)
+        rows = lax.dynamic_slice_in_dim(pattern, dest * local_blocks, local_blocks, 1)
+        far = rows[:, :, 2:].reshape(KV_HEADS, -1)
+        on_me = (far // local_blocks) == position
+        choice = jnp.max(jnp.where(on_me, far - position * local_blocks, 0), axis=-1)
+        chosen = blocks[choice, :, heads, :]
+        pairs = [(i, i + shift) for i in range(devices - shift)]
+        pieces.append(lax.ppermute(chosen, "seq", pairs))
+        source = position - shift
+        on_src = (my_far // local_blocks) == source
+        got_id = jnp.max(jnp.where(on_src, my_far, -1), axis=-1)
+        ids.append(jnp.where(source >= 0, got_id, -1)[:, None])
+    table = jnp.concatenate(pieces, axis=1)
+    slot_ids = jnp.concatenate(ids, axis=1)
+    present = jnp.any(mine[:, :, :, None] == slot_ids[:, None, None, :], axis=2)
+    present = present & (slot_ids >= 0)[:, None, :]
+    own = mine[:, :, :1] == slot_ids[:, None, :]
+    code = jnp.where(own, 2, present.astype(jnp.int32))
+    return table, code
 
 
 def local(
@@ -155,19 +193,13 @@
         ],
         axis=-1,
     )
-    whole = lax.all_gather(packed, "seq", axis=0, tiled=True)
     soft_query = jnp.dot(layer_in, soft_wq, preferred_element_type=jnp.float32).astype(jnp.bfloat16)
 
-    mine = lax.dynamic_slice_in_dim(pattern, position * local_blocks, local_blocks, 1)
-    total_blocks = devices * local_blocks
-    dense = total_blocks <= DENSE_MAX_BLOCKS
-    if dense:
-        block_ids = jnp.arange(total_blocks, dtype=jnp.int32)
-        present = jnp.any(mine[..., :, None] == block_ids, axis=-2)
-        own = mine[..., :1] == block_ids
-        code = jnp.where(own, 2, present.astype(jnp.int32))
-        kv = whole.reshape(total_blocks * BLOCK, KV_HEADS * 2 * HEAD_DIM)
+    if devices <= EXCHANGE_MAX_DEVICES:
+        kv, code = exchange_kv(packed, pattern, position, devices)
     else:
+        whole = lax.all_gather(packed, "seq", axis=0, tiled=True)
+        mine = lax.dynamic_slice_in_dim(pattern, position * local_blocks, local_blocks, 1)
         same = mine[..., :, None] == mine[..., None, :]
         earlier = jnp.arange(listed)[None, :] < jnp.arange(listed)[:, None]
         repeated = jnp.any(same & earlier, axis=-1)
@@ -178,7 +210,7 @@
         tiles = table[mine, :, group_ids, :]
         kv = tiles.reshape(KV_HEADS, local_blocks, listed * BLOCK, 2 * HEAD_DIM)
     code = jnp.repeat(code, BLOCK, axis=-1)[:, :, None, :]
-    return attention(soft_query, kv, code, dense)
+    return attention(soft_query, kv, code)
 
 
 def solution(mesh):

time: 101 us -> 86.1 us (0.85)
  the two profiles are of different devices: /device:TPU:0 before, /device:TPU:24 now
where the time goes in v2:
time: 86.1 us; the launch traced here: 85 us
  waiting for transfers between devices  26.4 us (31%)
  local copies, waits for them, and re-layouts  19.3 us (22%)
  starting transfers between devices  13.5 us (16%)
  matrix products  12.4 us (14%)
  Pallas kernels  10.8 us (13%)
  other arithmetic  2.13 us (2%)
    ppermute x3, waiting for transfers between devices, exclusive_prefix(): got = lax.ppermute(window, axis, pairs)  15.1 us
    ppermute x6, waiting for transfers between devices, exchange_kv(): pieces.append(lax.ppermute(chosen, 'seq', pairs))  11.3 us
    pallas_call x1, Pallas kernels, attention(): pl.pallas_call(functools.partial(attention_kernel, per_group=per_group),...  10.8 us
    gather x6, local copies, waits for them, and re-layouts, exchange_kv(): chosen = blocks[choice, :, heads, :]  7.24 us
    ppermute x6, starting transfers between devices, exchange_kv(): pieces.append(lax.ppermute(chosen, 'seq', pairs))  7.07 us
    unnamed x20, local copies, waits for them, and re-layouts  4.74 us
    ppermute x3, starting transfers between devices, exclusive_prefix(): got = lax.ppermute(window, axis, pairs)  4.5 us
    dot_general x1, matrix products, local(): branch = jnp.dot(normed, lin_out_weight, preferred_element_type=jnp.float32)  3.97 us
  transfers between devices with their start and end apart: 10, of which 3 were waited for; matrix products, arithmetic and copies ran while one was open for 23% of the time, Pallas kernels for 0%

profile of v2, /device:TPU:24, one launch (start us, length us, event | category | flops | bytes accessed | tf_op | source)
XLA Modules:
  0.0 85.0 jit_solution(15228421081221849971)
XLA Ops:
  0.0 1.1 %reshape.263 = bf16[2,128,2,128]{3,2,1,0:T(2,128)(2,1)S(1)} reshape(bf16[256,256]{1,0:T(8,128)(2,1)} %param.14) | data formatting | bytes 262144 | tf_op jit(solution)/shard_map/reshape | solution.py:147
  1.1 0.9 %reshape.262 = bf16[2,128,2,128]{3,2,1,0:T(2,128)(2,1)S(1)} reshape(bf16[256,256]{1,0:T(8,128)(2,1)} %param.13) | data formatting | bytes 262144 | tf_op jit(solution)/shard_map/reshape | solution.py:146
  2.0 0.2 fusion.74
  2.3 1.9 %collective-permute-start = (f32[2,128,128]{2,1,0:T(8,128)S(1)}, f32[2,128,128]{2,1,0:T(8,128)S(1)}, u32[]{:S(2)}, u32[]{:S(2)}) collective-permute-start(f32[2,128,128]{2,1,0:T(8,128)S(1)} %get-tuple-element.25), channel_id=1, source_target_pairs={{0,1},{1,2},{2,3},{3,4},{4,5},{5,6},{6,7},{8,9},{9,10},{10,11},{11... | collective-permute-start | bytes 393224 | tf_op jit(solution)/shard_map/ppermute | solution.py:26
  4.2 0.7 constant_dynamic-slice_fusion.2
  4.9 0.8 fusion.26
  5.7 1.4 %and_select_fusion = (s32[2,2,16]{2,1,0:T(2,128)S(1)}, s32[2,2,16]{2,1,0:T(2,128)S(1)}, s32[2]{0:T(128)S(1)}, s32[2]{0:T(128)S(1)}, s32[2]{0:T(128)S(1)}, /*index=5*/s32[2]{0:T(128)S(1)}, s32[2]{0:T(128)S(1)}, s32[2]{0:T(128)S(1)}) fusion(s32[2,16,18]{2,1,0:T(8,128)} %param.21, s32[]{:T(128)S(6)} %select_n.325, s32[]{:T(128)S(6)} %add.223, ...), kind=kLoop, calls=%fused_computation.62 | loop fusion | flops 8244 | bytes 2392 | tf_op jit(solution)/shard_map/jit(floor_divide)/jit(_where)/select_n | solution.py:113
  7.2 0.3 fusion.38
  7.5 0.1 copy.53
  7.6 0.1 copy.54
  7.7 0.1 copy.55
  7.8 0.1 copy.56
  7.9 0.1 copy.57
  8.0 0.1 copy.58
  8.1 0.1 concatenate.50
  8.2 0.2 compare_reduce_fusion
  8.4 0.1 compare_select_fusion
  8.5 0.0 collective-permute-done
  8.6 1.3 %collective-permute-start.1 = (f32[2,128,128]{2,1,0:T(8,128)S(1)}, f32[2,128,128]{2,1,0:T(8,128)S(1)}, u32[]{:S(2)}, u32[]{:S(2)}) collective-permute-start(f32[2,128,128]{2,1,0:T(8,128)S(1)} %add.189), channel_id=1, source_target_pairs={{0,2},{1,3},{2,4},{3,5},{4,6},{5,7},{8,10},{9,11},{10,12},{11,13},... | collective-permute-start | bytes 393224 | tf_op jit(solution)/shard_map/ppermute | solution.py:26
  9.9 6.4 %collective-permute-done.1 = f32[2,128,128]{2,1,0:T(8,128)S(1)} collective-permute-done((f32[2,128,128]{2,1,0:T(8,128)S(1)}, f32[2,128,128]{2,1,0:T(8,128)S(1)}, u32[]{:S(2)}, u32[]{:S(2)}) %collective-permute-start.1) | collective-permute-done | bytes 131104 | tf_op jit(solution)/shard_map/ppermute | solution.py:26
  16.3 1.3 %collective-permute-start.2 = (f32[2,128,128]{2,1,0:T(8,128)S(1)}, f32[2,128,128]{2,1,0:T(8,128)S(1)}, u32[]{:S(2)}, u32[]{:S(2)}) collective-permute-start(f32[2,128,128]{2,1,0:T(8,128)S(1)} %add.191), channel_id=1, source_target_pairs={{0,4},{1,5},{2,6},{3,7},{8,12},{9,13},{10,14},{11,15},{16,20},{17,... | collective-permute-start | bytes 393224 | tf_op jit(solution)/shard_map/ppermute | solution.py:26
  17.6 0.4 reshape.264
  18.0 0.1 broadcast_in_dim.79
  18.1 8.7 %collective-permute-done.2 = f32[2,128,128]{2,1,0:T(8,128)S(1)} collective-permute-done((f32[2,128,128]{2,1,0:T(8,128)S(1)}, f32[2,128,128]{2,1,0:T(8,128)S(1)}, u32[]{:S(2)}, u32[]{:S(2)}) %collective-permute-start.2) | collective-permute-done | bytes 131104 | tf_op jit(solution)/shard_map/ppermute | solution.py:26
  26.8 0.6 convolution_bitcast_fusion.2
  27.4 1.5 %multiply_reduce_fusion = (f32[2,128,2,4]{1,3,2,0:T(4,128)S(1)}, f32[2,128,2,4,128]{1,4,3,2,0:T(8,128)}) fusion(f32[2,128,2,4,128]{1,4,3,2,0:T(8,128)S(1)} %convolution_bitcast_fusion.2, pred[128,128]{0,1:T(8,128)(4,1)S(1)} %iota_compare_fusion, bf16[2,128,2,4,128]{4,3,2,1,0:T(4,128)(2,1)S(1)} %reshape.264, bf16[2,128,2,128,1]{3,2,1,0,4:T(2,128)(2,1)S(1)} %bitcast.92, ...), kind=kOutput, calls=%fused_computation.25 | convolution fusion | flops 135526400 | bytes 2908160 | tf_op jit(solution)/shard_map/ngpts,nsge->ntgpe/dot_general | solution.py:169
  28.9 1.7 %copy.49 = f32[2,128,2,4,128]{4,3,2,1,0:T(4,128)S(1)} copy(f32[2,128,2,4,128]{1,4,3,2,0:T(8,128)} %get-tuple-element.28) | data formatting | bytes 2097152 | tf_op jit(solution)/shard_map/add | solution.py:172
  30.6 0.0 copy-start.4
  30.6 0.4 reshape.265
  31.0 0.1 copy.50
  31.2 0.3 mul.72
  31.5 0.0 copy-start.3
  31.5 4.0 %fusion.1 = (f32[256]{0:T(256)S(1)}, bf16[256,2048]{1,0:T(8,128)(2,1)S(1)}) fusion(bf16[1024,2048]{1,0:T(8,128)(2,1)} %param.16, f32[256,1024]{1,0:T(8,128)S(1)} %reshape.265, f32[32,8,8,128]{3,2,1,0:T(8,128)S(1)} %bitcast.93, f32[1024]{0:T(1024)S(1)} %copy-done.4, bf16[256,2048]{1,0:T(8,128)(2,1)} %param.11), kind=kOutput, calls=%fused_computation.10 | convolution fusion | flops 1077673728 | bytes 8393728 | tf_op jit(solution)/shard_map/dot_general | solution.py:179
  35.5 0.0 copy-start.2
  35.5 1.0 %copy-done.5 = bf16[256,2048]{1,0:T(8,128)(2,1)} copy-done((bf16[256,2048]{1,0:T(8,128)(2,1)}, bf16[256,2048]{1,0:T(8,128)(2,1)S(1)}, u32[]{:S(2)}) %copy-start.5) | copy-done | bytes 1048600
  36.5 0.5 convolution_convert_fusion.2
  37.1 0.0 copy-done.2
  37.1 1.7 %convolution_convert_fusion.1 = bf16[256,256]{1,0:T(8,128)(2,1)S(1)} fusion(bf16[2048,256]{1,0:T(8,128)(2,1)S(1)} %copy-done.2, bf16[256,2048]{1,0:T(8,128)(2,1)} %copy-done.5, f32[2048]{0:T(1024)S(1)} %copy-done.3, f32[256]{0:T(256)S(1)} %add_rsqrt_fusion.1), kind=kOutput, calls=%fused_computation.20 | convolution fusion | flops 270598144 | bytes 2237440 | tf_op jit(solution)/shard_map/dot_general | solution.py:188
  38.9 1.9 %collective-permute-start.3 = (bf16[2,256,256]{2,1,0:T(8,128)(2,1)S(1)}, bf16[2,256,256]{2,1,0:T(8,128)(2,1)S(1)}, u32[]{:S(2)}, u32[]{:S(2)}) collective-permute-start(bf16[2,256,256]{2,1,0:T(8,128)(2,1)S(1)} %bitcast.89), channel_id=1, source_target_pairs={{0,1},{1,2},{2,3},{3,4},{4,5},{5,6},{6,7},{8,9},{9,10},{10,11},{11... | collective-permute-start | bytes 786440 | tf_op jit(solution)/shard_map/ppermute | solution.py:98
  40.9 3.8 %convolution_convert_fusion.q_ref = bf16[256,1024]{1,0:T(8,128)(2,1)S(1)} fusion(bf16[2048,1024]{1,0:T(8,128)(2,1)} %param.18, bf16[256,2048]{1,0:T(8,128)(2,1)} %copy-done.5, f32[2048]{0:T(1024)S(1)} %copy-done.3, f32[256]{0:T(256)S(1)} %add_rsqrt_fusion.1), kind=kOutput, calls=%fused_computation.19 | convolution fusion | flops 1076101120 | bytes 5776384 | tf_op jit(solution)/shard_map/dot_general | solution.py:196
  44.7 1.2 %gather_fusion = bf16[2,128,256]{2,1,0:T(8,128)(2,1)} fusion(bf16[2,128,2,256]{3,1,0,2:T(8,128)(2,1)S(1)} %copy_dynamic-update-slice_fusion, s32[2]{0:T(128)S(1)} %fusion.68), kind=kCustom, calls=%fused_computation | custom fusion | bytes 262160 | tf_op jit(solution)/shard_map/gather | solution.py:109
  45.9 1.3 %collective-permute-start.4 = (bf16[2,128,256]{2,1,0:T(8,128)(2,1)}, bf16[2,128,256]{2,1,0:T(8,128)(2,1)}, u32[]{:S(2)}, u32[]{:S(2)}) collective-permute-start(bf16[2,128,256]{2,1,0:T(8,128)(2,1)} %gather_fusion), channel_id=1, source_target_pairs={{0,2},{1,3},{2,4},{3,5},{4,6},{5,7},{8,10},{9,11},{10,12},{11,13},... | collective-permute-start | bytes 393224 | tf_op jit(solution)/shard_map/ppermute | solution.py:111
  47.2 1.2 %gather_fusion.1 = bf16[2,128,256]{2,1,0:T(8,128)(2,1)} fusion(bf16[2,128,2,256]{3,1,0,2:T(8,128)(2,1)S(1)} %copy_dynamic-update-slice_fusion, s32[2]{0:T(128)S(1)} %fusion.67), kind=kCustom, calls=%fused_computation.1 | custom fusion | bytes 262160 | tf_op jit(solution)/shard_map/gather | solution.py:109
  48.4 1.3 %collective-permute-start.5 = (bf16[2,128,256]{2,1,0:T(8,128)(2,1)}, bf16[2,128,256]{2,1,0:T(8,128)(2,1)}, u32[]{:S(2)}, u32[]{:S(2)}) collective-permute-start(bf16[2,128,256]{2,1,0:T(8,128)(2,1)} %gather_fusion.1), channel_id=1, source_target_pairs={{0,3},{1,4},{2,5},{3,6},{4,7},{8,11},{9,12},{10,13},{11,14},{12,15... | collective-permute-start | bytes 393224 | tf_op jit(solution)/shard_map/ppermute | solution.py:111
  49.7 1.2 %gather_fusion.2 = bf16[2,128,256]{2,1,0:T(8,128)(2,1)} fusion(bf16[2,128,2,256]{3,1,0,2:T(8,128)(2,1)S(1)} %copy_dynamic-update-slice_fusion, s32[2]{0:T(128)S(1)} %fusion.66), kind=kCustom, calls=%fused_computation.2 | custom fusion | bytes 262160 | tf_op jit(solution)/shard_map/gather | solution.py:109
  50.9 1.3 %collective-permute-start.6 = (bf16[2,128,256]{2,1,0:T(8,128)(2,1)}, bf16[2,128,256]{2,1,0:T(8,128)(2,1)}, u32[]{:S(2)}, u32[]{:S(2)}) collective-permute-start(bf16[2,128,256]{2,1,0:T(8,128)(2,1)} %gather_fusion.2), channel_id=1, source_target_pairs={{0,4},{1,5},{2,6},{3,7},{8,12},{9,13},{10,14},{11,15},{16,20},{17,... | collective-permute-start | bytes 393224 | tf_op jit(solution)/shard_map/ppermute | solution.py:111
  52.2 1.2 %gather_fusion.3 = bf16[2,128,256]{2,1,0:T(8,128)(2,1)} fusion(bf16[2,128,2,256]{3,1,0,2:T(8,128)(2,1)S(1)} %copy_dynamic-update-slice_fusion, s32[2]{0:T(128)S(1)} %fusion.65), kind=kCustom, calls=%fused_computation.3 | custom fusion | bytes 262160 | tf_op jit(solution)/shard_map/gather | solution.py:109
  53.4 1.3 %collective-permute-start.7 = (bf16[2,128,256]{2,1,0:T(8,128)(2,1)}, bf16[2,128,256]{2,1,0:T(8,128)(2,1)}, u32[]{:S(2)}, u32[]{:S(2)}) collective-permute-start(bf16[2,128,256]{2,1,0:T(8,128)(2,1)} %gather_fusion.3), channel_id=1, source_target_pairs={{0,5},{1,6},{2,7},{8,13},{9,14},{10,15},{16,21},{17,22},{18,23},{2... | collective-permute-start | bytes 393224 | tf_op jit(solution)/shard_map/ppermute | solution.py:111
  54.7 1.2 %gather_fusion.4 = bf16[2,128,256]{2,1,0:T(8,128)(2,1)} fusion(bf16[2,128,2,256]{3,1,0,2:T(8,128)(2,1)S(1)} %copy_dynamic-update-slice_fusion, s32[2]{0:T(128)S(1)} %fusion.64), kind=kCustom, calls=%fused_computation.4 | custom fusion | bytes 262160 | tf_op jit(solution)/shard_map/gather | solution.py:109
  55.9 1.2 %gather_fusion.5 = bf16[2,128,256]{2,1,0:T(8,128)(2,1)} fusion(bf16[2,128,2,256]{3,1,0,2:T(8,128)(2,1)S(1)} %copy_dynamic-update-slice_fusion, s32[2]{0:T(128)S(1)} %fusion.63), kind=kCustom, calls=%fused_computation.5 | custom fusion | bytes 262160 | tf_op jit(solution)/shard_map/gather | solution.py:109
  57.1 0.0 collective-permute-done.3
  57.1 1.3 %collective-permute-start.8 = (bf16[2,128,256]{2,1,0:T(8,128)(2,1)}, bf16[2,128,256]{2,1,0:T(8,128)(2,1)S(1)}, u32[]{:S(2)}, u32[]{:S(2)}) collective-permute-start(bf16[2,128,256]{2,1,0:T(8,128)(2,1)} %gather_fusion.4), channel_id=1, source_target_pairs={{0,6},{1,7},{8,14},{9,15},{16,22},{17,23},{24,30},{25,31}} | collective-permute-start | bytes 393224 | tf_op jit(solution)/shard_map/ppermute | solution.py:111
  58.4 0.0 collective-permute-done.4
  58.4 0.7 collective-permute-start.9
  59.1 0.9 %constant_dynamic-update-slice_fusion.5 = bf16[2,1280,256]{2,1,0:T(8,128)(2,1)S(1)} fusion(bf16[2,1280,256]{2,1,0:T(8,128)(2,1)S(1)} %constant_dynamic-update-slice_fusion.6, bf16[2,128,256]{2,1,0:T(8,128)(2,1)} %collective-permute-done.4), kind=kLoop, calls=%fused_computation.50 | loop fusion | bytes 262144
  60.0 0.0 collective-permute-done.5
  60.1 0.9 %constant_dynamic-update-slice_fusion.4 = bf16[2,1280,256]{2,1,0:T(8,128)(2,1)S(1)} fusion(bf16[2,1280,256]{2,1,0:T(8,128)(2,1)S(1)} %constant_dynamic-update-slice_fusion.5, bf16[2,128,256]{2,1,0:T(8,128)(2,1)} %collective-permute-done.5), kind=kLoop, calls=%fused_computation.49 | loop fusion | bytes 262144
  61.0 11.3 %collective-permute-done.6 = bf16[2,128,256]{2,1,0:T(8,128)(2,1)} collective-permute-done((bf16[2,128,256]{2,1,0:T(8,128)(2,1)}, bf16[2,128,256]{2,1,0:T(8,128)(2,1)}, u32[]{:S(2)}, u32[]{:S(2)}) %collective-permute-start.6) | collective-permute-done | bytes 131104 | tf_op jit(solution)/shard_map/ppermute | solution.py:111
  72.3 0.9 %constant_dynamic-update-slice_fusion.3 = bf16[2,1280,256]{2,1,0:T(8,128)(2,1)S(1)} fusion(bf16[2,1280,256]{2,1,0:T(8,128)(2,1)S(1)} %constant_dynamic-update-slice_fusion.4, bf16[2,128,256]{2,1,0:T(8,128)(2,1)} %collective-permute-done.6), kind=kLoop, calls=%fused_computation.48 | loop fusion | bytes 262144
  73.2 0.0 collective-permute-done.7
  73.2 0.9 %constant_dynamic-update-slice_fusion.2 = bf16[2,1280,256]{2,1,0:T(8,128)(2,1)S(1)} fusion(bf16[2,1280,256]{2,1,0:T(8,128)(2,1)S(1)} %constant_dynamic-update-slice_fusion.3, bf16[2,128,256]{2,1,0:T(8,128)(2,1)} %collective-permute-done.7), kind=kLoop, calls=%fused_computation.47 | loop fusion | bytes 262144
  74.1 0.0 collective-permute-done.8
  74.2 0.0 collective-permute-done.9
  74.2 10.8 %shard_map.109 = bf16[256,1024]{1,0:T(8,128)(2,1)} custom-call(bf16[256,1024]{1,0:T(8,128)(2,1)S(1)} %convolution_convert_fusion.q_ref, bf16[2,1280,256]{2,1,0:T(8,128)(2,1)S(1)} %constant_dynamic-update-slice_fusion.kv_ref, s32[2,2,1,1280]{3,2,1,0:T(1,128)S(1)} %broadcast_in_dim_reshape.5.code_ref), custom_call_target="tpu_custom_call" | custom-call | flops 1342177280 | bytes 3670016 | tf_op jit(solution)/shard_map/pallas_call | solution.py:70
  (36 shorter events, 0.4 us)
Async XLA Ops:
  0.0 36.5 %copy-start = (bf16[2048,256]{1,0:T(8,128)(2,1)S(1)}, bf16[2048,256]{1,0:T(8,128)(2,1)}, u32[]{:S(2)}) copy-start(bf16[2048,256]{1,0:T(8,128)(2,1)} %param.19) | copy-start | bytes 3145732
  0.0 17.6 %copy-start.1 = (bf16[256,1024]{1,0:T(8,128)(2,1)S(1)}, bf16[256,1024]{1,0:T(8,128)(2,1)}, u32[]{:S(2)}) copy-start(bf16[256,1024]{1,0:T(8,128)(2,1)} %param.12) | copy-start | bytes 1572868
  2.3 6.3 %collective-permute-start = (f32[2,128,128]{2,1,0:T(8,128)S(1)}, f32[2,128,128]{2,1,0:T(8,128)S(1)}, u32[]{:S(2)}, u32[]{:S(2)}) collective-permute-start(f32[2,128,128]{2,1,0:T(8,128)S(1)} %get-tuple-element.25), channel_id=1, source_target_pairs={{0,1},{1,2},{2,3},{3,4},{4,5},{5,6},{6,7},{8,9},{9,10},{10,11},{11... | collective-permute-start | bytes 393224 | tf_op jit(solution)/shard_map/ppermute | solution.py:26
  8.6 7.7 %collective-permute-start.1 = (f32[2,128,128]{2,1,0:T(8,128)S(1)}, f32[2,128,128]{2,1,0:T(8,128)S(1)}, u32[]{:S(2)}, u32[]{:S(2)}) collective-permute-start(f32[2,128,128]{2,1,0:T(8,128)S(1)} %add.189), channel_id=1, source_target_pairs={{0,2},{1,3},{2,4},{3,5},{4,6},{5,7},{8,10},{9,11},{10,12},{11,13},... | collective-permute-start | bytes 393224 | tf_op jit(solution)/shard_map/ppermute | solution.py:26
  16.3 10.5 %collective-permute-start.2 = (f32[2,128,128]{2,1,0:T(8,128)S(1)}, f32[2,128,128]{2,1,0:T(8,128)S(1)}, u32[]{:S(2)}, u32[]{:S(2)}) collective-permute-start(f32[2,128,128]{2,1,0:T(8,128)S(1)} %add.191), channel_id=1, source_target_pairs={{0,4},{1,5},{2,6},{3,7},{8,12},{9,13},{10,14},{11,15},{16,20},{17,... | collective-permute-start | bytes 393224 | tf_op jit(solution)/shard_map/ppermute | solution.py:26
  30.6 0.9 %copy-start.4 = (f32[1024]{0:T(1024)S(1)}, f32[1024]{0:T(1024)}, u32[]{:S(2)}) copy-start(f32[1024]{0:T(1024)} %param.15) | copy-start | bytes 12292
  31.5 5.0 %copy-start.3 = (f32[2048]{0:T(1024)S(1)}, f32[2048]{0:T(1024)}, u32[]{:S(2)}) copy-start(f32[2048]{0:T(1024)} %param.17) | copy-start | bytes 24580
  35.5 1.0 %copy-start.5 = (bf16[256,2048]{1,0:T(8,128)(2,1)}, bf16[256,2048]{1,0:T(8,128)(2,1)S(1)}, u32[]{:S(2)}) copy-start(bf16[256,2048]{1,0:T(8,128)(2,1)S(1)} %get-tuple-element.30) | copy-start | bytes 3145732
  35.5 1.6 %copy-start.2 = (bf16[2048,256]{1,0:T(8,128)(2,1)S(1)}, bf16[2048,256]{1,0:T(8,128)(2,1)}, u32[]{:S(2)}) copy-start(bf16[2048,256]{1,0:T(8,128)(2,1)} %param.20) | copy-start | bytes 3145732
  38.9 18.2 %collective-permute-start.3 = (bf16[2,256,256]{2,1,0:T(8,128)(2,1)S(1)}, bf16[2,256,256]{2,1,0:T(8,128)(2,1)S(1)}, u32[]{:S(2)}, u32[]{:S(2)}) collective-permute-start(bf16[2,256,256]{2,1,0:T(8,128)(2,1)S(1)} %bitcast.89), channel_id=1, source_target_pairs={{0,1},{1,2},{2,3},{3,4},{4,5},{5,6},{6,7},{8,9},{9,10},{10,11},{11... | collective-permute-start | bytes 786440 | tf_op jit(solution)/shard_map/ppermute | solution.py:98
  45.9 12.5 %collective-permute-start.4 = (bf16[2,128,256]{2,1,0:T(8,128)(2,1)}, bf16[2,128,256]{2,1,0:T(8,128)(2,1)}, u32[]{:S(2)}, u32[]{:S(2)}) collective-permute-start(bf16[2,128,256]{2,1,0:T(8,128)(2,1)} %gather_fusion), channel_id=1, source_target_pairs={{0,2},{1,3},{2,4},{3,5},{4,6},{5,7},{8,10},{9,11},{10,12},{11,13},... | collective-permute-start | bytes 393224 | tf_op jit(solution)/shard_map/ppermute | solution.py:111
  48.4 11.6 %collective-permute-start.5 = (bf16[2,128,256]{2,1,0:T(8,128)(2,1)}, bf16[2,128,256]{2,1,0:T(8,128)(2,1)}, u32[]{:S(2)}, u32[]{:S(2)}) collective-permute-start(bf16[2,128,256]{2,1,0:T(8,128)(2,1)} %gather_fusion.1), channel_id=1, source_target_pairs={{0,3},{1,4},{2,5},{3,6},{4,7},{8,11},{9,12},{10,13},{11,14},{12,15... | collective-permute-start | bytes 393224 | tf_op jit(solution)/shard_map/ppermute | solution.py:111
  50.9 21.3 %collective-permute-start.6 = (bf16[2,128,256]{2,1,0:T(8,128)(2,1)}, bf16[2,128,256]{2,1,0:T(8,128)(2,1)}, u32[]{:S(2)}, u32[]{:S(2)}) collective-permute-start(bf16[2,128,256]{2,1,0:T(8,128)(2,1)} %gather_fusion.2), channel_id=1, source_target_pairs={{0,4},{1,5},{2,6},{3,7},{8,12},{9,13},{10,14},{11,15},{16,20},{17,... | collective-permute-start | bytes 393224 | tf_op jit(solution)/shard_map/ppermute | solution.py:111
  53.4 19.8 %collective-permute-start.7 = (bf16[2,128,256]{2,1,0:T(8,128)(2,1)}, bf16[2,128,256]{2,1,0:T(8,128)(2,1)}, u32[]{:S(2)}, u32[]{:S(2)}) collective-permute-start(bf16[2,128,256]{2,1,0:T(8,128)(2,1)} %gather_fusion.3), channel_id=1, source_target_pairs={{0,5},{1,6},{2,7},{8,13},{9,14},{10,15},{16,21},{17,22},{18,23},{2... | collective-permute-start | bytes 393224 | tf_op jit(solution)/shard_map/ppermute | solution.py:111
  57.1 17.0 %collective-permute-start.8 = (bf16[2,128,256]{2,1,0:T(8,128)(2,1)}, bf16[2,128,256]{2,1,0:T(8,128)(2,1)S(1)}, u32[]{:S(2)}, u32[]{:S(2)}) collective-permute-start(bf16[2,128,256]{2,1,0:T(8,128)(2,1)} %gather_fusion.4), channel_id=1, source_target_pairs={{0,6},{1,7},{8,14},{9,15},{16,22},{17,23},{24,30},{25,31}} | collective-permute-start | bytes 393224 | tf_op jit(solution)/shard_map/ppermute | solution.py:111
  58.4 15.7 %collective-permute-start.9 = (bf16[2,128,256]{2,1,0:T(8,128)(2,1)}, bf16[2,128,256]{2,1,0:T(8,128)(2,1)S(1)}, u32[]{:S(2)}, u32[]{:S(2)}) collective-permute-start(bf16[2,128,256]{2,1,0:T(8,128)(2,1)} %gather_fusion.5), channel_id=1, source_target_pairs={{0,7},{8,15},{16,23},{24,31}} | collective-permute-start | bytes 393224 | tf_op jit(solution)/shard_map/ppermute | solution.py:111

commit v3 on v2

--- a/solution.py
+++ b/solution.py
@@ -31,64 +31,82 @@
     return total
 
 
-def attention_kernel(q_ref, kv_ref, code_ref, o_ref, *, per_group):
-    keys_total = kv_ref.shape[0]
-    keys = kv_ref[:, :HEAD_DIM]
-    values = kv_ref[:, HEAD_DIM:]
+def attention_kernel(q_ref, *refs, per_group, kv_count):
+    kv_refs = refs[:kv_count]
+    code_ref = refs[kv_count]
+    o_ref = refs[kv_count + 1]
+    chunks = []
+    for ref in kv_refs:
+        for start in range(0, ref.shape[0], BLOCK):
+            chunks.append((ref, start))
     code = code_ref[...]
-    rows = lax.broadcasted_iota(jnp.int32, (BLOCK, keys_total), 0)
-    cols = lax.broadcasted_iota(jnp.int32, (BLOCK, keys_total), 1)
-    cols = jnp.bitwise_and(cols, BLOCK - 1)
-    allowed = (code == 1) | ((code == 2) & (cols <= rows))
+    rows = lax.broadcasted_iota(jnp.int32, (BLOCK, BLOCK), 0)
+    cols = lax.broadcasted_iota(jnp.int32, (BLOCK, BLOCK), 1)
+    lower = cols <= rows
+    masks = []
+    for c in range(len(chunks)):
+        part = code[:, c * BLOCK:(c + 1) * BLOCK]
+        masks.append((part == 1) | ((part == 2) & lower))
     scale = HEAD_DIM ** (-0.5)
     for p in range(per_group):
         qp = q_ref[:, p * HEAD_DIM:(p + 1) * HEAD_DIM]
-        scores = lax.dot_general(
-            qp, keys, (((1,), (1,)), ((), ())), preferred_element_type=jnp.float32
-        ) * scale
-        scores = jnp.where(allowed, scores, -jnp.inf)
-        highest = jnp.max(scores, axis=-1, keepdims=True)
-        weights = jnp.where(allowed, jnp.exp(scores - highest), 0.0)
-        total = jnp.sum(weights, axis=-1, keepdims=True)
-        probs = (weights * (1.0 / total)).astype(jnp.bfloat16)
-        out = jnp.dot(probs, values, preferred_element_type=jnp.float32)
+        scores = []
+        for (ref, start), allowed in zip(chunks, masks):
+            keys = ref[start:start + BLOCK, :HEAD_DIM]
+            s = lax.dot_general(
+                qp, keys, (((1,), (1,)), ((), ())), preferred_element_type=jnp.float32
+            ) * scale
+            scores.append(jnp.where(allowed, s, -jnp.inf))
+        highest = scores[0].max(axis=-1, keepdims=True)
+        for s in scores[1:]:
+            highest = jnp.maximum(highest, s.max(axis=-1, keepdims=True))
+        weights = [jnp.where(allowed, jnp.exp(s - highest), 0.0) for s, allowed in zip(scores, masks)]
+        total = weights[0].sum(axis=-1, keepdims=True)
+        for w in weights[1:]:
+            total = total + w.sum(axis=-1, keepdims=True)
+        inverse = 1.0 / total
+        out = None
+        for (ref, start), w in zip(chunks, weights):
+            probs = (w * inverse).astype(jnp.bfloat16)
+            values = ref[start:start + BLOCK, HEAD_DIM:]
+            term = jnp.dot(probs, values, preferred_element_type=jnp.float32)
+            out = term if out is None else out + term
         o_ref[:, p * HEAD_DIM:(p + 1) * HEAD_DIM] = out.astype(o_ref.dtype)
 
 
-def attention(soft_query, kv, code):
+def kv_spec(piece):
+    if piece.ndim == 3:
+        return pl.BlockSpec((None, piece.shape[1], 2 * HEAD_DIM), lambda g, n: (g, 0, 0))
+    return pl.BlockSpec((None, None, piece.shape[2], 2 * HEAD_DIM), lambda g, n: (g, n, 0, 0))
+
+
+def attention(soft_query, pieces, code):
     tok_count = soft_query.shape[0]
     local_blocks = tok_count // BLOCK
     per_group = HEADS // KV_HEADS
     keys_total = code.shape[-1]
     width = per_group * HEAD_DIM
-    if kv.ndim == 3:
-        kv_spec = pl.BlockSpec((None, keys_total, 2 * HEAD_DIM), lambda g, n: (g, 0, 0))
-    else:
-        kv_spec = pl.BlockSpec((None, None, keys_total, 2 * HEAD_DIM), lambda g, n: (g, n, 0, 0))
     flops = 4 * tok_count * HEADS * keys_total * HEAD_DIM
     bytes_accessed = 2 * (2 * soft_query.size + KV_HEADS * local_blocks * keys_total * 2 * HEAD_DIM)
     return pl.pallas_call(
-        functools.partial(attention_kernel, per_group=per_group),
+        functools.partial(attention_kernel, per_group=per_group, kv_count=len(pieces)),
         out_shape=jax.ShapeDtypeStruct(soft_query.shape, jnp.bfloat16),
         grid=(KV_HEADS, local_blocks),
-        in_specs=[
-            pl.BlockSpec((BLOCK, width), lambda g, n: (n, g)),
-            kv_spec,
-            pl.BlockSpec((None, None, 1, keys_total), lambda g, n: (g, n, 0, 0)),
-        ],
+        in_specs=[pl.BlockSpec((BLOCK, width), lambda g, n: (n, g))]
+        + [kv_spec(piece) for piece in pieces]
+        + [pl.BlockSpec((None, None, 1, keys_total), lambda g, n: (g, n, 0, 0))],
         out_specs=pl.BlockSpec((BLOCK, width), lambda g, n: (n, g)),
         compiler_params=pltpu.CompilerParams(vmem_limit_bytes=48 * 1024 * 1024),
         cost_estimate=pl.CostEstimate(
             flops=flops, transcendentals=tok_count * HEADS * keys_total, bytes_accessed=bytes_accessed
         ),
-    )(soft_query, kv, code)
+    )(soft_query, *pieces, code)
 
 
 def exchange_kv(packed, pattern, position, devices):
     tok_count = packed.shape[0]
     local_blocks = tok_count // BLOCK
     blocks = packed.reshape(local_blocks, BLOCK, KV_HEADS, 2 * HEAD_DIM)
-    heads = jnp.arange(KV_HEADS)
     per_head = jnp.transpose(blocks, (2, 0, 1, 3)).reshape(KV_HEADS, tok_count, 2 * HEAD_DIM)
     pieces = [per_head]
     own_ids = position * local_blocks + jnp.arange(local_blocks, dtype=jnp.int32)
@@ -100,26 +118,33 @@
         ids.append(jnp.broadcast_to(jnp.where(position >= 1, near, -1), (KV_HEADS, local_blocks)))
     mine = lax.dynamic_slice_in_dim(pattern, position * local_blocks, local_blocks, 1)
     my_far = mine[:, :, 2:].reshape(KV_HEADS, -1)
-    for shift in range(2, devices):
-        dest = jnp.minimum(position + shift, devices - 1)
-        rows = lax.dynamic_slice_in_dim(pattern, dest * local_blocks, local_blocks, 1)
-        far = rows[:, :, 2:].reshape(KV_HEADS, -1)
+    shifts = list(range(2, devices))
+    if shifts:
+        dests = jnp.minimum(position + jnp.array(shifts, jnp.int32), devices - 1)
+        firsts = dests * local_blocks
+        rows = jnp.stack(
+            [lax.dynamic_slice_in_dim(pattern, firsts[i], local_blocks, 1) for i in range(len(shifts))]
+        )
+        far = rows[:, :, :, 2:].reshape(len(shifts), KV_HEADS, -1)
         on_me = (far // local_blocks) == position
         choice = jnp.max(jnp.where(on_me, far - position * local_blocks, 0), axis=-1)
-        chosen = blocks[choice, :, heads, :]
-        pairs = [(i, i + shift) for i in range(devices - shift)]
-        pieces.append(lax.ppermute(chosen, "seq", pairs))
+        split = per_head.reshape(KV_HEADS, local_blocks, BLOCK, 2 * HEAD_DIM)
+        chosen = split[None, :, 0]
+        for j in range(1, local_blocks):
+            chosen = jnp.where((choice == j)[:, :, None, None], split[None, :, j], chosen)
+    for i, shift in enumerate(shifts):
+        pairs = [(k, k + shift) for k in range(devices - shift)]
+        pieces.append(lax.ppermute(chosen[i], "seq", pairs))
         source = position - shift
         on_src = (my_far // local_blocks) == source
         got_id = jnp.max(jnp.where(on_src, my_far, -1), axis=-1)
         ids.append(jnp.where(source >= 0, got_id, -1)[:, None])
-    table = jnp.concatenate(pieces, axis=1)
     slot_ids = jnp.concatenate(ids, axis=1)
     present = jnp.any(mine[:, :, :, None] == slot_ids[:, None, None, :], axis=2)
     present = present & (slot_ids >= 0)[:, None, :]
     own = mine[:, :, :1] == slot_ids[:, None, :]
     code = jnp.where(own, 2, present.astype(jnp.int32))
-    return table, code
+    return pieces, code
 
 
 def local(
@@ -196,7 +221,7 @@
     soft_query = jnp.dot(layer_in, soft_wq, preferred_element_type=jnp.float32).astype(jnp.bfloat16)
 
     if devices <= EXCHANGE_MAX_DEVICES:
-        kv, code = exchange_kv(packed, pattern, position, devices)
+        pieces, code = exchange_kv(packed, pattern, position, devices)
     else:
         whole = lax.all_gather(packed, "seq", axis=0, tiled=True)
         mine = lax.dynamic_slice_in_dim(pattern, position * local_blocks, local_blocks, 1)
@@ -208,9 +233,9 @@
         table = whole.reshape(-1, BLOCK, KV_HEADS, 2 * HEAD_DIM)
         group_ids = jnp.arange(KV_HEADS)[:, None, None]
         tiles = table[mine, :, group_ids, :]
-        kv = tiles.reshape(KV_HEADS, local_blocks, listed * BLOCK, 2 * HEAD_DIM)
+        pieces = [tiles.reshape(KV_HEADS, local_blocks, listed * BLOCK, 2 * HEAD_DIM)]
     code = jnp.repeat(code, BLOCK, axis=-1)[:, :, None, :]
-    return attention(soft_query, kv, code)
+    return attention(soft_query, pieces, code)
 
 
 def solution(mesh):

time: 86.1 us -> 97.9 us (1.14)
  between operations: 0.47 us -> 11.7 us
  local copies, waits for them, and re-layouts: 19.3 us -> 13.4 us
  waiting for transfers between devices: 26.4 us -> 29.5 us
  Pallas kernels: 10.8 us -> 13.5 us
    gather x6 -> x0, local copies, waits for them, and re-layouts: 7.24 us -> none  [exchange_kv(): chosen = blocks[choice, :, heads, :]]
    pallas_call x1, Pallas kernels: 10.8 us -> 13.5 us  [attention(): pl.pallas_call(functools.partial(attention_kernel, per_group=per_group, k...]
    ppermute x1, waiting for transfers between devices: 0.01 us -> 2.63 us  [exchange_kv(): pieces.append(lax.ppermute(per_head, 'seq', pairs))]
    ppermute x6, waiting for transfers between devices: 11.3 us -> 13.4 us  [exchange_kv(): pieces.append(lax.ppermute(chosen[i], 'seq', pairs))]
    ppermute x3, waiting for transfers between devices: 15.1 us -> 13.4 us  [exclusive_prefix(): got = lax.ppermute(window, axis, pairs)]
    unnamed x20 -> x15, local copies, waits for them, and re-layouts: 4.74 us -> 4.58 us
  transfers between devices with their start and end apart: 10 -> 10, of which waited for: 3 -> 5; matrix products, arithmetic and copies ran while one was open for 23% -> 14% of each run, Pallas kernels for 0% -> 0%
where the time goes in v3:
time: 97.9 us; the launch traced here: 96.9 us
  waiting for transfers between devices  29.5 us (30%)
  starting transfers between devices  13.5 us (14%)
  Pallas kernels  13.5 us (14%)
  local copies, waits for them, and re-layouts  13.4 us (14%)
  matrix products  12.6 us (13%)
  between operations  11.7 us (12%)
  other arithmetic  2.71 us (3%)
    pallas_call x1, Pallas kernels, attention(): pl.pallas_call(functools.partial(attention_kernel, per_group=per_group, k...  13.5 us
    ppermute x3, waiting for transfers between devices, exclusive_prefix(): got = lax.ppermute(window, axis, pairs)  13.4 us
    ppermute x6, waiting for transfers between devices, exchange_kv(): pieces.append(lax.ppermute(chosen[i], 'seq', pairs))  13.4 us
    ppermute x6, starting transfers between devices, exchange_kv(): pieces.append(lax.ppermute(chosen[i], 'seq', pairs))  7.12 us
    unnamed x15, local copies, waits for them, and re-layouts  4.58 us
    ppermute x3, starting transfers between devices, exclusive_prefix(): got = lax.ppermute(window, axis, pairs)  4.5 us
    dot_general x1, matrix products, local(): branch = jnp.dot(normed, lin_out_weight, preferred_element_type=jnp.float32)  3.92 us
    dot_general x1, matrix products, local(): jnp.dot(layer_in, soft_wq, preferred_element_type=jnp.float32)  3.81 us
  transfers between devices with their start and end apart: 10, of which 5 were waited for; matrix products, arithmetic and copies ran while one was open for 14% of the time, Pallas kernels for 0%

profile of v3, /device:TPU:24, one launch (start us, length us, event | category | flops | bytes accessed | tf_op | source)
XLA Modules:
  0.0 96.9 jit_solution(4483592024588476032)
XLA Ops:
  0.0 0.0 copy-start
  0.0 1.1 %reshape.184 = bf16[2,128,2,128]{3,2,1,0:T(2,128)(2,1)S(1)} reshape(bf16[256,256]{1,0:T(8,128)(2,1)} %param.14) | data formatting | bytes 262144 | tf_op jit(solution)/shard_map/reshape | solution.py:171
  1.1 0.9 reshape.185
  2.0 0.2 fusion.52
  2.3 1.9 %collective-permute-start = (f32[2,128,128]{2,1,0:T(8,128)S(1)}, f32[2,128,128]{2,1,0:T(8,128)S(1)}, u32[]{:S(2)}, u32[]{:S(2)}) collective-permute-start(f32[2,128,128]{2,1,0:T(8,128)S(1)} %get-tuple-element.27), channel_id=1, source_target_pairs={{0,1},{1,2},{2,3},{3,4},{4,5},{5,6},{6,7},{8,9},{9,10},{10,11},{11... | collective-permute-start | bytes 393224 | tf_op jit(solution)/shard_map/ppermute | solution.py:26
  4.2 0.7 minimum_multiply_fusion
  4.8 0.7 fusion.51
  13.7 0.7 constant_dynamic-update-slice_fusion.5
  15.0 0.7 constant_dynamic-update-slice_fusion.4
  16.4 0.7 constant_dynamic-update-slice_fusion.3
  17.7 0.7 constant_dynamic-update-slice_fusion.2
  19.1 0.7 constant_dynamic-update-slice_fusion.1
  20.5 0.7 constant_dynamic-update-slice_fusion
  21.2 0.4 fusion.26
  21.6 0.8 and_select_fusion.1
  22.4 0.3 fusion.39
  22.7 0.1 copy.57
  22.8 0.1 copy.58
  22.9 0.1 copy.59
  23.0 0.1 copy.60
  23.1 0.1 copy.61
  23.2 0.1 copy.62
  23.3 0.1 concatenate.22
  23.4 0.0 collective-permute-done
  23.4 1.3 %collective-permute-start.1 = (f32[2,128,128]{2,1,0:T(8,128)S(1)}, f32[2,128,128]{2,1,0:T(8,128)S(1)}, u32[]{:S(2)}, u32[]{:S(2)}) collective-permute-start(f32[2,128,128]{2,1,0:T(8,128)S(1)} %add.101), channel_id=1, source_target_pairs={{0,2},{1,3},{2,4},{3,5},{4,6},{5,7},{8,10},{9,11},{10,12},{11,13},... | collective-permute-start | bytes 393224 | tf_op jit(solution)/shard_map/ppermute | solution.py:26
  24.8 6.4 %collective-permute-done.1 = f32[2,128,128]{2,1,0:T(8,128)S(1)} collective-permute-done((f32[2,128,128]{2,1,0:T(8,128)S(1)}, f32[2,128,128]{2,1,0:T(8,128)S(1)}, u32[]{:S(2)}, u32[]{:S(2)}) %collective-permute-start.1) | collective-permute-done | bytes 131104 | tf_op jit(solution)/shard_map/ppermute | solution.py:26
  31.1 1.3 %collective-permute-start.2 = (f32[2,128,128]{2,1,0:T(8,128)S(1)}, f32[2,128,128]{2,1,0:T(8,128)S(1)}, u32[]{:S(2)}, u32[]{:S(2)}) collective-permute-start(f32[2,128,128]{2,1,0:T(8,128)S(1)} %add.103), channel_id=1, source_target_pairs={{0,4},{1,5},{2,6},{3,7},{8,12},{9,13},{10,14},{11,15},{16,20},{17,... | collective-permute-start | bytes 393224 | tf_op jit(solution)/shard_map/ppermute | solution.py:26
  32.4 0.7 constant_dynamic-slice_fusion.2
  33.2 0.4 reshape.186
  33.5 0.8 fusion.33
  34.4 0.2 compare_reduce_fusion
  34.6 7.1 %collective-permute-done.2 = f32[2,128,128]{2,1,0:T(8,128)S(1)} collective-permute-done((f32[2,128,128]{2,1,0:T(8,128)S(1)}, f32[2,128,128]{2,1,0:T(8,128)S(1)}, u32[]{:S(2)}, u32[]{:S(2)}) %collective-permute-start.2) | collective-permute-done | bytes 131104 | tf_op jit(solution)/shard_map/ppermute | solution.py:26
  41.7 0.6 convolution_bitcast_fusion.2
  42.3 1.5 %multiply_reduce_fusion = (f32[2,128,2,4]{1,3,2,0:T(4,128)S(1)}, f32[2,128,2,4,128]{1,4,3,2,0:T(8,128)}) fusion(f32[2,128,2,4,128]{1,4,3,2,0:T(8,128)S(1)} %convolution_bitcast_fusion.2, pred[128,128]{0,1:T(8,128)(4,1)S(1)} %iota_compare_fusion, bf16[2,128,2,4,128]{4,3,2,1,0:T(4,128)(2,1)S(1)} %reshape.186, bf16[2,128,2,128,1]{3,2,1,0,4:T(2,128)(2,1)S(1)} %bitcast.101, ...), kind=kOutput, calls=%fused_computation.19 | convolution fusion | flops 135526400 | bytes 2908160 | tf_op jit(solution)/shard_map/ngpts,nsge->ntgpe/dot_general | solution.py:194
  43.8 1.7 %copy.52 = f32[2,128,2,4,128]{4,3,2,1,0:T(4,128)S(1)} copy(f32[2,128,2,4,128]{1,4,3,2,0:T(8,128)} %get-tuple-element.30) | data formatting | bytes 2097152 | tf_op jit(solution)/shard_map/add | solution.py:197
  45.5 0.0 copy-start.3
  45.5 0.4 reshape.187
  45.9 0.1 copy.53
  46.1 0.3 mul.52
  46.4 0.0 copy-start.2
  46.4 3.9 %fusion.1 = (f32[256]{0:T(256)S(1)}, bf16[256,2048]{1,0:T(8,128)(2,1)S(1)}) fusion(bf16[1024,2048]{1,0:T(8,128)(2,1)} %param.17, f32[256,1024]{1,0:T(8,128)S(1)} %reshape.187, f32[32,8,8,128]{3,2,1,0:T(8,128)S(1)} %bitcast.103, f32[1024]{0:T(1024)S(1)} %copy-done.3, bf16[256,2048]{1,0:T(8,128)(2,1)} %param.12), kind=kOutput, calls=%fused_computation.4 | convolution fusion | flops 1077673728 | bytes 8393728 | tf_op jit(solution)/shard_map/dot_general | solution.py:204
  50.4 1.0 %copy-done.4 = bf16[256,2048]{1,0:T(8,128)(2,1)} copy-done((bf16[256,2048]{1,0:T(8,128)(2,1)}, bf16[256,2048]{1,0:T(8,128)(2,1)S(1)}, u32[]{:S(2)}) %copy-start.4) | copy-done | bytes 1048600
  51.3 0.5 convolution_convert_fusion.2
  51.9 2.0 %convolution_convert_fusion.1 = bf16[256,256]{1,0:T(8,128)(2,1)S(1)} fusion(bf16[2048,256]{1,0:T(8,128)(2,1)} %param.21, bf16[256,2048]{1,0:T(8,128)(2,1)} %copy-done.4, f32[2048]{0:T(1024)S(1)} %copy-done.2, f32[256]{0:T(256)S(1)} %add_rsqrt_fusion.1), kind=kOutput, calls=%fused_computation.14 | convolution fusion | flops 270598144 | bytes 2237440 | tf_op jit(solution)/shard_map/dot_general | solution.py:213
  54.1 0.1 broadcast_select_fusion
  54.2 0.1 slice_bitcast_fusion
  54.3 1.3 %collective-permute-start.4 = (bf16[2,128,256]{2,1,0:T(8,128)(2,1)S(1)}, bf16[2,128,256]{2,1,0:T(8,128)(2,1)S(1)}, u32[]{:S(2)}, u32[]{:S(2)}) collective-permute-start(bf16[2,128,256]{2,1,0:T(8,128)(2,1)S(1)} %get-tuple-element.18), channel_id=1, source_target_pairs={{0,2},{1,3},{2,4},{3,5},{4,6},{5,7},{8,10},{9,11},{10,12},{11,13},... | collective-permute-start | bytes 393224 | tf_op jit(solution)/shard_map/ppermute | solution.py:137
  55.6 1.3 %collective-permute-start.5 = (bf16[2,128,256]{2,1,0:T(8,128)(2,1)S(1)}, bf16[2,128,256]{2,1,0:T(8,128)(2,1)S(1)}, u32[]{:S(2)}, u32[]{:S(2)}) collective-permute-start(bf16[2,128,256]{2,1,0:T(8,128)(2,1)S(1)} %get-tuple-element.17), channel_id=1, source_target_pairs={{0,3},{1,4},{2,5},{3,6},{4,7},{8,11},{9,12},{10,13},{11,14},{12,15... | collective-permute-start | bytes 393224 | tf_op jit(solution)/shard_map/ppermute | solution.py:137
  56.9 0.1 compare_select_fusion.1
  57.0 0.1 broadcast_in_dim.97
  57.1 1.3 %collective-permute-start.6 = (bf16[2,128,256]{2,1,0:T(8,128)(2,1)S(1)}, bf16[2,128,256]{2,1,0:T(8,128)(2,1)S(1)}, u32[]{:S(2)}, u32[]{:S(2)}) collective-permute-start(bf16[2,128,256]{2,1,0:T(8,128)(2,1)S(1)} %get-tuple-element.16), channel_id=1, source_target_pairs={{0,4},{1,5},{2,6},{3,7},{8,12},{9,13},{10,14},{11,15},{16,20},{17,... | collective-permute-start | bytes 393224 | tf_op jit(solution)/shard_map/ppermute | solution.py:137
  58.4 1.3 %collective-permute-start.7 = (bf16[2,128,256]{2,1,0:T(8,128)(2,1)S(1)}, bf16[2,128,256]{2,1,0:T(8,128)(2,1)S(1)}, u32[]{:S(2)}, u32[]{:S(2)}) collective-permute-start(bf16[2,128,256]{2,1,0:T(8,128)(2,1)S(1)} %get-tuple-element.15), channel_id=1, source_target_pairs={{0,5},{1,6},{2,7},{8,13},{9,14},{10,15},{16,21},{17,22},{18,23},{2... | collective-permute-start | bytes 393224 | tf_op jit(solution)/shard_map/ppermute | solution.py:137
  59.7 1.3 %collective-permute-start.8 = (bf16[2,128,256]{2,1,0:T(8,128)(2,1)S(1)}, bf16[2,128,256]{2,1,0:T(8,128)(2,1)S(1)}, u32[]{:S(2)}, u32[]{:S(2)}) collective-permute-start(bf16[2,128,256]{2,1,0:T(8,128)(2,1)S(1)} %get-tuple-element.14), channel_id=1, source_target_pairs={{0,6},{1,7},{8,14},{9,15},{16,22},{17,23},{24,30},{25,31}} | collective-permute-start | bytes 393224 | tf_op jit(solution)/shard_map/ppermute | solution.py:137
  61.0 0.2 collective-permute-done.4.refs_2_
  61.2 0.7 collective-permute-start.9
  61.8 13.2 %collective-permute-done.5.refs_3_ = bf16[2,128,256]{2,1,0:T(8,128)(2,1)S(1)} collective-permute-done((bf16[2,128,256]{2,1,0:T(8,128)(2,1)S(1)}, bf16[2,128,256]{2,1,0:T(8,128)(2,1)S(1)}, u32[]{:S(2)}, u32[]{:S(2)}) %collective-permute-start.5) | collective-permute-done | bytes 131104 | tf_op jit(solution)/shard_map/ppermute | solution.py:137
  75.1 1.9 %collective-permute-start.3 = (bf16[2,256,256]{2,1,0:T(8,128)(2,1)S(1)}, bf16[2,256,256]{2,1,0:T(8,128)(2,1)S(1)}, u32[]{:S(2)}, u32[]{:S(2)}) collective-permute-start(bf16[2,256,256]{2,1,0:T(8,128)(2,1)S(1)} %bitcast.99), channel_id=1, source_target_pairs={{0,1},{1,2},{2,3},{3,4},{4,5},{5,6},{6,7},{8,9},{9,10},{10,11},{11... | collective-permute-start | bytes 786440 | tf_op jit(solution)/shard_map/ppermute | solution.py:116
  77.0 3.8 %convolution_convert_fusion.q_ref = bf16[256,1024]{1,0:T(8,128)(2,1)S(1)} fusion(bf16[2048,1024]{1,0:T(8,128)(2,1)} %param.19, bf16[256,2048]{1,0:T(8,128)(2,1)} %copy-done.4, f32[2048]{0:T(1024)S(1)} %copy-done.2, f32[256]{0:T(256)S(1)} %add_rsqrt_fusion.1), kind=kOutput, calls=%fused_computation.13 | convolution fusion | flops 1076101120 | bytes 5776384 | tf_op jit(solution)/shard_map/dot_general | solution.py:221
  80.8 0.0 collective-permute-done.6.refs_4_
  80.8 0.0 collective-permute-done.7.refs_5_
  80.8 0.0 collective-permute-done.8.refs_6_
  80.8 0.0 collective-permute-done.9.refs_7_
  80.8 2.6 %collective-permute-done.3.refs_1_ = bf16[2,256,256]{2,1,0:T(8,128)(2,1)S(1)} collective-permute-done((bf16[2,256,256]{2,1,0:T(8,128)(2,1)S(1)}, bf16[2,256,256]{2,1,0:T(8,128)(2,1)S(1)}, u32[]{:S(2)}, u32[]{:S(2)}) %collective-permute-start.3) | collective-permute-done | bytes 262176 | tf_op jit(solution)/shard_map/ppermute | solution.py:116
  83.5 13.5 %shard_map.118 = bf16[256,1024]{1,0:T(8,128)(2,1)} custom-call(bf16[256,1024]{1,0:T(8,128)(2,1)S(1)} %convolution_convert_fusion.q_ref, bf16[2,256,256]{2,1,0:T(8,128)(2,1)S(1)} %bitcast.100, bf16[2,256,256]{2,1,0:T(8,128)(2,1)S(1)} %collective-permute-done.3.refs_1_, bf16[2,128,256]{2,1,0:T(8,128)(2,1)S(1)} %collective-permute-done.4.refs_2_, ...), custom_call_target="tpu_custom_call" | custom-call | flops 1342177280 | bytes 3670016 | tf_op jit(solution)/shard_map/pallas_call | solution.py:91
  (29 shorter events, 0.4 us)
Async XLA Ops:
  0.0 51.3 %copy-start = (bf16[2048,256]{1,0:T(8,128)(2,1)S(1)}, bf16[2048,256]{1,0:T(8,128)(2,1)}, u32[]{:S(2)}) copy-start(bf16[2048,256]{1,0:T(8,128)(2,1)} %param.20) | copy-start | bytes 3145732
  0.0 33.1 %copy-start.1 = (bf16[256,1024]{1,0:T(8,128)(2,1)S(1)}, bf16[256,1024]{1,0:T(8,128)(2,1)}, u32[]{:S(2)}) copy-start(bf16[256,1024]{1,0:T(8,128)(2,1)} %param.13) | copy-start | bytes 1572868
  2.3 21.1 %collective-permute-start = (f32[2,128,128]{2,1,0:T(8,128)S(1)}, f32[2,128,128]{2,1,0:T(8,128)S(1)}, u32[]{:S(2)}, u32[]{:S(2)}) collective-permute-start(f32[2,128,128]{2,1,0:T(8,128)S(1)} %get-tuple-element.27), channel_id=1, source_target_pairs={{0,1},{1,2},{2,3},{3,4},{4,5},{5,6},{6,7},{8,9},{9,10},{10,11},{11... | collective-permute-start | bytes 393224 | tf_op jit(solution)/shard_map/ppermute | solution.py:26
  23.4 7.7 %collective-permute-start.1 = (f32[2,128,128]{2,1,0:T(8,128)S(1)}, f32[2,128,128]{2,1,0:T(8,128)S(1)}, u32[]{:S(2)}, u32[]{:S(2)}) collective-permute-start(f32[2,128,128]{2,1,0:T(8,128)S(1)} %add.101), channel_id=1, source_target_pairs={{0,2},{1,3},{2,4},{3,5},{4,6},{5,7},{8,10},{9,11},{10,12},{11,13},... | collective-permute-start | bytes 393224 | tf_op jit(solution)/shard_map/ppermute | solution.py:26
  31.1 10.5 %collective-permute-start.2 = (f32[2,128,128]{2,1,0:T(8,128)S(1)}, f32[2,128,128]{2,1,0:T(8,128)S(1)}, u32[]{:S(2)}, u32[]{:S(2)}) collective-permute-start(f32[2,128,128]{2,1,0:T(8,128)S(1)} %add.103), channel_id=1, source_target_pairs={{0,4},{1,5},{2,6},{3,7},{8,12},{9,13},{10,14},{11,15},{16,20},{17,... | collective-permute-start | bytes 393224 | tf_op jit(solution)/shard_map/ppermute | solution.py:26
  45.5 0.9 copy-start.3
  46.4 4.9 %copy-start.2 = (f32[2048]{0:T(1024)S(1)}, f32[2048]{0:T(1024)}, u32[]{:S(2)}) copy-start(f32[2048]{0:T(1024)} %param.18) | copy-start | bytes 24580
  50.3 1.0 %copy-start.4 = (bf16[256,2048]{1,0:T(8,128)(2,1)}, bf16[256,2048]{1,0:T(8,128)(2,1)S(1)}, u32[]{:S(2)}) copy-start(bf16[256,2048]{1,0:T(8,128)(2,1)S(1)} %get-tuple-element.32) | copy-start | bytes 3145732
  54.3 6.9 %collective-permute-start.4 = (bf16[2,128,256]{2,1,0:T(8,128)(2,1)S(1)}, bf16[2,128,256]{2,1,0:T(8,128)(2,1)S(1)}, u32[]{:S(2)}, u32[]{:S(2)}) collective-permute-start(bf16[2,128,256]{2,1,0:T(8,128)(2,1)S(1)} %get-tuple-element.18), channel_id=1, source_target_pairs={{0,2},{1,3},{2,4},{3,5},{4,6},{5,7},{8,10},{9,11},{10,12},{11,13},... | collective-permute-start | bytes 393224 | tf_op jit(solution)/shard_map/ppermute | solution.py:137
  55.6 19.5 %collective-permute-start.5 = (bf16[2,128,256]{2,1,0:T(8,128)(2,1)S(1)}, bf16[2,128,256]{2,1,0:T(8,128)(2,1)S(1)}, u32[]{:S(2)}, u32[]{:S(2)}) collective-permute-start(bf16[2,128,256]{2,1,0:T(8,128)(2,1)S(1)} %get-tuple-element.17), channel_id=1, source_target_pairs={{0,3},{1,4},{2,5},{3,6},{4,7},{8,11},{9,12},{10,13},{11,14},{12,15... | collective-permute-start | bytes 393224 | tf_op jit(solution)/shard_map/ppermute | solution.py:137
  57.1 23.7 %collective-permute-start.6 = (bf16[2,128,256]{2,1,0:T(8,128)(2,1)S(1)}, bf16[2,128,256]{2,1,0:T(8,128)(2,1)S(1)}, u32[]{:S(2)}, u32[]{:S(2)}) collective-permute-start(bf16[2,128,256]{2,1,0:T(8,128)(2,1)S(1)} %get-tuple-element.16), channel_id=1, source_target_pairs={{0,4},{1,5},{2,6},{3,7},{8,12},{9,13},{10,14},{11,15},{16,20},{17,... | collective-permute-start | bytes 393224 | tf_op jit(solution)/shard_map/ppermute | solution.py:137
  58.4 22.4 %collective-permute-start.7 = (bf16[2,128,256]{2,1,0:T(8,128)(2,1)S(1)}, bf16[2,128,256]{2,1,0:T(8,128)(2,1)S(1)}, u32[]{:S(2)}, u32[]{:S(2)}) collective-permute-start(bf16[2,128,256]{2,1,0:T(8,128)(2,1)S(1)} %get-tuple-element.15), channel_id=1, source_target_pairs={{0,5},{1,6},{2,7},{8,13},{9,14},{10,15},{16,21},{17,22},{18,23},{2... | collective-permute-start | bytes 393224 | tf_op jit(solution)/shard_map/ppermute | solution.py:137
  59.7 21.1 %collective-permute-start.8 = (bf16[2,128,256]{2,1,0:T(8,128)(2,1)S(1)}, bf16[2,128,256]{2,1,0:T(8,128)(2,1)S(1)}, u32[]{:S(2)}, u32[]{:S(2)}) collective-permute-start(bf16[2,128,256]{2,1,0:T(8,128)(2,1)S(1)} %get-tuple-element.14), channel_id=1, source_target_pairs={{0,6},{1,7},{8,14},{9,15},{16,22},{17,23},{24,30},{25,31}} | collective-permute-start | bytes 393224 | tf_op jit(solution)/shard_map/ppermute | solution.py:137
  61.2 19.7 %collective-permute-start.9 = (bf16[2,128,256]{2,1,0:T(8,128)(2,1)S(1)}, bf16[2,128,256]{2,1,0:T(8,128)(2,1)S(1)}, u32[]{:S(2)}, u32[]{:S(2)}) collective-permute-start(bf16[2,128,256]{2,1,0:T(8,128)(2,1)S(1)} %get-tuple-element.13), channel_id=1, source_target_pairs={{0,7},{8,15},{16,23},{24,31}} | collective-permute-start | bytes 393224 | tf_op jit(solution)/shard_map/ppermute | solution.py:137
  75.1 8.4 %collective-permute-start.3 = (bf16[2,256,256]{2,1,0:T(8,128)(2,1)S(1)}, bf16[2,256,256]{2,1,0:T(8,128)(2,1)S(1)}, u32[]{:S(2)}, u32[]{:S(2)}) collective-permute-start(bf16[2,256,256]{2,1,0:T(8,128)(2,1)S(1)} %bitcast.99), channel_id=1, source_target_pairs={{0,1},{1,2},{2,3},{3,4},{4,5},{5,6},{6,7},{8,9},{9,10},{10,11},{11... | collective-permute-start | bytes 786440 | tf_op jit(solution)/shard_map/ppermute | solution.py:116

commit v4 on v3

--- a/solution.py
+++ b/solution.py
@@ -35,42 +35,32 @@
     kv_refs = refs[:kv_count]
     code_ref = refs[kv_count]
     o_ref = refs[kv_count + 1]
-    chunks = []
+    table = refs[kv_count + 2]
+    offset = 0
     for ref in kv_refs:
-        for start in range(0, ref.shape[0], BLOCK):
-            chunks.append((ref, start))
+        rows_in = ref.shape[0]
+        table[offset:offset + rows_in, :] = ref[...]
+        offset += rows_in
+    keys_total = table.shape[0]
+    keys = table[:, :HEAD_DIM]
+    values = table[:, HEAD_DIM:]
     code = code_ref[...]
-    rows = lax.broadcasted_iota(jnp.int32, (BLOCK, BLOCK), 0)
-    cols = lax.broadcasted_iota(jnp.int32, (BLOCK, BLOCK), 1)
-    lower = cols <= rows
-    masks = []
-    for c in range(len(chunks)):
-        part = code[:, c * BLOCK:(c + 1) * BLOCK]
-        masks.append((part == 1) | ((part == 2) & lower))
+    rows = lax.broadcasted_iota(jnp.int32, (BLOCK, keys_total), 0)
+    cols = lax.broadcasted_iota(jnp.int32, (BLOCK, keys_total), 1)
+    cols = jnp.bitwise_and(cols, BLOCK - 1)
+    allowed = (code == 1) | ((code == 2) & (cols <= rows))
     scale = HEAD_DIM ** (-0.5)
     for p in range(per_group):
         qp = q_ref[:, p * HEAD_DIM:(p + 1) * HEAD_DIM]
-        scores = []
-        for (ref, start), allowed in zip(chunks, masks):
-            keys = ref[start:start + BLOCK, :HEAD_DIM]
-            s = lax.dot_general(
-                qp, keys, (((1,), (1,)), ((), ())), preferred_element_type=jnp.float32
-            ) * scale
-            scores.append(jnp.where(allowed, s, -jnp.inf))
-        highest = scores[0].max(axis=-1, keepdims=True)
-        for s in scores[1:]:
-            highest = jnp.maximum(highest, s.max(axis=-1, keepdims=True))
-        weights = [jnp.where(allowed, jnp.exp(s - highest), 0.0) for s, allowed in zip(scores, masks)]
-        total = weights[0].sum(axis=-1, keepdims=True)
-        for w in weights[1:]:
-            total = total + w.sum(axis=-1, keepdims=True)
-        inverse = 1.0 / total
-        out = None
-        for (ref, start), w in zip(chunks, weights):
-            probs = (w * inverse).astype(jnp.bfloat16)
-            values = ref[start:start + BLOCK, HEAD_DIM:]
-            term = jnp.dot(probs, values, preferred_element_type=jnp.float32)
-            out = term if out is None else out + term
+        scores = lax.dot_general(
+            qp, keys, (((1,), (1,)), ((), ())), preferred_element_type=jnp.float32
+        ) * scale
+        scores = jnp.where(allowed, scores, -jnp.inf)
+        highest = jnp.max(scores, axis=-1, keepdims=True)
+        weights = jnp.where(allowed, jnp.exp(scores - highest), 0.0)
+        total = jnp.sum(weights, axis=-1, keepdims=True)
+        probs = (weights * (1.0 / total)).astype(jnp.bfloat16)
+        out = jnp.dot(probs, values, preferred_element_type=jnp.float32)
         o_ref[:, p * HEAD_DIM:(p + 1) * HEAD_DIM] = out.astype(o_ref.dtype)
 
 
@@ -96,6 +86,7 @@
         + [kv_spec(piece) for piece in pieces]
         + [pl.BlockSpec((None, None, 1, keys_total), lambda g, n: (g, n, 0, 0))],
         out_specs=pl.BlockSpec((BLOCK, width), lambda g, n: (n, g)),
+        scratch_shapes=[pltpu.VMEM((keys_total, 2 * HEAD_DIM), jnp.bfloat16)],
         compiler_params=pltpu.CompilerParams(vmem_limit_bytes=48 * 1024 * 1024),
         cost_estimate=pl.CostEstimate(
             flops=flops, transcendentals=tok_count * HEADS * keys_total, bytes_accessed=bytes_accessed
@@ -120,25 +111,25 @@
     my_far = mine[:, :, 2:].reshape(KV_HEADS, -1)
     shifts = list(range(2, devices))
     if shifts:
-        dests = jnp.minimum(position + jnp.array(shifts, jnp.int32), devices - 1)
-        firsts = dests * local_blocks
-        rows = jnp.stack(
-            [lax.dynamic_slice_in_dim(pattern, firsts[i], local_blocks, 1) for i in range(len(shifts))]
-        )
-        far = rows[:, :, :, 2:].reshape(len(shifts), KV_HEADS, -1)
-        on_me = (far // local_blocks) == position
-        choice = jnp.max(jnp.where(on_me, far - position * local_blocks, 0), axis=-1)
+        steps = jnp.array(shifts, jnp.int32)
+        far_all = pattern[:, :, 2:].reshape(KV_HEADS, devices, -1)
+        on_me = (far_all // local_blocks) == position
+        choice_all = jnp.max(jnp.where(on_me, far_all - position * local_blocks, 0), axis=-1)
+        dest_ids = jnp.arange(devices, dtype=jnp.int32)
+        hit = dest_ids[None, :] == (position + steps)[:, None]
+        choice = jnp.sum(jnp.where(hit[:, None, :], choice_all[None], 0), axis=-1)
         split = per_head.reshape(KV_HEADS, local_blocks, BLOCK, 2 * HEAD_DIM)
         chosen = split[None, :, 0]
         for j in range(1, local_blocks):
             chosen = jnp.where((choice == j)[:, :, None, None], split[None, :, j], chosen)
+        sources = position - steps
+        on_src = (my_far[None] // local_blocks) == sources[:, None, None]
+        got = jnp.max(jnp.where(on_src, my_far[None], -1), axis=-1)
+        got = jnp.where((sources >= 0)[:, None], got, -1)
     for i, shift in enumerate(shifts):
         pairs = [(k, k + shift) for k in range(devices - shift)]
         pieces.append(lax.ppermute(chosen[i], "seq", pairs))
-        source = position - shift
-        on_src = (my_far // local_blocks) == source
-        got_id = jnp.max(jnp.where(on_src, my_far, -1), axis=-1)
-        ids.append(jnp.where(source >= 0, got_id, -1)[:, None])
+        ids.append(got[i][:, None])
     slot_ids = jnp.concatenate(ids, axis=1)
     present = jnp.any(mine[:, :, :, None] == slot_ids[:, None, None, :], axis=2)
     present = present & (slot_ids >= 0)[:, None, :]

time: 97.9 us -> 80.4 us (0.82)
  between operations: 11.7 us -> 0.39 us
  local copies, waits for them, and re-layouts: 13.4 us -> 9.38 us
  Pallas kernels: 13.5 us -> 10.9 us
    unnamed x15 -> x10, local copies, waits for them, and re-layouts: 4.58 us -> 1 us
    pallas_call x1, Pallas kernels: 13.5 us -> 10.9 us  [attention(): pl.pallas_call(functools.partial(attention_kernel, per_group=per_group, k...]
  transfers between devices with their start and end apart: 10 -> 10, of which waited for: 5 -> 5; matrix products, arithmetic and copies ran while one was open for 14% -> 13% of each run, Pallas kernels for 0% -> 0%
where the time goes in v4:
time: 80.4 us; the launch traced here: 79.7 us
  waiting for transfers between devices  29.5 us (37%)
  starting transfers between devices  13.5 us (17%)
  matrix products  12.6 us (16%)
  Pallas kernels  10.9 us (14%)
  local copies, waits for them, and re-layouts  9.38 us (12%)
  other arithmetic  3.51 us (4%)
    ppermute x3, waiting for transfers between devices, exclusive_prefix(): got = lax.ppermute(window, axis, pairs)  13.4 us
    ppermute x6, waiting for transfers between devices, exchange_kv(): pieces.append(lax.ppermute(chosen[i], 'seq', pairs))  13.4 us
    pallas_call x1, Pallas kernels, attention(): pl.pallas_call(functools.partial(attention_kernel, per_group=per_group, k...  10.9 us
    ppermute x6, starting transfers between devices, exchange_kv(): pieces.append(lax.ppermute(chosen[i], 'seq', pairs))  7.12 us
    ppermute x3, starting transfers between devices, exclusive_prefix(): got = lax.ppermute(window, axis, pairs)  4.5 us
    dot_general x1, matrix products, local(): branch = jnp.dot(normed, lin_out_weight, preferred_element_type=jnp.float32)  3.91 us
    dot_general x1, matrix products, local(): jnp.dot(layer_in, soft_wq, preferred_element_type=jnp.float32)  3.81 us
    ppermute x1, waiting for transfers between devices, exchange_kv(): pieces.append(lax.ppermute(per_head, 'seq', pairs))  2.62 us
  transfers between devices with their start and end apart: 10, of which 5 were waited for; matrix products, arithmetic and copies ran while one was open for 13% of the time, Pallas kernels for 0%

profile of v4, /device:TPU:24, one launch (start us, length us, event | category | flops | bytes accessed | tf_op | source)
XLA Modules:
  0.0 79.7 jit_solution(3548194603341201825)
XLA Ops:
  0.0 0.0 copy-start
  0.0 1.1 %reshape.210 = bf16[2,128,2,128]{3,2,1,0:T(2,128)(2,1)S(1)} reshape(bf16[256,256]{1,0:T(8,128)(2,1)} %param.14) | data formatting | bytes 262144 | tf_op jit(solution)/shard_map/reshape | solution.py:162
  1.1 0.9 %reshape.211 = bf16[2,128,2,128]{3,2,1,0:T(2,128)(2,1)S(1)} reshape(bf16[256,256]{1,0:T(8,128)(2,1)} %param.15) | data formatting | bytes 262144 | tf_op jit(solution)/shard_map/reshape | solution.py:163
  2.0 0.2 fusion.35
  2.3 1.9 %collective-permute-start = (f32[2,128,128]{2,1,0:T(8,128)S(1)}, f32[2,128,128]{2,1,0:T(8,128)S(1)}, u32[]{:S(2)}, u32[]{:S(2)}) collective-permute-start(f32[2,128,128]{2,1,0:T(8,128)S(1)} %get-tuple-element.19), channel_id=1, source_target_pairs={{0,1},{1,2},{2,3},{3,4},{4,5},{5,6},{6,7},{8,9},{9,10},{10,11},{11... | collective-permute-start | bytes 393224 | tf_op jit(solution)/shard_map/ppermute | solution.py:26
  4.2 0.9 %select_reduce_fusion = s32[2,16]{1,0:T(2,128)S(1)} fusion(s32[2,16,18]{2,1,0:T(8,128)} %param.22, s32[]{:T(128)S(6)} %mul.59, s32[]{:T(128)S(6)} %axis_index.12), kind=kLoop, calls=%fused_computation.53 | loop fusion | flops 9696 | bytes 2184 | tf_op jit(solution)/shard_map/reduce_max | solution.py:117
  5.1 0.1 reduce_max.26
  5.2 0.7 broadcast_compare_fusion.2
  5.8 0.7 broadcast_add_fusion
  6.5 0.1 iota_compare_fusion.1
  6.6 0.8 constant_dynamic-slice_fusion.1
  7.4 0.1 broadcast_in_dim_reshape.8
  7.5 0.2 fusion.29
  7.7 0.1 broadcast_select_fusion.1
  7.8 0.1 copy.57
  7.9 0.1 copy.58
  8.0 0.1 copy.59
  8.1 0.1 copy.60
  8.2 0.1 copy.61
  8.3 0.1 copy.62
  8.4 0.1 reduce_max.27
  8.5 0.2 select_reduce_fusion.1
  8.7 0.1 concatenate.22
  8.8 0.0 collective-permute-done
  8.8 1.3 %collective-permute-start.1 = (f32[2,128,128]{2,1,0:T(8,128)S(1)}, f32[2,128,128]{2,1,0:T(8,128)S(1)}, u32[]{:S(2)}, u32[]{:S(2)}) collective-permute-start(f32[2,128,128]{2,1,0:T(8,128)S(1)} %add.76), channel_id=1, source_target_pairs={{0,2},{1,3},{2,4},{3,5},{4,6},{5,7},{8,10},{9,11},{10,12},{11,13},... | collective-permute-start | bytes 393224 | tf_op jit(solution)/shard_map/ppermute | solution.py:26
  10.2 6.4 %collective-permute-done.1 = f32[2,128,128]{2,1,0:T(8,128)S(1)} collective-permute-done((f32[2,128,128]{2,1,0:T(8,128)S(1)}, f32[2,128,128]{2,1,0:T(8,128)S(1)}, u32[]{:S(2)}, u32[]{:S(2)}) %collective-permute-start.1) | collective-permute-done | bytes 131104 | tf_op jit(solution)/shard_map/ppermute | solution.py:26
  16.5 1.3 %collective-permute-start.2 = (f32[2,128,128]{2,1,0:T(8,128)S(1)}, f32[2,128,128]{2,1,0:T(8,128)S(1)}, u32[]{:S(2)}, u32[]{:S(2)}) collective-permute-start(f32[2,128,128]{2,1,0:T(8,128)S(1)} %add.78), channel_id=1, source_target_pairs={{0,4},{1,5},{2,6},{3,7},{8,12},{9,13},{10,14},{11,15},{16,20},{17,... | collective-permute-start | bytes 393224 | tf_op jit(solution)/shard_map/ppermute | solution.py:26
  17.8 0.7 constant_dynamic-slice_fusion
  18.6 0.4 reshape.212
  18.9 0.8 %dynamic-slice_reduce_fusion = s32[2,2]{1,0:T(2,128)S(1)} fusion(s32[2,16,18]{2,1,0:T(8,128)} %param.22, s32[]{:T(128)S(6)} %select_n.61), kind=kLoop, calls=%fused_computation.63 | loop fusion | bytes 36 | tf_op jit(solution)/shard_map/slice | solution.py:136
  19.8 0.2 compare_reduce_fusion
  20.0 7.1 %collective-permute-done.2 = f32[2,128,128]{2,1,0:T(8,128)S(1)} collective-permute-done((f32[2,128,128]{2,1,0:T(8,128)S(1)}, f32[2,128,128]{2,1,0:T(8,128)S(1)}, u32[]{:S(2)}, u32[]{:S(2)}) %collective-permute-start.2) | collective-permute-done | bytes 131104 | tf_op jit(solution)/shard_map/ppermute | solution.py:26
  27.1 0.6 convolution_bitcast_fusion.2
  27.7 1.5 %multiply_reduce_fusion = (f32[2,128,2,4]{1,3,2,0:T(4,128)S(1)}, f32[2,128,2,4,128]{1,4,3,2,0:T(8,128)}) fusion(f32[2,128,2,4,128]{1,4,3,2,0:T(8,128)S(1)} %convolution_bitcast_fusion.2, pred[128,128]{0,1:T(8,128)(4,1)S(1)} %iota_compare_fusion, bf16[2,128,2,4,128]{4,3,2,1,0:T(4,128)(2,1)S(1)} %reshape.212, bf16[2,128,2,128,1]{3,2,1,0,4:T(2,128)(2,1)S(1)} %bitcast.71, ...), kind=kOutput, calls=%fused_computation.19 | convolution fusion | flops 135526400 | bytes 2908160 | tf_op jit(solution)/shard_map/ngpts,nsge->ntgpe/dot_general | solution.py:185
  29.2 1.7 %copy.52 = f32[2,128,2,4,128]{4,3,2,1,0:T(4,128)S(1)} copy(f32[2,128,2,4,128]{1,4,3,2,0:T(8,128)} %get-tuple-element.22) | data formatting | bytes 2097152 | tf_op jit(solution)/shard_map/add | solution.py:188
  30.9 0.0 copy-start.3
  30.9 0.4 reshape.213
  31.3 0.1 copy.53
  31.5 0.3 mul.49
  31.8 0.0 copy-start.2
  31.8 3.9 %fusion.1 = (f32[256]{0:T(256)S(1)}, bf16[256,2048]{1,0:T(8,128)(2,1)S(1)}) fusion(bf16[1024,2048]{1,0:T(8,128)(2,1)} %param.17, f32[256,1024]{1,0:T(8,128)S(1)} %reshape.213, f32[32,8,8,128]{3,2,1,0:T(8,128)S(1)} %bitcast.73, f32[1024]{0:T(1024)S(1)} %copy-done.3, bf16[256,2048]{1,0:T(8,128)(2,1)} %param.12), kind=kOutput, calls=%fused_computation.4 | convolution fusion | flops 1077673728 | bytes 8393728 | tf_op jit(solution)/shard_map/dot_general | solution.py:195
  35.8 1.0 %copy-done.4 = bf16[256,2048]{1,0:T(8,128)(2,1)} copy-done((bf16[256,2048]{1,0:T(8,128)(2,1)}, bf16[256,2048]{1,0:T(8,128)(2,1)S(1)}, u32[]{:S(2)}) %copy-start.4) | copy-done | bytes 1048600
  36.7 0.5 convolution_convert_fusion.2
  37.3 2.0 %convolution_convert_fusion.1 = bf16[256,256]{1,0:T(8,128)(2,1)S(1)} fusion(bf16[2048,256]{1,0:T(8,128)(2,1)} %param.21, bf16[256,2048]{1,0:T(8,128)(2,1)} %copy-done.4, f32[2048]{0:T(1024)S(1)} %copy-done.2, f32[256]{0:T(256)S(1)} %add_rsqrt_fusion.1), kind=kOutput, calls=%fused_computation.14 | convolution fusion | flops 270598144 | bytes 2237440 | tf_op jit(solution)/shard_map/dot_general | solution.py:204
  39.5 0.1 broadcast_select_fusion
  39.6 0.1 slice_bitcast_fusion
  39.7 1.3 %collective-permute-start.4 = (bf16[2,128,256]{2,1,0:T(8,128)(2,1)S(1)}, bf16[2,128,256]{2,1,0:T(8,128)(2,1)S(1)}, u32[]{:S(2)}, u32[]{:S(2)}) collective-permute-start(bf16[2,128,256]{2,1,0:T(8,128)(2,1)S(1)} %get-tuple-element.10), channel_id=1, source_target_pairs={{0,2},{1,3},{2,4},{3,5},{4,6},{5,7},{8,10},{9,11},{10,12},{11,13},... | collective-permute-start | bytes 393224 | tf_op jit(solution)/shard_map/ppermute | solution.py:131
  41.0 1.3 %collective-permute-start.5 = (bf16[2,128,256]{2,1,0:T(8,128)(2,1)S(1)}, bf16[2,128,256]{2,1,0:T(8,128)(2,1)S(1)}, u32[]{:S(2)}, u32[]{:S(2)}) collective-permute-start(bf16[2,128,256]{2,1,0:T(8,128)(2,1)S(1)} %get-tuple-element.9), channel_id=1, source_target_pairs={{0,3},{1,4},{2,5},{3,6},{4,7},{8,11},{9,12},{10,13},{11,14},{12,15... | collective-permute-start | bytes 393224 | tf_op jit(solution)/shard_map/ppermute | solution.py:131
  42.3 0.1 compare_select_fusion.1
  42.4 0.1 broadcast_in_dim.135
  42.5 1.3 %collective-permute-start.6 = (bf16[2,128,256]{2,1,0:T(8,128)(2,1)S(1)}, bf16[2,128,256]{2,1,0:T(8,128)(2,1)S(1)}, u32[]{:S(2)}, u32[]{:S(2)}) collective-permute-start(bf16[2,128,256]{2,1,0:T(8,128)(2,1)S(1)} %get-tuple-element.8), channel_id=1, source_target_pairs={{0,4},{1,5},{2,6},{3,7},{8,12},{9,13},{10,14},{11,15},{16,20},{17,... | collective-permute-start | bytes 393224 | tf_op jit(solution)/shard_map/ppermute | solution.py:131
  43.8 1.3 %collective-permute-start.7 = (bf16[2,128,256]{2,1,0:T(8,128)(2,1)S(1)}, bf16[2,128,256]{2,1,0:T(8,128)(2,1)S(1)}, u32[]{:S(2)}, u32[]{:S(2)}) collective-permute-start(bf16[2,128,256]{2,1,0:T(8,128)(2,1)S(1)} %get-tuple-element.7), channel_id=1, source_target_pairs={{0,5},{1,6},{2,7},{8,13},{9,14},{10,15},{16,21},{17,22},{18,23},{2... | collective-permute-start | bytes 393224 | tf_op jit(solution)/shard_map/ppermute | solution.py:131
  45.1 1.3 %collective-permute-start.8 = (bf16[2,128,256]{2,1,0:T(8,128)(2,1)S(1)}, bf16[2,128,256]{2,1,0:T(8,128)(2,1)S(1)}, u32[]{:S(2)}, u32[]{:S(2)}) collective-permute-start(bf16[2,128,256]{2,1,0:T(8,128)(2,1)S(1)} %get-tuple-element.6), channel_id=1, source_target_pairs={{0,6},{1,7},{8,14},{9,15},{16,22},{17,23},{24,30},{25,31}} | collective-permute-start | bytes 393224 | tf_op jit(solution)/shard_map/ppermute | solution.py:131
  46.4 0.2 collective-permute-done.4.refs_2_
  46.6 0.7 collective-permute-start.9
  47.2 13.3 %collective-permute-done.5.refs_3_ = bf16[2,128,256]{2,1,0:T(8,128)(2,1)S(1)} collective-permute-done((bf16[2,128,256]{2,1,0:T(8,128)(2,1)S(1)}, bf16[2,128,256]{2,1,0:T(8,128)(2,1)S(1)}, u32[]{:S(2)}, u32[]{:S(2)}) %collective-permute-start.5) | collective-permute-done | bytes 131104 | tf_op jit(solution)/shard_map/ppermute | solution.py:131
  60.5 1.9 %collective-permute-start.3 = (bf16[2,256,256]{2,1,0:T(8,128)(2,1)S(1)}, bf16[2,256,256]{2,1,0:T(8,128)(2,1)S(1)}, u32[]{:S(2)}, u32[]{:S(2)}) collective-permute-start(bf16[2,256,256]{2,1,0:T(8,128)(2,1)S(1)} %bitcast.69), channel_id=1, source_target_pairs={{0,1},{1,2},{2,3},{3,4},{4,5},{5,6},{6,7},{8,9},{9,10},{10,11},{11... | collective-permute-start | bytes 786440 | tf_op jit(solution)/shard_map/ppermute | solution.py:107
  62.4 3.8 %convolution_convert_fusion.q_ref = bf16[256,1024]{1,0:T(8,128)(2,1)S(1)} fusion(bf16[2048,1024]{1,0:T(8,128)(2,1)} %param.19, bf16[256,2048]{1,0:T(8,128)(2,1)} %copy-done.4, f32[2048]{0:T(1024)S(1)} %copy-done.2, f32[256]{0:T(256)S(1)} %add_rsqrt_fusion.1), kind=kOutput, calls=%fused_computation.13 | convolution fusion | flops 1076101120 | bytes 5776384 | tf_op jit(solution)/shard_map/dot_general | solution.py:212
  66.2 0.0 collective-permute-done.6.refs_4_
  66.2 0.0 collective-permute-done.7.refs_5_
  66.2 0.0 collective-permute-done.8.refs_6_
  66.2 0.0 collective-permute-done.9.refs_7_
  66.3 2.6 %collective-permute-done.3.refs_1_ = bf16[2,256,256]{2,1,0:T(8,128)(2,1)S(1)} collective-permute-done((bf16[2,256,256]{2,1,0:T(8,128)(2,1)S(1)}, bf16[2,256,256]{2,1,0:T(8,128)(2,1)S(1)}, u32[]{:S(2)}, u32[]{:S(2)}) %collective-permute-start.3) | collective-permute-done | bytes 262176 | tf_op jit(solution)/shard_map/ppermute | solution.py:107
  68.9 10.9 %shard_map.118 = bf16[256,1024]{1,0:T(8,128)(2,1)} custom-call(bf16[256,1024]{1,0:T(8,128)(2,1)S(1)} %convolution_convert_fusion.q_ref, bf16[2,256,256]{2,1,0:T(8,128)(2,1)S(1)} %bitcast.70, bf16[2,256,256]{2,1,0:T(8,128)(2,1)S(1)} %collective-permute-done.3.refs_1_, bf16[2,128,256]{2,1,0:T(8,128)(2,1)S(1)} %collective-permute-done.4.refs_2_, ...), custom_call_target="tpu_custom_call" | custom-call | flops 1342177280 | bytes 3670016 | tf_op jit(solution)/shard_map/pallas_call | solution.py:81
  (28 shorter events, 0.4 us)
Async XLA Ops:
  0.0 36.7 %copy-start = (bf16[2048,256]{1,0:T(8,128)(2,1)S(1)}, bf16[2048,256]{1,0:T(8,128)(2,1)}, u32[]{:S(2)}) copy-start(bf16[2048,256]{1,0:T(8,128)(2,1)} %param.20) | copy-start | bytes 3145732
  0.0 18.6 %copy-start.1 = (bf16[256,1024]{1,0:T(8,128)(2,1)S(1)}, bf16[256,1024]{1,0:T(8,128)(2,1)}, u32[]{:S(2)}) copy-start(bf16[256,1024]{1,0:T(8,128)(2,1)} %param.13) | copy-start | bytes 1572868
  2.3 6.5 %collective-permute-start = (f32[2,128,128]{2,1,0:T(8,128)S(1)}, f32[2,128,128]{2,1,0:T(8,128)S(1)}, u32[]{:S(2)}, u32[]{:S(2)}) collective-permute-start(f32[2,128,128]{2,1,0:T(8,128)S(1)} %get-tuple-element.19), channel_id=1, source_target_pairs={{0,1},{1,2},{2,3},{3,4},{4,5},{5,6},{6,7},{8,9},{9,10},{10,11},{11... | collective-permute-start | bytes 393224 | tf_op jit(solution)/shard_map/ppermute | solution.py:26
  8.8 7.7 %collective-permute-start.1 = (f32[2,128,128]{2,1,0:T(8,128)S(1)}, f32[2,128,128]{2,1,0:T(8,128)S(1)}, u32[]{:S(2)}, u32[]{:S(2)}) collective-permute-start(f32[2,128,128]{2,1,0:T(8,128)S(1)} %add.76), channel_id=1, source_target_pairs={{0,2},{1,3},{2,4},{3,5},{4,6},{5,7},{8,10},{9,11},{10,12},{11,13},... | collective-permute-start | bytes 393224 | tf_op jit(solution)/shard_map/ppermute | solution.py:26
  16.5 10.5 %collective-permute-start.2 = (f32[2,128,128]{2,1,0:T(8,128)S(1)}, f32[2,128,128]{2,1,0:T(8,128)S(1)}, u32[]{:S(2)}, u32[]{:S(2)}) collective-permute-start(f32[2,128,128]{2,1,0:T(8,128)S(1)} %add.78), channel_id=1, source_target_pairs={{0,4},{1,5},{2,6},{3,7},{8,12},{9,13},{10,14},{11,15},{16,20},{17,... | collective-permute-start | bytes 393224 | tf_op jit(solution)/shard_map/ppermute | solution.py:26
  30.9 0.9 %copy-start.3 = (f32[1024]{0:T(1024)S(1)}, f32[1024]{0:T(1024)}, u32[]{:S(2)}) copy-start(f32[1024]{0:T(1024)} %param.16) | copy-start | bytes 12292
  31.8 4.9 %copy-start.2 = (f32[2048]{0:T(1024)S(1)}, f32[2048]{0:T(1024)}, u32[]{:S(2)}) copy-start(f32[2048]{0:T(1024)} %param.18) | copy-start | bytes 24580
  35.7 1.0 %copy-start.4 = (bf16[256,2048]{1,0:T(8,128)(2,1)}, bf16[256,2048]{1,0:T(8,128)(2,1)S(1)}, u32[]{:S(2)}) copy-start(bf16[256,2048]{1,0:T(8,128)(2,1)S(1)} %get-tuple-element.24) | copy-start | bytes 3145732
  39.7 6.9 %collective-permute-start.4 = (bf16[2,128,256]{2,1,0:T(8,128)(2,1)S(1)}, bf16[2,128,256]{2,1,0:T(8,128)(2,1)S(1)}, u32[]{:S(2)}, u32[]{:S(2)}) collective-permute-start(bf16[2,128,256]{2,1,0:T(8,128)(2,1)S(1)} %get-tuple-element.10), channel_id=1, source_target_pairs={{0,2},{1,3},{2,4},{3,5},{4,6},{5,7},{8,10},{9,11},{10,12},{11,13},... | collective-permute-start | bytes 393224 | tf_op jit(solution)/shard_map/ppermute | solution.py:131
  41.0 19.5 %collective-permute-start.5 = (bf16[2,128,256]{2,1,0:T(8,128)(2,1)S(1)}, bf16[2,128,256]{2,1,0:T(8,128)(2,1)S(1)}, u32[]{:S(2)}, u32[]{:S(2)}) collective-permute-start(bf16[2,128,256]{2,1,0:T(8,128)(2,1)S(1)} %get-tuple-element.9), channel_id=1, source_target_pairs={{0,3},{1,4},{2,5},{3,6},{4,7},{8,11},{9,12},{10,13},{11,14},{12,15... | collective-permute-start | bytes 393224 | tf_op jit(solution)/shard_map/ppermute | solution.py:131
  42.5 23.7 %collective-permute-start.6 = (bf16[2,128,256]{2,1,0:T(8,128)(2,1)S(1)}, bf16[2,128,256]{2,1,0:T(8,128)(2,1)S(1)}, u32[]{:S(2)}, u32[]{:S(2)}) collective-permute-start(bf16[2,128,256]{2,1,0:T(8,128)(2,1)S(1)} %get-tuple-element.8), channel_id=1, source_target_pairs={{0,4},{1,5},{2,6},{3,7},{8,12},{9,13},{10,14},{11,15},{16,20},{17,... | collective-permute-start | bytes 393224 | tf_op jit(solution)/shard_map/ppermute | solution.py:131
  43.8 22.4 %collective-permute-start.7 = (bf16[2,128,256]{2,1,0:T(8,128)(2,1)S(1)}, bf16[2,128,256]{2,1,0:T(8,128)(2,1)S(1)}, u32[]{:S(2)}, u32[]{:S(2)}) collective-permute-start(bf16[2,128,256]{2,1,0:T(8,128)(2,1)S(1)} %get-tuple-element.7), channel_id=1, source_target_pairs={{0,5},{1,6},{2,7},{8,13},{9,14},{10,15},{16,21},{17,22},{18,23},{2... | collective-permute-start | bytes 393224 | tf_op jit(solution)/shard_map/ppermute | solution.py:131
  45.1 21.1 %collective-permute-start.8 = (bf16[2,128,256]{2,1,0:T(8,128)(2,1)S(1)}, bf16[2,128,256]{2,1,0:T(8,128)(2,1)S(1)}, u32[]{:S(2)}, u32[]{:S(2)}) collective-permute-start(bf16[2,128,256]{2,1,0:T(8,128)(2,1)S(1)} %get-tuple-element.6), channel_id=1, source_target_pairs={{0,6},{1,7},{8,14},{9,15},{16,22},{17,23},{24,30},{25,31}} | collective-permute-start | bytes 393224 | tf_op jit(solution)/shard_map/ppermute | solution.py:131
  46.6 19.7 %collective-permute-start.9 = (bf16[2,128,256]{2,1,0:T(8,128)(2,1)S(1)}, bf16[2,128,256]{2,1,0:T(8,128)(2,1)S(1)}, u32[]{:S(2)}, u32[]{:S(2)}) collective-permute-start(bf16[2,128,256]{2,1,0:T(8,128)(2,1)S(1)} %get-tuple-element.5), channel_id=1, source_target_pairs={{0,7},{8,15},{16,23},{24,31}} | collective-permute-start | bytes 393224 | tf_op jit(solution)/shard_map/ppermute | solution.py:131
  60.5 8.4 %collective-permute-start.3 = (bf16[2,256,256]{2,1,0:T(8,128)(2,1)S(1)}, bf16[2,256,256]{2,1,0:T(8,128)(2,1)S(1)}, u32[]{:S(2)}, u32[]{:S(2)}) collective-permute-start(bf16[2,256,256]{2,1,0:T(8,128)(2,1)S(1)} %bitcast.69), channel_id=1, source_target_pairs={{0,1},{1,2},{2,3},{3,4},{4,5},{5,6},{6,7},{8,9},{9,10},{10,11},{11... | collective-permute-start | bytes 786440 | tf_op jit(solution)/shard_map/ppermute | solution.py:107

commit v5 on v4

--- a/solution.py
+++ b/solution.py
@@ -31,7 +31,8 @@
     return total
 
 
-def attention_kernel(q_ref, *refs, per_group, kv_count):
+def attention_kernel(x_ref, w_ref, *refs, per_group, kv_count):
+    q_all = jnp.dot(x_ref[...], w_ref[...], preferred_element_type=jnp.float32).astype(jnp.bfloat16)
     kv_refs = refs[:kv_count]
     code_ref = refs[kv_count]
     o_ref = refs[kv_count + 1]
@@ -51,7 +52,7 @@
     allowed = (code == 1) | ((code == 2) & (cols <= rows))
     scale = HEAD_DIM ** (-0.5)
     for p in range(per_group):
-        qp = q_ref[:, p * HEAD_DIM:(p + 1) * HEAD_DIM]
+        qp = q_all[:, p * HEAD_DIM:(p + 1) * HEAD_DIM]
         scores = lax.dot_general(
             qp, keys, (((1,), (1,)), ((), ())), preferred_element_type=jnp.float32
         ) * scale
@@ -70,19 +71,24 @@
     return pl.BlockSpec((None, None, piece.shape[2], 2 * HEAD_DIM), lambda g, n: (g, n, 0, 0))
 
 
-def attention(soft_query, pieces, code):
-    tok_count = soft_query.shape[0]
+def attention(layer_in, soft_wq, pieces, code):
+    tok_count = layer_in.shape[0]
     local_blocks = tok_count // BLOCK
     per_group = HEADS // KV_HEADS
     keys_total = code.shape[-1]
     width = per_group * HEAD_DIM
     flops = 4 * tok_count * HEADS * keys_total * HEAD_DIM
-    bytes_accessed = 2 * (2 * soft_query.size + KV_HEADS * local_blocks * keys_total * 2 * HEAD_DIM)
+    flops += 2 * tok_count * layer_in.shape[1] * soft_wq.shape[1]
+    bytes_accessed = 2 * (layer_in.size + soft_wq.size + tok_count * soft_wq.shape[1])
+    bytes_accessed += 2 * KV_HEADS * local_blocks * keys_total * 2 * HEAD_DIM
     return pl.pallas_call(
         functools.partial(attention_kernel, per_group=per_group, kv_count=len(pieces)),
-        out_shape=jax.ShapeDtypeStruct(soft_query.shape, jnp.bfloat16),
+        out_shape=jax.ShapeDtypeStruct((tok_count, soft_wq.shape[1]), jnp.bfloat16),
         grid=(KV_HEADS, local_blocks),
-        in_specs=[pl.BlockSpec((BLOCK, width), lambda g, n: (n, g))]
+        in_specs=[
+            pl.BlockSpec((BLOCK, layer_in.shape[1]), lambda g, n: (n, 0)),
+            pl.BlockSpec((soft_wq.shape[0], width), lambda g, n: (0, g)),
+        ]
         + [kv_spec(piece) for piece in pieces]
         + [pl.BlockSpec((None, None, 1, keys_total), lambda g, n: (g, n, 0, 0))],
         out_specs=pl.BlockSpec((BLOCK, width), lambda g, n: (n, g)),
@@ -91,7 +97,7 @@
         cost_estimate=pl.CostEstimate(
             flops=flops, transcendentals=tok_count * HEADS * keys_total, bytes_accessed=bytes_accessed
         ),
-    )(soft_query, *pieces, code)
+    )(layer_in, soft_wq, *pieces, code)
 
 
 def exchange_kv(packed, pattern, position, devices):
@@ -209,7 +215,6 @@
         ],
         axis=-1,
     )
-    soft_query = jnp.dot(layer_in, soft_wq, preferred_element_type=jnp.float32).astype(jnp.bfloat16)
 
     if devices <= EXCHANGE_MAX_DEVICES:
         pieces, code = exchange_kv(packed, pattern, position, devices)
@@ -226,7 +231,7 @@
         tiles = table[mine, :, group_ids, :]
         pieces = [tiles.reshape(KV_HEADS, local_blocks, listed * BLOCK, 2 * HEAD_DIM)]
     code = jnp.repeat(code, BLOCK, axis=-1)[:, :, None, :]
-    return attention(soft_query, pieces, code)
+    return attention(layer_in, soft_wq, pieces, code)
 
 
 def solution(mesh):

time: 80.4 us -> 81.2 us (level)
  the two profiles are of different devices: /device:TPU:24 before, /device:TPU:31 now
where the time goes in v5:
time: 81.2 us; the launch traced here: 80.6 us
  waiting for transfers between devices  32.9 us (41%)
  Pallas kernels  13.9 us (17%)
  starting transfers between devices  12.9 us (16%)
  local copies, waits for them, and re-layouts  9.54 us (12%)
  matrix products  7.12 us (9%)
  other arithmetic  3.81 us (5%)
    ppermute x6, waiting for transfers between devices, exchange_kv(): pieces.append(lax.ppermute(chosen[i], 'seq', pairs))  17.6 us
    ppermute x3, waiting for transfers between devices, exclusive_prefix(): got = lax.ppermute(window, axis, pairs)  15.3 us
    pallas_call x1, Pallas kernels, attention(): pl.pallas_call(functools.partial(attention_kernel, per_group=per_group, k...  13.9 us
    ppermute x6, starting transfers between devices, exchange_kv(): pieces.append(lax.ppermute(chosen[i], 'seq', pairs))  7.73 us
    dot_general x1, matrix products, local(): branch = jnp.dot(normed, lin_out_weight, preferred_element_type=jnp.float32)  3.93 us
    ppermute x3, starting transfers between devices, exclusive_prefix(): got = lax.ppermute(window, axis, pairs)  3.88 us
    add x1, local copies, waits for them, and re-layouts, local(): mixed = (inter + intra).reshape(tok_count, HEADS, HEAD_DIM)  1.67 us
  transfers between devices with their start and end apart: 10, of which 5 were waited for; matrix products, arithmetic and copies ran while one was open for 9% of the time, Pallas kernels for 0%

profile of v5, /device:TPU:31, one launch (start us, length us, event | category | flops | bytes accessed | tf_op | source)
XLA Modules:
  0.0 80.6 jit_solution(186624658106117724)
XLA Ops:
  0.0 1.1 %reshape.210 = bf16[2,128,2,128]{3,2,1,0:T(2,128)(2,1)S(1)} reshape(bf16[256,256]{1,0:T(8,128)(2,1)} %param.14) | data formatting | bytes 262144 | tf_op jit(solution)/shard_map/reshape | solution.py:168
  1.1 0.9 %reshape.211 = bf16[2,128,2,128]{3,2,1,0:T(2,128)(2,1)S(1)} reshape(bf16[256,256]{1,0:T(8,128)(2,1)} %param.15) | data formatting | bytes 262144 | tf_op jit(solution)/shard_map/reshape | solution.py:169
  2.0 0.2 fusion.32
  2.3 1.3 %collective-permute-start = (f32[2,128,128]{2,1,0:T(8,128)S(1)}, f32[2,128,128]{2,1,0:T(8,128)S(1)}, u32[]{:S(2)}, u32[]{:S(2)}) collective-permute-start(f32[2,128,128]{2,1,0:T(8,128)S(1)} %get-tuple-element.19), channel_id=1, source_target_pairs={{0,1},{1,2},{2,3},{3,4},{4,5},{5,6},{6,7},{8,9},{9,10},{10,11},{11... | collective-permute-start | bytes 393224 | tf_op jit(solution)/shard_map/ppermute | solution.py:26
  3.6 0.7 broadcast_compare_fusion.2
  4.2 0.7 broadcast_add_fusion
  4.9 0.1 iota_compare_fusion.1
  5.0 0.9 %select_reduce_fusion = s32[2,16]{1,0:T(2,128)S(1)} fusion(s32[2,16,18]{2,1,0:T(8,128)} %param.22, s32[]{:T(128)S(6)} %mul.59, s32[]{:T(128)S(6)} %axis_index.12), kind=kLoop, calls=%fused_computation.52 | loop fusion | flops 9696 | bytes 2184 | tf_op jit(solution)/shard_map/reduce_max | solution.py:123
  5.9 0.8 constant_dynamic-slice_fusion.1
  6.7 0.1 broadcast_in_dim_reshape.8
  6.8 0.2 fusion.29
  7.0 0.1 broadcast_select_fusion.1
  7.1 0.1 reduce_max.26
  7.2 0.1 copy.57
  7.3 0.1 copy.58
  7.4 0.1 copy.59
  7.5 0.1 copy.60
  7.5 0.1 copy.61
  7.6 0.1 copy.62
  7.7 0.1 reduce_max.27
  7.9 0.1 concatenate.22
  8.0 0.2 select_reduce_fusion.1
  8.2 0.0 collective-permute-done
  8.2 1.3 %collective-permute-start.1 = (f32[2,128,128]{2,1,0:T(8,128)S(1)}, f32[2,128,128]{2,1,0:T(8,128)S(1)}, u32[]{:S(2)}, u32[]{:S(2)}) collective-permute-start(f32[2,128,128]{2,1,0:T(8,128)S(1)} %add.76), channel_id=1, source_target_pairs={{0,2},{1,3},{2,4},{3,5},{4,6},{5,7},{8,10},{9,11},{10,12},{11,13},... | collective-permute-start | bytes 393224 | tf_op jit(solution)/shard_map/ppermute | solution.py:26
  9.5 6.7 %collective-permute-done.1 = f32[2,128,128]{2,1,0:T(8,128)S(1)} collective-permute-done((f32[2,128,128]{2,1,0:T(8,128)S(1)}, f32[2,128,128]{2,1,0:T(8,128)S(1)}, u32[]{:S(2)}, u32[]{:S(2)}) %collective-permute-start.1) | collective-permute-done | bytes 131104 | tf_op jit(solution)/shard_map/ppermute | solution.py:26
  16.2 1.3 %collective-permute-start.2 = (f32[2,128,128]{2,1,0:T(8,128)S(1)}, f32[2,128,128]{2,1,0:T(8,128)S(1)}, u32[]{:S(2)}, u32[]{:S(2)}) collective-permute-start(f32[2,128,128]{2,1,0:T(8,128)S(1)} %add.78), channel_id=1, source_target_pairs={{0,4},{1,5},{2,6},{3,7},{8,12},{9,13},{10,14},{11,15},{16,20},{17,... | collective-permute-start | bytes 393224 | tf_op jit(solution)/shard_map/ppermute | solution.py:26
  17.6 0.4 reshape.212
  18.0 8.5 %collective-permute-done.2 = f32[2,128,128]{2,1,0:T(8,128)S(1)} collective-permute-done((f32[2,128,128]{2,1,0:T(8,128)S(1)}, f32[2,128,128]{2,1,0:T(8,128)S(1)}, u32[]{:S(2)}, u32[]{:S(2)}) %collective-permute-start.2) | collective-permute-done | bytes 131104 | tf_op jit(solution)/shard_map/ppermute | solution.py:26
  26.5 0.6 convolution_bitcast_fusion.2
  27.2 1.5 %multiply_reduce_fusion = (f32[2,128,2,4]{1,3,2,0:T(4,128)S(1)}, f32[2,128,2,4,128]{1,4,3,2,0:T(8,128)}) fusion(f32[2,128,2,4,128]{1,4,3,2,0:T(8,128)S(1)} %convolution_bitcast_fusion.2, pred[128,128]{0,1:T(8,128)(4,1)S(1)} %iota_compare_fusion, bf16[2,128,2,4,128]{4,3,2,1,0:T(4,128)(2,1)S(1)} %reshape.212, bf16[2,128,2,128,1]{3,2,1,0,4:T(2,128)(2,1)S(1)} %bitcast.72, ...), kind=kOutput, calls=%fused_computation.18 | convolution fusion | flops 135526400 | bytes 2908160 | tf_op jit(solution)/shard_map/ngpts,nsge->ntgpe/dot_general | solution.py:191
  28.6 1.7 %copy.52 = f32[2,128,2,4,128]{4,3,2,1,0:T(4,128)S(1)} copy(f32[2,128,2,4,128]{1,4,3,2,0:T(8,128)} %get-tuple-element.22) | data formatting | bytes 2097152 | tf_op jit(solution)/shard_map/add | solution.py:194
  30.3 0.0 copy-start.4
  30.3 0.4 reshape.213
  30.8 0.1 copy.53
  30.9 0.3 mul.49
  31.2 0.0 copy-start.3
  31.3 3.9 %fusion.1 = (f32[256]{0:T(256)S(1)}, bf16[256,2048]{1,0:T(8,128)(2,1)S(1)}) fusion(bf16[1024,2048]{1,0:T(8,128)(2,1)} %param.17, f32[256,1024]{1,0:T(8,128)S(1)} %reshape.213, f32[32,8,8,128]{3,2,1,0:T(8,128)S(1)} %bitcast.74, f32[1024]{0:T(1024)S(1)} %copy-done.4, bf16[256,2048]{1,0:T(8,128)(2,1)} %param.12), kind=kOutput, calls=%fused_computation.4 | convolution fusion | flops 1077673728 | bytes 8393728 | tf_op jit(solution)/shard_map/dot_general | solution.py:201
  35.2 0.0 copy-start.1
  35.2 0.3 fusion.3.x_ref
  35.5 0.4 convolution_convert_fusion.1
  36.1 0.4 copy-done.1
  36.4 0.4 convolution_convert_fusion
  37.0 0.1 broadcast_select_fusion
  37.1 0.8 slice_bitcast_fusion
  37.9 1.3 %collective-permute-start.4 = (bf16[2,128,256]{2,1,0:T(8,128)(2,1)S(1)}, bf16[2,128,256]{2,1,0:T(8,128)(2,1)S(1)}, u32[]{:S(2)}, u32[]{:S(2)}) collective-permute-start(bf16[2,128,256]{2,1,0:T(8,128)(2,1)S(1)} %get-tuple-element.10), channel_id=1, source_target_pairs={{0,2},{1,3},{2,4},{3,5},{4,6},{5,7},{8,10},{9,11},{10,12},{11,13},... | collective-permute-start | bytes 393224 | tf_op jit(solution)/shard_map/ppermute | solution.py:137
  39.2 1.3 %collective-permute-start.5 = (bf16[2,128,256]{2,1,0:T(8,128)(2,1)S(1)}, bf16[2,128,256]{2,1,0:T(8,128)(2,1)S(1)}, u32[]{:S(2)}, u32[]{:S(2)}) collective-permute-start(bf16[2,128,256]{2,1,0:T(8,128)(2,1)S(1)} %get-tuple-element.9), channel_id=1, source_target_pairs={{0,3},{1,4},{2,5},{3,6},{4,7},{8,11},{9,12},{10,13},{11,14},{12,15... | collective-permute-start | bytes 393224 | tf_op jit(solution)/shard_map/ppermute | solution.py:137
  40.5 0.7 constant_dynamic-slice_fusion
  41.3 1.3 %collective-permute-start.3 = (bf16[2,256,256]{2,1,0:T(8,128)(2,1)S(1)}, bf16[2,256,256]{2,1,0:T(8,128)(2,1)S(1)}, u32[]{:S(2)}, u32[]{:S(2)}) collective-permute-start(bf16[2,256,256]{2,1,0:T(8,128)(2,1)S(1)} %bitcast.70), channel_id=1, source_target_pairs={{0,1},{1,2},{2,3},{3,4},{4,5},{5,6},{6,7},{8,9},{9,10},{10,11},{11... | collective-permute-start | bytes 786440 | tf_op jit(solution)/shard_map/ppermute | solution.py:113
  42.6 0.2 compare_reduce_fusion
  42.8 0.8 %dynamic-slice_reduce_fusion = s32[2,2]{1,0:T(2,128)S(1)} fusion(s32[2,16,18]{2,1,0:T(8,128)} %param.22, s32[]{:T(128)S(6)} %select_n.61), kind=kLoop, calls=%fused_computation.62 | loop fusion | bytes 36 | tf_op jit(solution)/shard_map/slice | solution.py:142
  43.6 1.3 %collective-permute-start.6 = (bf16[2,128,256]{2,1,0:T(8,128)(2,1)}, bf16[2,128,256]{2,1,0:T(8,128)(2,1)S(1)}, u32[]{:S(2)}, u32[]{:S(2)}) collective-permute-start(bf16[2,128,256]{2,1,0:T(8,128)(2,1)} %get-tuple-element.8), channel_id=1, source_target_pairs={{0,4},{1,5},{2,6},{3,7},{8,12},{9,13},{10,14},{11,15},{16,20},{17,... | collective-permute-start | bytes 393224 | tf_op jit(solution)/shard_map/ppermute | solution.py:137
  44.9 1.3 %collective-permute-start.7 = (bf16[2,128,256]{2,1,0:T(8,128)(2,1)}, bf16[2,128,256]{2,1,0:T(8,128)(2,1)S(1)}, u32[]{:S(2)}, u32[]{:S(2)}) collective-permute-start(bf16[2,128,256]{2,1,0:T(8,128)(2,1)} %get-tuple-element.7), channel_id=1, source_target_pairs={{0,5},{1,6},{2,7},{8,13},{9,14},{10,15},{16,21},{17,22},{18,23},{2... | collective-permute-start | bytes 393224 | tf_op jit(solution)/shard_map/ppermute | solution.py:137
  46.2 0.0 collective-permute-done.4.refs_2_
  46.2 1.3 %collective-permute-start.8 = (bf16[2,128,256]{2,1,0:T(8,128)(2,1)}, bf16[2,128,256]{2,1,0:T(8,128)(2,1)S(1)}, u32[]{:S(2)}, u32[]{:S(2)}) collective-permute-start(bf16[2,128,256]{2,1,0:T(8,128)(2,1)} %get-tuple-element.6), channel_id=1, source_target_pairs={{0,6},{1,7},{8,14},{9,15},{16,22},{17,23},{24,30},{25,31}} | collective-permute-start | bytes 393224 | tf_op jit(solution)/shard_map/ppermute | solution.py:137
  47.5 2.1 %collective-permute-done.5.refs_3_ = bf16[2,128,256]{2,1,0:T(8,128)(2,1)S(1)} collective-permute-done((bf16[2,128,256]{2,1,0:T(8,128)(2,1)S(1)}, bf16[2,128,256]{2,1,0:T(8,128)(2,1)S(1)}, u32[]{:S(2)}, u32[]{:S(2)}) %collective-permute-start.5) | collective-permute-done | bytes 131104 | tf_op jit(solution)/shard_map/ppermute | solution.py:137
  49.6 1.3 %collective-permute-start.9 = (bf16[2,128,256]{2,1,0:T(8,128)(2,1)}, bf16[2,128,256]{2,1,0:T(8,128)(2,1)S(1)}, u32[]{:S(2)}, u32[]{:S(2)}) collective-permute-start(bf16[2,128,256]{2,1,0:T(8,128)(2,1)} %get-tuple-element.5), channel_id=1, source_target_pairs={{0,7},{8,15},{16,23},{24,31}} | collective-permute-start | bytes 393224 | tf_op jit(solution)/shard_map/ppermute | solution.py:137
  50.9 0.1 compare_select_fusion.1
  51.0 0.1 broadcast_in_dim.135
  51.1 15.2 %collective-permute-done.6.refs_4_ = bf16[2,128,256]{2,1,0:T(8,128)(2,1)S(1)} collective-permute-done((bf16[2,128,256]{2,1,0:T(8,128)(2,1)}, bf16[2,128,256]{2,1,0:T(8,128)(2,1)S(1)}, u32[]{:S(2)}, u32[]{:S(2)}) %collective-permute-start.6) | collective-permute-done | bytes 131104 | tf_op jit(solution)/shard_map/ppermute | solution.py:137
  66.3 0.3 collective-permute-done.7.refs_5_
  66.6 0.0 collective-permute-done.8.refs_6_
  66.6 0.0 collective-permute-done.9.refs_7_
  66.6 0.0 collective-permute-done.3.refs_1_
  66.6 13.9 %shard_map.118 = bf16[256,1024]{1,0:T(8,128)(2,1)} custom-call(bf16[256,2048]{1,0:T(8,128)(2,1)S(1)} %fusion.3.x_ref, bf16[2048,1024]{1,0:T(8,128)(2,1)} %w_ref.1, bf16[2,256,256]{2,1,0:T(8,128)(2,1)S(1)} %bitcast.71, bf16[2,256,256]{2,1,0:T(8,128)(2,1)S(1)} %collective-permute-done.3.refs_1_, bf16[2,128,256]{2,1,0:T(8,128)(2,1)S(1)} %collective-permute-done.4.refs_2_, ...), custom_call_target="tpu_custom_call" | custom-call | flops 2415919104 | bytes 8388608 | tf_op jit(solution)/shard_map/pallas_call | solution.py:84
  (28 shorter events, 0.4 us)
Async XLA Ops:
  0.0 35.5 %copy-start = (bf16[2048,256]{1,0:T(8,128)(2,1)S(1)}, bf16[2048,256]{1,0:T(8,128)(2,1)}, u32[]{:S(2)}) copy-start(bf16[2048,256]{1,0:T(8,128)(2,1)} %param.20) | copy-start | bytes 3145732
  0.0 17.6 %copy-start.2 = (bf16[256,1024]{1,0:T(8,128)(2,1)S(1)}, bf16[256,1024]{1,0:T(8,128)(2,1)}, u32[]{:S(2)}) copy-start(bf16[256,1024]{1,0:T(8,128)(2,1)} %param.13) | copy-start | bytes 1572868
  2.3 5.9 %collective-permute-start = (f32[2,128,128]{2,1,0:T(8,128)S(1)}, f32[2,128,128]{2,1,0:T(8,128)S(1)}, u32[]{:S(2)}, u32[]{:S(2)}) collective-permute-start(f32[2,128,128]{2,1,0:T(8,128)S(1)} %get-tuple-element.19), channel_id=1, source_target_pairs={{0,1},{1,2},{2,3},{3,4},{4,5},{5,6},{6,7},{8,9},{9,10},{10,11},{11... | collective-permute-start | bytes 393224 | tf_op jit(solution)/shard_map/ppermute | solution.py:26
  8.2 8.0 %collective-permute-start.1 = (f32[2,128,128]{2,1,0:T(8,128)S(1)}, f32[2,128,128]{2,1,0:T(8,128)S(1)}, u32[]{:S(2)}, u32[]{:S(2)}) collective-permute-start(f32[2,128,128]{2,1,0:T(8,128)S(1)} %add.76), channel_id=1, source_target_pairs={{0,2},{1,3},{2,4},{3,5},{4,6},{5,7},{8,10},{9,11},{10,12},{11,13},... | collective-permute-start | bytes 393224 | tf_op jit(solution)/shard_map/ppermute | solution.py:26
  16.2 10.3 %collective-permute-start.2 = (f32[2,128,128]{2,1,0:T(8,128)S(1)}, f32[2,128,128]{2,1,0:T(8,128)S(1)}, u32[]{:S(2)}, u32[]{:S(2)}) collective-permute-start(f32[2,128,128]{2,1,0:T(8,128)S(1)} %add.78), channel_id=1, source_target_pairs={{0,4},{1,5},{2,6},{3,7},{8,12},{9,13},{10,14},{11,15},{16,20},{17,... | collective-permute-start | bytes 393224 | tf_op jit(solution)/shard_map/ppermute | solution.py:26
  30.3 0.9 %copy-start.4 = (f32[1024]{0:T(1024)S(1)}, f32[1024]{0:T(1024)}, u32[]{:S(2)}) copy-start(f32[1024]{0:T(1024)} %param.16) | copy-start | bytes 12292
  31.2 4.0 %copy-start.3 = (f32[2048]{0:T(1024)S(1)}, f32[2048]{0:T(1024)}, u32[]{:S(2)}) copy-start(f32[2048]{0:T(1024)} %param.18) | copy-start | bytes 24580
  35.2 1.2 %copy-start.1 = (bf16[2048,256]{1,0:T(8,128)(2,1)S(1)}, bf16[2048,256]{1,0:T(8,128)(2,1)}, u32[]{:S(2)}) copy-start(bf16[2048,256]{1,0:T(8,128)(2,1)} %param.21) | copy-start | bytes 3145732
  37.9 8.3 %collective-permute-start.4 = (bf16[2,128,256]{2,1,0:T(8,128)(2,1)S(1)}, bf16[2,128,256]{2,1,0:T(8,128)(2,1)S(1)}, u32[]{:S(2)}, u32[]{:S(2)}) collective-permute-start(bf16[2,128,256]{2,1,0:T(8,128)(2,1)S(1)} %get-tuple-element.10), channel_id=1, source_target_pairs={{0,2},{1,3},{2,4},{3,5},{4,6},{5,7},{8,10},{9,11},{10,12},{11,13},... | collective-permute-start | bytes 393224 | tf_op jit(solution)/shard_map/ppermute | solution.py:137
  39.2 10.4 %collective-permute-start.5 = (bf16[2,128,256]{2,1,0:T(8,128)(2,1)S(1)}, bf16[2,128,256]{2,1,0:T(8,128)(2,1)S(1)}, u32[]{:S(2)}, u32[]{:S(2)}) collective-permute-start(bf16[2,128,256]{2,1,0:T(8,128)(2,1)S(1)} %get-tuple-element.9), channel_id=1, source_target_pairs={{0,3},{1,4},{2,5},{3,6},{4,7},{8,11},{9,12},{10,13},{11,14},{12,15... | collective-permute-start | bytes 393224 | tf_op jit(solution)/shard_map/ppermute | solution.py:137
  41.3 25.4 %collective-permute-start.3 = (bf16[2,256,256]{2,1,0:T(8,128)(2,1)S(1)}, bf16[2,256,256]{2,1,0:T(8,128)(2,1)S(1)}, u32[]{:S(2)}, u32[]{:S(2)}) collective-permute-start(bf16[2,256,256]{2,1,0:T(8,128)(2,1)S(1)} %bitcast.70), channel_id=1, source_target_pairs={{0,1},{1,2},{2,3},{3,4},{4,5},{5,6},{6,7},{8,9},{9,10},{10,11},{11... | collective-permute-start | bytes 786440 | tf_op jit(solution)/shard_map/ppermute | solution.py:113
  43.6 22.7 %collective-permute-start.6 = (bf16[2,128,256]{2,1,0:T(8,128)(2,1)}, bf16[2,128,256]{2,1,0:T(8,128)(2,1)S(1)}, u32[]{:S(2)}, u32[]{:S(2)}) collective-permute-start(bf16[2,128,256]{2,1,0:T(8,128)(2,1)} %get-tuple-element.8), channel_id=1, source_target_pairs={{0,4},{1,5},{2,6},{3,7},{8,12},{9,13},{10,14},{11,15},{16,20},{17,... | collective-permute-start | bytes 393224 | tf_op jit(solution)/shard_map/ppermute | solution.py:137
  44.9 21.7 %collective-permute-start.7 = (bf16[2,128,256]{2,1,0:T(8,128)(2,1)}, bf16[2,128,256]{2,1,0:T(8,128)(2,1)S(1)}, u32[]{:S(2)}, u32[]{:S(2)}) collective-permute-start(bf16[2,128,256]{2,1,0:T(8,128)(2,1)} %get-tuple-element.7), channel_id=1, source_target_pairs={{0,5},{1,6},{2,7},{8,13},{9,14},{10,15},{16,21},{17,22},{18,23},{2... | collective-permute-start | bytes 393224 | tf_op jit(solution)/shard_map/ppermute | solution.py:137
  46.2 20.4 %collective-permute-start.8 = (bf16[2,128,256]{2,1,0:T(8,128)(2,1)}, bf16[2,128,256]{2,1,0:T(8,128)(2,1)S(1)}, u32[]{:S(2)}, u32[]{:S(2)}) collective-permute-start(bf16[2,128,256]{2,1,0:T(8,128)(2,1)} %get-tuple-element.6), channel_id=1, source_target_pairs={{0,6},{1,7},{8,14},{9,15},{16,22},{17,23},{24,30},{25,31}} | collective-permute-start | bytes 393224 | tf_op jit(solution)/shard_map/ppermute | solution.py:137
  49.6 17.0 %collective-permute-start.9 = (bf16[2,128,256]{2,1,0:T(8,128)(2,1)}, bf16[2,128,256]{2,1,0:T(8,128)(2,1)S(1)}, u32[]{:S(2)}, u32[]{:S(2)}) collective-permute-start(bf16[2,128,256]{2,1,0:T(8,128)(2,1)} %get-tuple-element.5), channel_id=1, source_target_pairs={{0,7},{8,15},{16,23},{24,31}} | collective-permute-start | bytes 393224 | tf_op jit(solution)/shard_map/ppermute | solution.py:137

commit v6 on v4

--- a/solution.py
+++ b/solution.py
@@ -6,6 +6,7 @@
 from jax.experimental import pallas as pl
 from jax.experimental.pallas import tpu as pltpu
 from jax.sharding import PartitionSpec as P
+
 
 HEAD_DIM = 128
 HEADS = 8
@@ -31,20 +32,63 @@
     return total
 
 
-def attention_kernel(q_ref, *refs, per_group, kv_count):
+def slot_ids_exchange(pat_ref, pos, g, nblk, listed, devices, local_blocks):
+    ids = [pos * local_blocks + c for c in range(local_blocks)]
+    ids += [jnp.where(pos >= 1, (pos - 1) * local_blocks + c, -1) for c in range(local_blocks)]
+    for shift in range(2, devices):
+        src = pos - shift
+        low = src * local_blocks
+        best = jnp.int32(-1)
+        for j in range(local_blocks):
+            row = (g * nblk + pos * local_blocks + j) * listed
+            for k in range(2, listed):
+                entry = pat_ref[row + k]
+                inside = (entry >= low) & (entry < low + local_blocks)
+                best = jnp.where(inside & (entry > best), entry, best)
+        ids.append(jnp.where(src >= 0, best, -1))
+    return ids
+
+
+def attention_kernel(pat_ref, pos_ref, q_ref, *refs, per_group, kv_count, devices, exchange, nblk, listed):
     kv_refs = refs[:kv_count]
-    code_ref = refs[kv_count]
-    o_ref = refs[kv_count + 1]
-    table = refs[kv_count + 2]
+    o_ref = refs[kv_count]
+    table = refs[kv_count + 1]
+    g = pl.program_id(0)
+    n = pl.program_id(1)
+    pos = pos_ref[0]
     offset = 0
     for ref in kv_refs:
         rows_in = ref.shape[0]
         table[offset:offset + rows_in, :] = ref[...]
         offset += rows_in
     keys_total = table.shape[0]
+    slots = keys_total // BLOCK
+    lb = nblk // devices
+    row = (g * nblk + pos * lb + n) * listed
+    first = pat_ref[row]
+    if exchange:
+        ids = slot_ids_exchange(pat_ref, pos, g, nblk, listed, devices, lb)
+        codes = []
+        for bid in ids:
+            hit = jnp.int32(0)
+            for j in range(listed):
+                hit = jnp.where(pat_ref[row + j] == bid, 1, hit)
+            hit = jnp.where(bid >= 0, hit, 0)
+            codes.append(jnp.where(bid == first, 2, hit))
+    else:
+        codes = [jnp.int32(2)]
+        for c in range(1, slots):
+            entry = pat_ref[row + c]
+            seen = jnp.int32(0)
+            for j in range(c):
+                seen = jnp.where(pat_ref[row + j] == entry, 1, seen)
+            codes.append(1 - seen)
+    slot_of_col = lax.broadcasted_iota(jnp.int32, (1, keys_total), 1) // BLOCK
+    code = jnp.zeros((1, keys_total), jnp.int32)
+    for c in range(slots):
+        code = jnp.where(slot_of_col == c, codes[c], code)
     keys = table[:, :HEAD_DIM]
     values = table[:, HEAD_DIM:]
-    code = code_ref[...]
     rows = lax.broadcasted_iota(jnp.int32, (BLOCK, keys_total), 0)
     cols = lax.broadcasted_iota(jnp.int32, (BLOCK, keys_total), 1)
     cols = jnp.bitwise_and(cols, BLOCK - 1)
@@ -66,32 +110,44 @@
 
 def kv_spec(piece):
     if piece.ndim == 3:
-        return pl.BlockSpec((None, piece.shape[1], 2 * HEAD_DIM), lambda g, n: (g, 0, 0))
-    return pl.BlockSpec((None, None, piece.shape[2], 2 * HEAD_DIM), lambda g, n: (g, n, 0, 0))
-
-
-def attention(soft_query, pieces, code):
+        return pl.BlockSpec((None, piece.shape[1], 2 * HEAD_DIM), lambda g, n, pat, pos: (g, 0, 0))
+    return pl.BlockSpec((None, None, piece.shape[2], 2 * HEAD_DIM), lambda g, n, pat, pos: (g, n, 0, 0))
+
+
+def attention(soft_query, pieces, pattern, position, devices, exchange):
     tok_count = soft_query.shape[0]
     local_blocks = tok_count // BLOCK
     per_group = HEADS // KV_HEADS
-    keys_total = code.shape[-1]
+    keys_total = sum(piece.shape[-2] for piece in pieces)
     width = per_group * HEAD_DIM
     flops = 4 * tok_count * HEADS * keys_total * HEAD_DIM
     bytes_accessed = 2 * (2 * soft_query.size + KV_HEADS * local_blocks * keys_total * 2 * HEAD_DIM)
+    kernel = functools.partial(
+        attention_kernel,
+        per_group=per_group,
+        kv_count=len(pieces),
+        devices=devices,
+        exchange=exchange,
+        nblk=pattern.shape[1],
+        listed=pattern.shape[2],
+    )
+    grid_spec = pltpu.PrefetchScalarGridSpec(
+        num_scalar_prefetch=2,
+        grid=(KV_HEADS, local_blocks),
+        in_specs=[pl.BlockSpec((BLOCK, width), lambda g, n, pat, pos: (n, g))]
+        + [kv_spec(piece) for piece in pieces],
+        out_specs=pl.BlockSpec((BLOCK, width), lambda g, n, pat, pos: (n, g)),
+        scratch_shapes=[pltpu.VMEM((keys_total, 2 * HEAD_DIM), jnp.bfloat16)],
+    )
     return pl.pallas_call(
-        functools.partial(attention_kernel, per_group=per_group, kv_count=len(pieces)),
+        kernel,
         out_shape=jax.ShapeDtypeStruct(soft_query.shape, jnp.bfloat16),
-        grid=(KV_HEADS, local_blocks),
-        in_specs=[pl.BlockSpec((BLOCK, width), lambda g, n: (n, g))]
-        + [kv_spec(piece) for piece in pieces]
-        + [pl.BlockSpec((None, None, 1, keys_total), lambda g, n: (g, n, 0, 0))],
-        out_specs=pl.BlockSpec((BLOCK, width), lambda g, n: (n, g)),
-        scratch_shapes=[pltpu.VMEM((keys_total, 2 * HEAD_DIM), jnp.bfloat16)],
+        grid_spec=grid_spec,
         compiler_params=pltpu.CompilerParams(vmem_limit_bytes=48 * 1024 * 1024),
         cost_estimate=pl.CostEstimate(
             flops=flops, transcendentals=tok_count * HEADS * keys_total, bytes_accessed=bytes_accessed
         ),
-    )(soft_query, *pieces, code)
+    )(pattern.reshape(-1), position.reshape(1).astype(jnp.int32), soft_query, *pieces)
 
 
 def exchange_kv(packed, pattern, position, devices):
@@ -100,15 +156,9 @@
     blocks = packed.reshape(local_blocks, BLOCK, KV_HEADS, 2 * HEAD_DIM)
     per_head = jnp.transpose(blocks, (2, 0, 1, 3)).reshape(KV_HEADS, tok_count, 2 * HEAD_DIM)
     pieces = [per_head]
-    own_ids = position * local_blocks + jnp.arange(local_blocks, dtype=jnp.int32)
-    ids = [jnp.broadcast_to(own_ids, (KV_HEADS, local_blocks))]
     if devices > 1:
         pairs = [(i, i + 1) for i in range(devices - 1)]
         pieces.append(lax.ppermute(per_head, "seq", pairs))
-        near = own_ids - local_blocks
-        ids.append(jnp.broadcast_to(jnp.where(position >= 1, near, -1), (KV_HEADS, local_blocks)))
-    mine = lax.dynamic_slice_in_dim(pattern, position * local_blocks, local_blocks, 1)
-    my_far = mine[:, :, 2:].reshape(KV_HEADS, -1)
     shifts = list(range(2, devices))
     if shifts:
         steps = jnp.array(shifts, jnp.int32)
@@ -122,20 +172,10 @@
         chosen = split[None, :, 0]
         for j in range(1, local_blocks):
             chosen = jnp.where((choice == j)[:, :, None, None], split[None, :, j], chosen)
-        sources = position - steps
-        on_src = (my_far[None] // local_blocks) == sources[:, None, None]
-        got = jnp.max(jnp.where(on_src, my_far[None], -1), axis=-1)
-        got = jnp.where((sources >= 0)[:, None], got, -1)
     for i, shift in enumerate(shifts):
         pairs = [(k, k + shift) for k in range(devices - shift)]
         pieces.append(lax.ppermute(chosen[i], "seq", pairs))
-        ids.append(got[i][:, None])
-    slot_ids = jnp.concatenate(ids, axis=1)
-    present = jnp.any(mine[:, :, :, None] == slot_ids[:, None, None, :], axis=2)
-    present = present & (slot_ids >= 0)[:, None, :]
-    own = mine[:, :, :1] == slot_ids[:, None, :]
-    code = jnp.where(own, 2, present.astype(jnp.int32))
-    return pieces, code
+    return pieces
 
 
 def local(
@@ -211,22 +251,17 @@
     )
     soft_query = jnp.dot(layer_in, soft_wq, preferred_element_type=jnp.float32).astype(jnp.bfloat16)
 
-    if devices <= EXCHANGE_MAX_DEVICES:
-        pieces, code = exchange_kv(packed, pattern, position, devices)
+    exchange = devices <= EXCHANGE_MAX_DEVICES
+    if exchange:
+        pieces = exchange_kv(packed, pattern, position, devices)
     else:
         whole = lax.all_gather(packed, "seq", axis=0, tiled=True)
         mine = lax.dynamic_slice_in_dim(pattern, position * local_blocks, local_blocks, 1)
-        same = mine[..., :, None] == mine[..., None, :]
-        earlier = jnp.arange(listed)[None, :] < jnp.arange(listed)[:, None]
-        repeated = jnp.any(same & earlier, axis=-1)
-        first_slot = (jnp.arange(listed) == 0)[None, None, :]
-        code = jnp.where(first_slot, 2, jnp.logical_not(repeated).astype(jnp.int32))
         table = whole.reshape(-1, BLOCK, KV_HEADS, 2 * HEAD_DIM)
         group_ids = jnp.arange(KV_HEADS)[:, None, None]
         tiles = table[mine, :, group_ids, :]
         pieces = [tiles.reshape(KV_HEADS, local_blocks, listed * BLOCK, 2 * HEAD_DIM)]
-    code = jnp.repeat(code, BLOCK, axis=-1)[:, :, None, :]
-    return attention(soft_query, pieces, code)
+    return attention(soft_query, pieces, pattern, position, devices, exchange)
 
 
 def solution(mesh):
@@ -244,5 +279,6 @@
         P(),
     )
     out_specs = P(("dp", "seq"), None)
-    body = functools.partial(local, devices=mesh.shape["seq"])
+    devices = mesh.shape["seq"]
+    body = functools.partial(local, devices=devices)
     return jax.shard_map(body, mesh=mesh, in_specs=in_specs, out_specs=out_specs, check_vma=False)

time: 80.4 us -> 77.3 us (0.961)
  the two profiles are of different devices: /device:TPU:24 before, /device:TPU:16 now
where the time goes in v6:
time: 77.3 us; the launch traced here: 76.8 us
  waiting for transfers between devices  24.1 us (31%)
  starting transfers between devices  18.5 us (24%)
  Pallas kernels  12.8 us (17%)
  matrix products  12.6 us (16%)
  local copies, waits for them, and re-layouts  6.28 us (8%)
  other arithmetic  2.21 us (3%)
    pallas_call x1, Pallas kernels, attention(): pl.pallas_call(kernel, out_shape=jax.ShapeDtypeStruct(soft_query.shape, j...  12.8 us
    ppermute x3, waiting for transfers between devices, exclusive_prefix(): got = lax.ppermute(window, axis, pairs)  11.8 us
    ppermute x1, waiting for transfers between devices, exchange_kv(): pieces.append(lax.ppermute(per_head, 'seq', pairs))  10.4 us
    ppermute x6, starting transfers between devices, exchange_kv(): pieces.append(lax.ppermute(chosen[i], 'seq', pairs))  9.91 us
    ppermute x3, starting transfers between devices, exclusive_prefix(): got = lax.ppermute(window, axis, pairs)  6.7 us
    dot_general x1, matrix products, local(): branch = jnp.dot(normed, lin_out_weight, preferred_element_type=jnp.float32)  3.91 us
    dot_general x1, matrix products, local(): jnp.dot(layer_in, soft_wq, preferred_element_type=jnp.float32)  3.82 us
    dot_general x1, matrix products, local(): jnp.dot(layer_in, soft_wv, preferred_element_type=jnp.float32)  2.03 us
  transfers between devices with their start and end apart: 10, of which 5 were waited for; matrix products, arithmetic and copies ran while one was open for 8% of the time, Pallas kernels for 0%

profile of v6, /device:TPU:16, one launch (start us, length us, event | category | flops | bytes accessed | tf_op | source)
XLA Modules:
  0.0 76.8 jit_solution(3224838971235342586)
XLA Ops:
  0.0 0.0 copy-start
  0.0 0.0 copy-start.1
  0.0 1.1 %reshape.88 = bf16[2,128,2,128]{3,2,1,0:T(2,128)(2,1)S(1)} reshape(bf16[256,256]{1,0:T(8,128)(2,1)} %param.14) | data formatting | bytes 262144 | tf_op jit(solution)/shard_map/reshape | solution.py:202
  1.1 0.9 %reshape.89 = bf16[2,128,2,128]{3,2,1,0:T(2,128)(2,1)S(1)} reshape(bf16[256,256]{1,0:T(8,128)(2,1)} %param.15) | data formatting | bytes 262144 | tf_op jit(solution)/shard_map/reshape | solution.py:203
  2.0 0.2 fusion.34
  2.3 1.9 %collective-permute-start = (f32[2,128,128]{2,1,0:T(8,128)S(1)}, f32[2,128,128]{2,1,0:T(8,128)S(1)}, u32[]{:S(2)}, u32[]{:S(2)}) collective-permute-start(f32[2,128,128]{2,1,0:T(8,128)S(1)} %get-tuple-element.13), channel_id=1, source_target_pairs={{0,1},{1,2},{2,3},{3,4},{4,5},{5,6},{6,7},{8,9},{9,10},{10,11},{11... | collective-permute-start | bytes 393224 | tf_op jit(solution)/shard_map/ppermute | solution.py:27
  4.2 0.7 broadcast_add_fusion
  4.8 0.1 iota_compare_fusion.1
  4.9 3.6 %collective-permute-done = f32[2,128,128]{2,1,0:T(8,128)S(1)} collective-permute-done((f32[2,128,128]{2,1,0:T(8,128)S(1)}, f32[2,128,128]{2,1,0:T(8,128)S(1)}, u32[]{:S(2)}, u32[]{:S(2)}) %collective-permute-start) | collective-permute-done | bytes 131104 | tf_op jit(solution)/shard_map/ppermute | solution.py:27
  8.6 3.5 %collective-permute-start.1 = (f32[2,128,128]{2,1,0:T(8,128)S(1)}, f32[2,128,128]{2,1,0:T(8,128)S(1)}, u32[]{:S(2)}, u32[]{:S(2)}) collective-permute-start(f32[2,128,128]{2,1,0:T(8,128)S(1)} %add.60), channel_id=1, source_target_pairs={{0,2},{1,3},{2,4},{3,5},{4,6},{5,7},{8,10},{9,11},{10,12},{11,13},... | collective-permute-start | bytes 393224 | tf_op jit(solution)/shard_map/ppermute | solution.py:27
  12.0 0.9 %select_reduce_fusion = s32[2,16]{1,0:T(2,128)S(1)} fusion(s32[2,16,18]{2,1,0:T(8,128)} %param.22, s32[]{:T(128)S(6)} %mul.57, s32[]{:T(128)} %axis_index.12), kind=kLoop, calls=%fused_computation.52 | loop fusion | flops 9696 | bytes 2184 | tf_op jit(solution)/shard_map/reduce_max | solution.py:167
  13.0 0.1 reduce_max.14
  13.0 0.1 reduce_max.18
  13.2 0.2 select_reduce_fusion.1
  13.4 2.1 %collective-permute-done.1 = f32[2,128,128]{2,1,0:T(8,128)S(1)} collective-permute-done((f32[2,128,128]{2,1,0:T(8,128)S(1)}, f32[2,128,128]{2,1,0:T(8,128)S(1)}, u32[]{:S(2)}, u32[]{:S(2)}) %collective-permute-start.1) | collective-permute-done | bytes 131104 | tf_op jit(solution)/shard_map/ppermute | solution.py:27
  15.4 1.3 %collective-permute-start.2 = (f32[2,128,128]{2,1,0:T(8,128)S(1)}, f32[2,128,128]{2,1,0:T(8,128)S(1)}, u32[]{:S(2)}, u32[]{:S(2)}) collective-permute-start(f32[2,128,128]{2,1,0:T(8,128)S(1)} %add.62), channel_id=1, source_target_pairs={{0,4},{1,5},{2,6},{3,7},{8,12},{9,13},{10,14},{11,15},{16,20},{17,... | collective-permute-start | bytes 393224 | tf_op jit(solution)/shard_map/ppermute | solution.py:27
  16.8 0.0 copy-done.1
  16.8 0.4 reshape.90
  17.2 6.1 %collective-permute-done.2 = f32[2,128,128]{2,1,0:T(8,128)S(1)} collective-permute-done((f32[2,128,128]{2,1,0:T(8,128)S(1)}, f32[2,128,128]{2,1,0:T(8,128)S(1)}, u32[]{:S(2)}, u32[]{:S(2)}) %collective-permute-start.2) | collective-permute-done | bytes 131104 | tf_op jit(solution)/shard_map/ppermute | solution.py:27
  23.3 0.6 convolution_bitcast_fusion.2
  23.9 1.5 %multiply_reduce_fusion = (f32[2,128,2,4]{1,3,2,0:T(4,128)S(1)}, f32[2,128,2,4,128]{1,4,3,2,0:T(8,128)}) fusion(f32[2,128,2,4,128]{1,4,3,2,0:T(8,128)S(1)} %convolution_bitcast_fusion.2, pred[128,128]{0,1:T(8,128)(4,1)S(1)} %iota_compare_fusion, bf16[2,128,2,4,128]{4,3,2,1,0:T(4,128)(2,1)S(1)} %reshape.90, bf16[2,128,2,128,1]{3,2,1,0,4:T(2,128)(2,1)S(1)} %bitcast.60, ...), kind=kOutput, calls=%fused_computation.19 | convolution fusion | flops 135526400 | bytes 2908160 | tf_op jit(solution)/shard_map/ngpts,nsge->ntgpe/dot_general | solution.py:225
  25.4 1.7 %copy.39 = f32[2,128,2,4,128]{4,3,2,1,0:T(4,128)S(1)} copy(f32[2,128,2,4,128]{1,4,3,2,0:T(8,128)} %get-tuple-element.16) | data formatting | bytes 2097152 | tf_op jit(solution)/shard_map/add | solution.py:228
  27.1 0.0 copy-start.4
  27.1 0.4 reshape.91
  27.5 0.1 copy.40
  27.7 0.3 mul.47
  28.0 0.0 copy-done.4
  28.0 0.0 copy-start.3
  28.0 3.9 %fusion.1 = (f32[256]{0:T(256)S(1)}, bf16[256,2048]{1,0:T(8,128)(2,1)S(1)}) fusion(bf16[1024,2048]{1,0:T(8,128)(2,1)} %param.17, f32[256,1024]{1,0:T(8,128)S(1)} %reshape.91, f32[32,8,8,128]{3,2,1,0:T(8,128)S(1)} %bitcast.62, f32[1024]{0:T(1024)S(1)} %copy-done.4, bf16[256,2048]{1,0:T(8,128)(2,1)} %param.12), kind=kOutput, calls=%fused_computation.4 | convolution fusion | flops 1077673728 | bytes 8393728 | tf_op jit(solution)/shard_map/dot_general | solution.py:235
  31.9 0.0 copy-start.5
  32.0 1.0 %copy-done.5 = bf16[256,2048]{1,0:T(8,128)(2,1)} copy-done((bf16[256,2048]{1,0:T(8,128)(2,1)}, bf16[256,2048]{1,0:T(8,128)(2,1)S(1)}, u32[]{:S(2)}) %copy-start.5) | copy-done | bytes 1048600
  32.9 0.0 copy-done
  32.9 0.0 copy-done.3
  32.9 0.5 convolution_convert_fusion.2
  33.5 2.0 %convolution_convert_fusion.1 = bf16[256,256]{1,0:T(8,128)(2,1)S(1)} fusion(bf16[2048,256]{1,0:T(8,128)(2,1)} %param.21, bf16[256,2048]{1,0:T(8,128)(2,1)} %copy-done.5, f32[2048]{0:T(1024)S(1)} %copy-done.3, f32[256]{0:T(256)S(1)} %add_rsqrt_fusion.1), kind=kOutput, calls=%fused_computation.14 | convolution fusion | flops 270598144 | bytes 2237440 | tf_op jit(solution)/shard_map/dot_general | solution.py:244
  35.5 0.0 copy-start.2
  35.7 0.1 broadcast_select_fusion
  35.8 0.1 slice_bitcast_fusion
  35.9 4.7 %collective-permute-start.4 = (bf16[2,128,256]{2,1,0:T(8,128)(2,1)S(1)}, bf16[2,128,256]{2,1,0:T(8,128)(2,1)S(1)}, u32[]{:S(2)}, u32[]{:S(2)}) collective-permute-start(bf16[2,128,256]{2,1,0:T(8,128)(2,1)S(1)} %get-tuple-element.10), channel_id=1, source_target_pairs={{0,2},{1,3},{2,4},{3,5},{4,6},{5,7},{8,10},{9,11},{10,12},{11,13},... | collective-permute-start | bytes 393224 | tf_op jit(solution)/shard_map/ppermute | solution.py:177
  40.6 1.9 %collective-permute-start.5 = (bf16[2,128,256]{2,1,0:T(8,128)(2,1)S(1)}, bf16[2,128,256]{2,1,0:T(8,128)(2,1)S(1)}, u32[]{:S(2)}, u32[]{:S(2)}) collective-permute-start(bf16[2,128,256]{2,1,0:T(8,128)(2,1)S(1)} %get-tuple-element.9), channel_id=1, source_target_pairs={{0,3},{1,4},{2,5},{3,6},{4,7},{8,11},{9,12},{10,13},{11,14},{12,15... | collective-permute-start | bytes 393224 | tf_op jit(solution)/shard_map/ppermute | solution.py:177
  42.5 0.0 copy-done.2
  42.5 0.1 reshape.86.pat_ref
  42.6 1.3 %collective-permute-start.6 = (bf16[2,128,256]{2,1,0:T(8,128)(2,1)S(1)}, bf16[2,128,256]{2,1,0:T(8,128)(2,1)S(1)}, u32[]{:S(2)}, u32[]{:S(2)}) collective-permute-start(bf16[2,128,256]{2,1,0:T(8,128)(2,1)S(1)} %get-tuple-element.8), channel_id=1, source_target_pairs={{0,4},{1,5},{2,6},{3,7},{8,12},{9,13},{10,14},{11,15},{16,20},{17,... | collective-permute-start | bytes 393224 | tf_op jit(solution)/shard_map/ppermute | solution.py:177
  43.9 0.7 collective-permute-start.7
  44.6 0.7 collective-permute-start.8
  45.3 0.0 collective-permute-done.4.refs_2_
  45.3 0.7 collective-permute-start.9
  46.0 1.9 %collective-permute-done.5.refs_3_ = bf16[2,128,256]{2,1,0:T(8,128)(2,1)S(1)} collective-permute-done((bf16[2,128,256]{2,1,0:T(8,128)(2,1)S(1)}, bf16[2,128,256]{2,1,0:T(8,128)(2,1)S(1)}, u32[]{:S(2)}, u32[]{:S(2)}) %collective-permute-start.5) | collective-permute-done | bytes 131104 | tf_op jit(solution)/shard_map/ppermute | solution.py:177
  47.9 1.9 %collective-permute-start.3 = (bf16[2,256,256]{2,1,0:T(8,128)(2,1)S(1)}, bf16[2,256,256]{2,1,0:T(8,128)(2,1)S(1)}, u32[]{:S(2)}, u32[]{:S(2)}) collective-permute-start(bf16[2,256,256]{2,1,0:T(8,128)(2,1)S(1)} %bitcast.58), channel_id=1, source_target_pairs={{0,1},{1,2},{2,3},{3,4},{4,5},{5,6},{6,7},{8,9},{9,10},{10,11},{11... | collective-permute-start | bytes 786440 | tf_op jit(solution)/shard_map/ppermute | solution.py:161
  49.8 3.8 %convolution_convert_fusion.q_ref = bf16[256,1024]{1,0:T(8,128)(2,1)S(1)} fusion(bf16[2048,1024]{1,0:T(8,128)(2,1)} %param.19, bf16[256,2048]{1,0:T(8,128)(2,1)} %copy-done.5, f32[2048]{0:T(1024)S(1)} %copy-done.3, f32[256]{0:T(256)S(1)} %add_rsqrt_fusion.1), kind=kOutput, calls=%fused_computation.13 | convolution fusion | flops 1076101120 | bytes 5776384 | tf_op jit(solution)/shard_map/dot_general | solution.py:252
  53.6 0.0 collective-permute-done.6.refs_4_
  53.6 0.0 collective-permute-done.7.refs_5_
  53.6 0.0 collective-permute-done.8.refs_6_
  53.6 0.0 collective-permute-done.9.refs_7_
  53.6 10.4 %collective-permute-done.3.refs_1_ = bf16[2,256,256]{2,1,0:T(8,128)(2,1)S(1)} collective-permute-done((bf16[2,256,256]{2,1,0:T(8,128)(2,1)S(1)}, bf16[2,256,256]{2,1,0:T(8,128)(2,1)S(1)}, u32[]{:S(2)}, u32[]{:S(2)}) %collective-permute-start.3) | collective-permute-done | bytes 262176 | tf_op jit(solution)/shard_map/ppermute | solution.py:161
  64.0 12.8 %shard_map.118 = bf16[256,1024]{1,0:T(8,128)(2,1)} custom-call(s32[576]{0:T(1024)S(1)} %reshape.86.pat_ref, s32[1]{0:T(128)} %bitcast.pos_ref, bf16[256,1024]{1,0:T(8,128)(2,1)S(1)} %convolution_convert_fusion.q_ref, bf16[2,256,256]{2,1,0:T(8,128)(2,1)S(1)} %bitcast.59, bf16[2,256,256]{2,1,0:T(8,128)(2,1)S(1)} %collective-permute-done.3.refs_1_, ...), custom_call_target="tpu_custom_call" | custom-call | flops 1342177280 | bytes 3670016 | tf_op jit(solution)/shard_map/pallas_call | solution.py:142
  (15 shorter events, 0.3 us)
Async XLA Ops:
  0.0 32.9 %copy-start = (bf16[2048,256]{1,0:T(8,128)(2,1)S(1)}, bf16[2048,256]{1,0:T(8,128)(2,1)}, u32[]{:S(2)}) copy-start(bf16[2048,256]{1,0:T(8,128)(2,1)} %param.20) | copy-start | bytes 3145732
  0.0 16.8 %copy-start.1 = (bf16[256,1024]{1,0:T(8,128)(2,1)S(1)}, bf16[256,1024]{1,0:T(8,128)(2,1)}, u32[]{:S(2)}) copy-start(bf16[256,1024]{1,0:T(8,128)(2,1)} %param.13) | copy-start | bytes 1572868
  2.3 6.3 %collective-permute-start = (f32[2,128,128]{2,1,0:T(8,128)S(1)}, f32[2,128,128]{2,1,0:T(8,128)S(1)}, u32[]{:S(2)}, u32[]{:S(2)}) collective-permute-start(f32[2,128,128]{2,1,0:T(8,128)S(1)} %get-tuple-element.13), channel_id=1, source_target_pairs={{0,1},{1,2},{2,3},{3,4},{4,5},{5,6},{6,7},{8,9},{9,10},{10,11},{11... | collective-permute-start | bytes 393224 | tf_op jit(solution)/shard_map/ppermute | solution.py:27
  8.6 6.9 %collective-permute-start.1 = (f32[2,128,128]{2,1,0:T(8,128)S(1)}, f32[2,128,128]{2,1,0:T(8,128)S(1)}, u32[]{:S(2)}, u32[]{:S(2)}) collective-permute-start(f32[2,128,128]{2,1,0:T(8,128)S(1)} %add.60), channel_id=1, source_target_pairs={{0,2},{1,3},{2,4},{3,5},{4,6},{5,7},{8,10},{9,11},{10,12},{11,13},... | collective-permute-start | bytes 393224 | tf_op jit(solution)/shard_map/ppermute | solution.py:27
  15.4 7.9 %collective-permute-start.2 = (f32[2,128,128]{2,1,0:T(8,128)S(1)}, f32[2,128,128]{2,1,0:T(8,128)S(1)}, u32[]{:S(2)}, u32[]{:S(2)}) collective-permute-start(f32[2,128,128]{2,1,0:T(8,128)S(1)} %add.62), channel_id=1, source_target_pairs={{0,4},{1,5},{2,6},{3,7},{8,12},{9,13},{10,14},{11,15},{16,20},{17,... | collective-permute-start | bytes 393224 | tf_op jit(solution)/shard_map/ppermute | solution.py:27
  27.1 0.9 %copy-start.4 = (f32[1024]{0:T(1024)S(1)}, f32[1024]{0:T(1024)}, u32[]{:S(2)}) copy-start(f32[1024]{0:T(1024)} %param.16) | copy-start | bytes 12292
  28.0 4.9 %copy-start.3 = (f32[2048]{0:T(1024)S(1)}, f32[2048]{0:T(1024)}, u32[]{:S(2)}) copy-start(f32[2048]{0:T(1024)} %param.18) | copy-start | bytes 24580
  31.9 1.0 %copy-start.5 = (bf16[256,2048]{1,0:T(8,128)(2,1)}, bf16[256,2048]{1,0:T(8,128)(2,1)S(1)}, u32[]{:S(2)}) copy-start(bf16[256,2048]{1,0:T(8,128)(2,1)S(1)} %get-tuple-element.18) | copy-start | bytes 3145732
  35.5 7.0 %copy-start.2 = (s32[2,16,18]{2,1,0:T(8,128)S(1)}, s32[2,16,18]{2,1,0:T(8,128)}, u32[]{:S(2)}) copy-start(s32[2,16,18]{2,1,0:T(8,128)} %param.22) | copy-start | bytes 6916
  35.9 9.4 %collective-permute-start.4 = (bf16[2,128,256]{2,1,0:T(8,128)(2,1)S(1)}, bf16[2,128,256]{2,1,0:T(8,128)(2,1)S(1)}, u32[]{:S(2)}, u32[]{:S(2)}) collective-permute-start(bf16[2,128,256]{2,1,0:T(8,128)(2,1)S(1)} %get-tuple-element.10), channel_id=1, source_target_pairs={{0,2},{1,3},{2,4},{3,5},{4,6},{5,7},{8,10},{9,11},{10,12},{11,13},... | collective-permute-start | bytes 393224 | tf_op jit(solution)/shard_map/ppermute | solution.py:177
  40.6 7.3 %collective-permute-start.5 = (bf16[2,128,256]{2,1,0:T(8,128)(2,1)S(1)}, bf16[2,128,256]{2,1,0:T(8,128)(2,1)S(1)}, u32[]{:S(2)}, u32[]{:S(2)}) collective-permute-start(bf16[2,128,256]{2,1,0:T(8,128)(2,1)S(1)} %get-tuple-element.9), channel_id=1, source_target_pairs={{0,3},{1,4},{2,5},{3,6},{4,7},{8,11},{9,12},{10,13},{11,14},{12,15... | collective-permute-start | bytes 393224 | tf_op jit(solution)/shard_map/ppermute | solution.py:177
  42.6 11.0 %collective-permute-start.6 = (bf16[2,128,256]{2,1,0:T(8,128)(2,1)S(1)}, bf16[2,128,256]{2,1,0:T(8,128)(2,1)S(1)}, u32[]{:S(2)}, u32[]{:S(2)}) collective-permute-start(bf16[2,128,256]{2,1,0:T(8,128)(2,1)S(1)} %get-tuple-element.8), channel_id=1, source_target_pairs={{0,4},{1,5},{2,6},{3,7},{8,12},{9,13},{10,14},{11,15},{16,20},{17,... | collective-permute-start | bytes 393224 | tf_op jit(solution)/shard_map/ppermute | solution.py:177
  43.9 9.7 %collective-permute-start.7 = (bf16[2,128,256]{2,1,0:T(8,128)(2,1)S(1)}, bf16[2,128,256]{2,1,0:T(8,128)(2,1)S(1)}, u32[]{:S(2)}, u32[]{:S(2)}) collective-permute-start(bf16[2,128,256]{2,1,0:T(8,128)(2,1)S(1)} %get-tuple-element.7), channel_id=1, source_target_pairs={{0,5},{1,6},{2,7},{8,13},{9,14},{10,15},{16,21},{17,22},{18,23},{2... | collective-permute-start | bytes 393224 | tf_op jit(solution)/shard_map/ppermute | solution.py:177
  44.6 9.0 %collective-permute-start.8 = (bf16[2,128,256]{2,1,0:T(8,128)(2,1)S(1)}, bf16[2,128,256]{2,1,0:T(8,128)(2,1)S(1)}, u32[]{:S(2)}, u32[]{:S(2)}) collective-permute-start(bf16[2,128,256]{2,1,0:T(8,128)(2,1)S(1)} %get-tuple-element.6), channel_id=1, source_target_pairs={{0,6},{1,7},{8,14},{9,15},{16,22},{17,23},{24,30},{25,31}} | collective-permute-start | bytes 393224 | tf_op jit(solution)/shard_map/ppermute | solution.py:177
  45.3 8.3 %collective-permute-start.9 = (bf16[2,128,256]{2,1,0:T(8,128)(2,1)S(1)}, bf16[2,128,256]{2,1,0:T(8,128)(2,1)S(1)}, u32[]{:S(2)}, u32[]{:S(2)}) collective-permute-start(bf16[2,128,256]{2,1,0:T(8,128)(2,1)S(1)} %get-tuple-element.5), channel_id=1, source_target_pairs={{0,7},{8,15},{16,23},{24,31}} | collective-permute-start | bytes 393224 | tf_op jit(solution)/shard_map/ppermute | solution.py:177
  47.9 16.2 %collective-permute-start.3 = (bf16[2,256,256]{2,1,0:T(8,128)(2,1)S(1)}, bf16[2,256,256]{2,1,0:T(8,128)(2,1)S(1)}, u32[]{:S(2)}, u32[]{:S(2)}) collective-permute-start(bf16[2,256,256]{2,1,0:T(8,128)(2,1)S(1)} %bitcast.58), channel_id=1, source_target_pairs={{0,1},{1,2},{2,3},{3,4},{4,5},{5,6},{6,7},{8,9},{9,10},{10,11},{11... | collective-permute-start | bytes 786440 | tf_op jit(solution)/shard_map/ppermute | solution.py:161

commit v7 on v6

--- a/solution.py
+++ b/solution.py
@@ -150,11 +150,76 @@
     )(pattern.reshape(-1), position.reshape(1).astype(jnp.int32), soft_query, *pieces)
 
 
-def exchange_kv(packed, pattern, position, devices):
-    tok_count = packed.shape[0]
+def post_mix_kernel(
+    mixed_ref, lin_gain_ref, lin_out_ref, hidden_ref, soft_gain_ref, wk_ref, wv_ref, wq_ref,
+    kv_ref, q_ref, normed_ref,
+):
+    for h in range(HEADS):
+        part = mixed_ref[:, h * HEAD_DIM:(h + 1) * HEAD_DIM]
+        power = jnp.mean(part * part, axis=-1, keepdims=True)
+        gain = lin_gain_ref[:, h * HEAD_DIM:(h + 1) * HEAD_DIM]
+        normed_ref[:, h * HEAD_DIM:(h + 1) * HEAD_DIM] = (
+            part * lax.rsqrt(power + EPSILON) * gain
+        ).astype(jnp.bfloat16)
+    branch = jnp.dot(normed_ref[...], lin_out_ref[...], preferred_element_type=jnp.float32)
+    residual = (hidden_ref[...].astype(jnp.float32) + branch).astype(jnp.bfloat16)
+    widened = residual.astype(jnp.float32)
+    power = jnp.mean(widened * widened, axis=-1, keepdims=True)
+    layer_in = (widened * lax.rsqrt(power + EPSILON) * soft_gain_ref[...]).astype(jnp.bfloat16)
+    keys = jnp.dot(layer_in, wk_ref[...], preferred_element_type=jnp.float32).astype(jnp.bfloat16)
+    values = jnp.dot(layer_in, wv_ref[...], preferred_element_type=jnp.float32).astype(jnp.bfloat16)
+    for g in range(KV_HEADS):
+        kv_ref[g, :, :HEAD_DIM] = keys[:, g * HEAD_DIM:(g + 1) * HEAD_DIM]
+        kv_ref[g, :, HEAD_DIM:] = values[:, g * HEAD_DIM:(g + 1) * HEAD_DIM]
+    q_ref[...] = jnp.dot(layer_in, wq_ref[...], preferred_element_type=jnp.float32).astype(jnp.bfloat16)
+
+
+def post_mix(mixed, lin_gain, lin_out_weight, hidden_in, soft_gain, soft_wk, soft_wv, soft_wq):
+    tok_count, width = mixed.shape
+    model = hidden_in.shape[1]
+    steps = tok_count // BLOCK
+    whole = lambda i: (0, 0)
+    flops = 2 * tok_count * (width * model + model * (soft_wk.shape[1] + soft_wv.shape[1] + soft_wq.shape[1]))
+    bytes_accessed = 4 * mixed.size + 2 * (lin_out_weight.size + hidden_in.size + soft_wk.size + soft_wv.size + soft_wq.size)
+    return pl.pallas_call(
+        post_mix_kernel,
+        out_shape=(
+            jax.ShapeDtypeStruct((KV_HEADS, tok_count, 2 * HEAD_DIM), jnp.bfloat16),
+            jax.ShapeDtypeStruct((tok_count, soft_wq.shape[1]), jnp.bfloat16),
+        ),
+        grid=(steps,),
+        in_specs=[
+            pl.BlockSpec((BLOCK, width), lambda i: (i, 0)),
+            pl.BlockSpec((1, width), whole),
+            pl.BlockSpec(lin_out_weight.shape, whole),
+            pl.BlockSpec((BLOCK, model), lambda i: (i, 0)),
+            pl.BlockSpec((1, model), whole),
+            pl.BlockSpec(soft_wk.shape, whole),
+            pl.BlockSpec(soft_wv.shape, whole),
+            pl.BlockSpec(soft_wq.shape, whole),
+        ],
+        out_specs=(
+            pl.BlockSpec((KV_HEADS, BLOCK, 2 * HEAD_DIM), lambda i: (0, i, 0)),
+            pl.BlockSpec((BLOCK, soft_wq.shape[1]), lambda i: (i, 0)),
+        ),
+        scratch_shapes=[pltpu.VMEM((BLOCK, width), jnp.bfloat16)],
+        compiler_params=pltpu.CompilerParams(vmem_limit_bytes=56 * 1024 * 1024),
+        cost_estimate=pl.CostEstimate(flops=flops, transcendentals=0, bytes_accessed=bytes_accessed),
+    )(
+        mixed,
+        lin_gain.reshape(1, -1),
+        lin_out_weight,
+        hidden_in,
+        soft_gain.reshape(1, -1),
+        soft_wk,
+        soft_wv,
+        soft_wq,
+    )
+
+
+def exchange_kv(per_head, pattern, position, devices):
+    tok_count = per_head.shape[1]
     local_blocks = tok_count // BLOCK
-    blocks = packed.reshape(local_blocks, BLOCK, KV_HEADS, 2 * HEAD_DIM)
-    per_head = jnp.transpose(blocks, (2, 0, 1, 3)).reshape(KV_HEADS, tok_count, 2 * HEAD_DIM)
     pieces = [per_head]
     if devices > 1:
         pairs = [(i, i + 1) for i in range(devices - 1)]
@@ -225,36 +290,16 @@
     intra = jnp.einsum(
         "ngpts,nsge->ntgpe", local_scores, value_blocks, preferred_element_type=jnp.float32
     )
-    mixed = (inter + intra).reshape(tok_count, HEADS, HEAD_DIM)
-    normed = (
-        mixed
-        * lax.rsqrt(jnp.mean(mixed * mixed, axis=-1, keepdims=True) + EPSILON)
-        * lin_gain.reshape(HEADS, HEAD_DIM)
-    )
-    normed = normed.reshape(tok_count, HEADS * HEAD_DIM).astype(jnp.bfloat16)
-    branch = jnp.dot(normed, lin_out_weight, preferred_element_type=jnp.float32)
-    residual = (hidden_in.astype(jnp.float32) + branch).astype(jnp.bfloat16)
-    widened = residual.astype(jnp.float32)
-    layer_in = (
-        widened
-        * lax.rsqrt(jnp.mean(widened * widened, axis=-1, keepdims=True) + EPSILON)
-        * soft_gain
-    ).astype(jnp.bfloat16)
-    soft_key = jnp.dot(layer_in, soft_wk, preferred_element_type=jnp.float32).astype(jnp.bfloat16)
-    soft_value = jnp.dot(layer_in, soft_wv, preferred_element_type=jnp.float32).astype(jnp.bfloat16)
-    packed = jnp.concatenate(
-        [
-            soft_key.reshape(tok_count, KV_HEADS, HEAD_DIM),
-            soft_value.reshape(tok_count, KV_HEADS, HEAD_DIM),
-        ],
-        axis=-1,
-    )
-    soft_query = jnp.dot(layer_in, soft_wq, preferred_element_type=jnp.float32).astype(jnp.bfloat16)
+    mixed = (inter + intra).reshape(tok_count, HEADS * HEAD_DIM)
+    per_head, soft_query = post_mix(
+        mixed, lin_gain, lin_out_weight, hidden_in, soft_gain, soft_wk, soft_wv, soft_wq
+    )
 
     exchange = devices <= EXCHANGE_MAX_DEVICES
     if exchange:
-        pieces = exchange_kv(packed, pattern, position, devices)
+        pieces = exchange_kv(per_head, pattern, position, devices)
     else:
+        packed = jnp.transpose(per_head, (1, 0, 2))
         whole = lax.all_gather(packed, "seq", axis=0, tiled=True)
         mine = lax.dynamic_slice_in_dim(pattern, position * local_blocks, local_blocks, 1)
         table = whole.reshape(-1, BLOCK, KV_HEADS, 2 * HEAD_DIM)

time: 77.3 us -> 80.4 us (1.040)
  the two profiles are of different devices: /device:TPU:16 before, /device:TPU:29 now
where the time goes in v7:
time: 80.4 us; the launch traced here: 79.8 us
  waiting for transfers between devices  33 us (41%)
  Pallas kernels  21.9 us (27%)
  starting transfers between devices  12.9 us (16%)
  local copies, waits for them, and re-layouts  8.33 us (10%)
  other arithmetic  2.15 us (3%)
  matrix products  1.33 us (2%)
    ppermute x6, waiting for transfers between devices, exchange_kv(): pieces.append(lax.ppermute(chosen[i], 'seq', pairs))  22.3 us
    pallas_call x1, Pallas kernels, attention(): pl.pallas_call(kernel, out_shape=jax.ShapeDtypeStruct(soft_query.shape, j...  12.9 us
    ppermute x3, waiting for transfers between devices, exclusive_prefix(): got = lax.ppermute(window, axis, pairs)  10.7 us
    pallas_call x1, Pallas kernels, post_mix(): pl.pallas_call(post_mix_kernel, out_shape=(jax.ShapeDtypeStruct((KV_HEADS...  9 us
    ppermute x6, starting transfers between devices, exchange_kv(): pieces.append(lax.ppermute(chosen[i], 'seq', pairs))  7.74 us
    ppermute x3, starting transfers between devices, exclusive_prefix(): got = lax.ppermute(window, axis, pairs)  3.88 us
    unnamed x6, local copies, waits for them, and re-layouts  1.99 us
  transfers between devices with their start and end apart: 10, of which 5 were waited for; matrix products, arithmetic and copies ran while one was open for 4% of the time, Pallas kernels for 0%

profile of v7, /device:TPU:29, one launch (start us, length us, event | category | flops | bytes accessed | tf_op | source)
XLA Modules:
  0.0 79.8 jit_solution(8068292404314177682)
XLA Ops:
  0.0 0.9 %reshape.55 = bf16[2,128,2,128]{3,2,1,0:T(2,128)(2,1)S(1)} reshape(bf16[256,256]{1,0:T(8,128)(2,1)} %param.14) | data formatting | bytes 262144 | tf_op jit(solution)/shard_map/reshape | solution.py:267
  0.9 0.9 %reshape.56 = bf16[2,128,2,128]{3,2,1,0:T(2,128)(2,1)S(1)} reshape(bf16[256,256]{1,0:T(8,128)(2,1)} %param.15) | data formatting | bytes 262144 | tf_op jit(solution)/shard_map/reshape | solution.py:268
  1.9 0.2 fusion.23
  2.1 1.3 %collective-permute-start = (f32[2,128,128]{2,1,0:T(8,128)S(1)}, f32[2,128,128]{2,1,0:T(8,128)S(1)}, u32[]{:S(2)}, u32[]{:S(2)}) collective-permute-start(f32[2,128,128]{2,1,0:T(8,128)S(1)} %get-tuple-element.17), channel_id=1, source_target_pairs={{0,1},{1,2},{2,3},{3,4},{4,5},{5,6},{6,7},{8,9},{9,10},{10,11},{11... | collective-permute-start | bytes 393224 | tf_op jit(solution)/shard_map/ppermute | solution.py:27
  3.4 0.7 broadcast_add_fusion
  4.1 0.1 iota_compare_fusion.1
  4.2 1.4 %collective-permute-done = f32[2,128,128]{2,1,0:T(8,128)S(1)} collective-permute-done((f32[2,128,128]{2,1,0:T(8,128)S(1)}, f32[2,128,128]{2,1,0:T(8,128)S(1)}, u32[]{:S(2)}, u32[]{:S(2)}) %collective-permute-start) | collective-permute-done | bytes 131104 | tf_op jit(solution)/shard_map/ppermute | solution.py:27
  5.6 1.3 %collective-permute-start.1 = (f32[2,128,128]{2,1,0:T(8,128)S(1)}, f32[2,128,128]{2,1,0:T(8,128)S(1)}, u32[]{:S(2)}, u32[]{:S(2)}) collective-permute-start(f32[2,128,128]{2,1,0:T(8,128)S(1)} %add.34), channel_id=1, source_target_pairs={{0,2},{1,3},{2,4},{3,5},{4,6},{5,7},{8,10},{9,11},{10,12},{11,13},... | collective-permute-start | bytes 393224 | tf_op jit(solution)/shard_map/ppermute | solution.py:27
  6.9 0.9 %select_reduce_fusion = s32[2,16]{1,0:T(2,128)S(1)} fusion(s32[2,16,18]{2,1,0:T(8,128)} %param.22, s32[]{:T(128)S(6)} %mul.3, s32[]{:T(128)} %axis_index.12), kind=kLoop, calls=%fused_computation.36 | loop fusion | flops 9696 | bytes 2184 | tf_op jit(solution)/shard_map/reduce_max | solution.py:232
  7.8 0.1 reduce_max.14
  7.9 0.1 reduce_max.18
  8.0 0.2 select_reduce_fusion.1
  8.2 4.1 %collective-permute-done.1 = f32[2,128,128]{2,1,0:T(8,128)S(1)} collective-permute-done((f32[2,128,128]{2,1,0:T(8,128)S(1)}, f32[2,128,128]{2,1,0:T(8,128)S(1)}, u32[]{:S(2)}, u32[]{:S(2)}) %collective-permute-start.1) | collective-permute-done | bytes 131104 | tf_op jit(solution)/shard_map/ppermute | solution.py:27
  12.3 1.3 %collective-permute-start.2 = (f32[2,128,128]{2,1,0:T(8,128)S(1)}, f32[2,128,128]{2,1,0:T(8,128)S(1)}, u32[]{:S(2)}, u32[]{:S(2)}) collective-permute-start(f32[2,128,128]{2,1,0:T(8,128)S(1)} %add.36), channel_id=1, source_target_pairs={{0,4},{1,5},{2,6},{3,7},{8,12},{9,13},{10,14},{11,15},{16,20},{17,... | collective-permute-start | bytes 393224 | tf_op jit(solution)/shard_map/ppermute | solution.py:27
  13.6 1.4 %reshape.57 = bf16[2,128,2,4,128]{4,3,2,1,0:T(4,128)(2,1)S(1)} reshape(bf16[256,1024]{1,0:T(8,128)(2,1)} %param.13) | data formatting | bytes 1048576 | tf_op jit(solution)/shard_map/reshape | solution.py:266
  15.1 5.3 %collective-permute-done.2 = f32[2,128,128]{2,1,0:T(8,128)S(1)} collective-permute-done((f32[2,128,128]{2,1,0:T(8,128)S(1)}, f32[2,128,128]{2,1,0:T(8,128)S(1)}, u32[]{:S(2)}, u32[]{:S(2)}) %collective-permute-start.2) | collective-permute-done | bytes 131104 | tf_op jit(solution)/shard_map/ppermute | solution.py:27
  20.3 0.6 convolution_bitcast_fusion.2
  21.0 0.5 fusion
  21.4 0.4 copy.40
  21.9 1.4 %reshape.58.mixed_ref = f32[256,1024]{1,0:T(8,128)} reshape(f32[2,128,2,4,128]{4,3,2,1,0:T(4,128)S(1)} %copy.40) | data formatting | bytes 2097152 | tf_op jit(solution)/shard_map/reshape | solution.py:293
  23.3 0.0 copy-start.2
  23.3 9.0 %shard_map.118 = (bf16[2,256,256]{2,1,0:T(8,128)(2,1)}, bf16[256,1024]{1,0:T(8,128)(2,1)}) custom-call(f32[256,1024]{1,0:T(8,128)} %reshape.58.mixed_ref, f32[1,1024]{1,0:T(1,128)} %bitcast.49, bf16[1024,2048]{1,0:T(8,128)(2,1)} %lin_out_ref.1, bf16[256,2048]{1,0:T(8,128)(2,1)} %hidden_ref.1, f32[1,2048]{1,0:T(1,128)} %bitcast.48, bf16[2048,256]{1,0:T(8,128)(2,1)} %wk_ref.1, ...), custom_call_target="tpu_custom_call" | custom-call | flops 2684354560 | bytes 12582912 | tf_op jit(solution)/shard_map/pallas_call | solution.py:184
  32.3 1.0 %slice_bitcast_fusion.7 = (bf16[2,128,256]{2,1,0:T(8,128)(2,1)S(1)}, bf16[2,128,256]{2,1,0:T(8,128)(2,1)S(1)}) fusion(bf16[2,2,128,256]{3,2,1,0:T(8,128)(2,1)} %bitcast.45), kind=kLoop, calls=%fused_computation.21 | loop fusion | bytes 524288 | tf_op jit(solution)/shard_map/jit(_where)/broadcast_in_dim | solution.py:239
  33.3 0.1 broadcast_select_fusion
  33.4 0.1 slice_bitcast_fusion
  33.5 1.3 %collective-permute-start.4 = (bf16[2,128,256]{2,1,0:T(8,128)(2,1)S(1)}, bf16[2,128,256]{2,1,0:T(8,128)(2,1)S(1)}, u32[]{:S(2)}, u32[]{:S(2)}) collective-permute-start(bf16[2,128,256]{2,1,0:T(8,128)(2,1)S(1)} %get-tuple-element.14), channel_id=1, source_target_pairs={{0,2},{1,3},{2,4},{3,5},{4,6},{5,7},{8,10},{9,11},{10,12},{11,13},... | collective-permute-start | bytes 393224 | tf_op jit(solution)/shard_map/ppermute | solution.py:242
  34.8 1.3 %collective-permute-start.5 = (bf16[2,128,256]{2,1,0:T(8,128)(2,1)S(1)}, bf16[2,128,256]{2,1,0:T(8,128)(2,1)S(1)}, u32[]{:S(2)}, u32[]{:S(2)}) collective-permute-start(bf16[2,128,256]{2,1,0:T(8,128)(2,1)S(1)} %get-tuple-element.13), channel_id=1, source_target_pairs={{0,3},{1,4},{2,5},{3,6},{4,7},{8,11},{9,12},{10,13},{11,14},{12,15... | collective-permute-start | bytes 393224 | tf_op jit(solution)/shard_map/ppermute | solution.py:242
  36.1 1.3 %collective-permute-start.3 = (bf16[2,256,256]{2,1,0:T(8,128)(2,1)}, bf16[2,256,256]{2,1,0:T(8,128)(2,1)S(1)}, u32[]{:S(2)}, u32[]{:S(2)}) collective-permute-start(bf16[2,256,256]{2,1,0:T(8,128)(2,1)} %get-tuple-element.8.refs_0_), channel_id=1, source_target_pairs={{0,1},{1,2},{2,3},{3,4},{4,5},{5,6},{6,7},{8,9},{9,10},{10,11},{11... | collective-permute-start | bytes 786440 | tf_op jit(solution)/shard_map/ppermute | solution.py:226
  37.4 1.3 %collective-permute-start.6 = (bf16[2,128,256]{2,1,0:T(8,128)(2,1)S(1)}, bf16[2,128,256]{2,1,0:T(8,128)(2,1)S(1)}, u32[]{:S(2)}, u32[]{:S(2)}) collective-permute-start(bf16[2,128,256]{2,1,0:T(8,128)(2,1)S(1)} %get-tuple-element.12), channel_id=1, source_target_pairs={{0,4},{1,5},{2,6},{3,7},{8,12},{9,13},{10,14},{11,15},{16,20},{17,... | collective-permute-start | bytes 393224 | tf_op jit(solution)/shard_map/ppermute | solution.py:242
  38.7 1.3 %collective-permute-start.7 = (bf16[2,128,256]{2,1,0:T(8,128)(2,1)S(1)}, bf16[2,128,256]{2,1,0:T(8,128)(2,1)S(1)}, u32[]{:S(2)}, u32[]{:S(2)}) collective-permute-start(bf16[2,128,256]{2,1,0:T(8,128)(2,1)S(1)} %get-tuple-element.11), channel_id=1, source_target_pairs={{0,5},{1,6},{2,7},{8,13},{9,14},{10,15},{16,21},{17,22},{18,23},{2... | collective-permute-start | bytes 393224 | tf_op jit(solution)/shard_map/ppermute | solution.py:242
  40.0 0.0 collective-permute-done.4.refs_2_
  40.0 1.3 %collective-permute-start.8 = (bf16[2,128,256]{2,1,0:T(8,128)(2,1)S(1)}, bf16[2,128,256]{2,1,0:T(8,128)(2,1)S(1)}, u32[]{:S(2)}, u32[]{:S(2)}) collective-permute-start(bf16[2,128,256]{2,1,0:T(8,128)(2,1)S(1)} %get-tuple-element.10), channel_id=1, source_target_pairs={{0,6},{1,7},{8,14},{9,15},{16,22},{17,23},{24,30},{25,31}} | collective-permute-start | bytes 393224 | tf_op jit(solution)/shard_map/ppermute | solution.py:242
  41.3 8.1 %collective-permute-done.5.refs_3_ = bf16[2,128,256]{2,1,0:T(8,128)(2,1)S(1)} collective-permute-done((bf16[2,128,256]{2,1,0:T(8,128)(2,1)S(1)}, bf16[2,128,256]{2,1,0:T(8,128)(2,1)S(1)}, u32[]{:S(2)}, u32[]{:S(2)}) %collective-permute-start.5) | collective-permute-done | bytes 131104 | tf_op jit(solution)/shard_map/ppermute | solution.py:242
  49.4 1.3 %collective-permute-start.9 = (bf16[2,128,256]{2,1,0:T(8,128)(2,1)S(1)}, bf16[2,128,256]{2,1,0:T(8,128)(2,1)S(1)}, u32[]{:S(2)}, u32[]{:S(2)}) collective-permute-start(bf16[2,128,256]{2,1,0:T(8,128)(2,1)S(1)} %get-tuple-element.9), channel_id=1, source_target_pairs={{0,7},{8,15},{16,23},{24,31}} | collective-permute-start | bytes 393224 | tf_op jit(solution)/shard_map/ppermute | solution.py:242
  50.6 0.0 copy-done.2
  50.7 0.1 reshape.53.pat_ref
  50.8 14.2 %collective-permute-done.6.refs_4_ = bf16[2,128,256]{2,1,0:T(8,128)(2,1)S(1)} collective-permute-done((bf16[2,128,256]{2,1,0:T(8,128)(2,1)S(1)}, bf16[2,128,256]{2,1,0:T(8,128)(2,1)S(1)}, u32[]{:S(2)}, u32[]{:S(2)}) %collective-permute-start.6) | collective-permute-done | bytes 131104 | tf_op jit(solution)/shard_map/ppermute | solution.py:242
  64.9 0.0 collective-permute-done.7.refs_5_
  64.9 0.0 collective-permute-done.8.refs_6_
  64.9 0.0 collective-permute-done.9.refs_7_
  64.9 0.0 collective-permute-done.3.refs_1_
  65.0 0.0 copy-start
  65.0 0.9 %copy-done = bf16[2,256,256]{2,1,0:T(8,128)(2,1)S(1)} copy-done((bf16[2,256,256]{2,1,0:T(8,128)(2,1)S(1)}, bf16[2,256,256]{2,1,0:T(8,128)(2,1)}, u32[]{:S(2)}) %copy-start) | copy-done | bytes 262168
  65.9 0.0 copy-start.1
  65.9 1.0 %copy-done.1 = bf16[256,1024]{1,0:T(8,128)(2,1)S(1)} copy-done((bf16[256,1024]{1,0:T(8,128)(2,1)S(1)}, bf16[256,1024]{1,0:T(8,128)(2,1)}, u32[]{:S(2)}) %copy-start.1) | copy-done | bytes 524312
  67.0 12.9 %shard_map.119 = bf16[256,1024]{1,0:T(8,128)(2,1)} custom-call(s32[576]{0:T(1024)S(1)} %reshape.53.pat_ref, s32[1]{0:T(128)} %bitcast.pos_ref, bf16[256,1024]{1,0:T(8,128)(2,1)S(1)} %copy-done.1, bf16[2,256,256]{2,1,0:T(8,128)(2,1)S(1)} %copy-done, bf16[2,256,256]{2,1,0:T(8,128)(2,1)S(1)} %collective-permute-done.3.refs_1_, ...), custom_call_target="tpu_custom_call" | custom-call | flops 1342177280 | bytes 3670016 | tf_op jit(solution)/shard_map/pallas_call | solution.py:142
  (6 shorter events, 0.1 us)
Async XLA Ops:
  2.1 3.4 %collective-permute-start = (f32[2,128,128]{2,1,0:T(8,128)S(1)}, f32[2,128,128]{2,1,0:T(8,128)S(1)}, u32[]{:S(2)}, u32[]{:S(2)}) collective-permute-start(f32[2,128,128]{2,1,0:T(8,128)S(1)} %get-tuple-element.17), channel_id=1, source_target_pairs={{0,1},{1,2},{2,3},{3,4},{4,5},{5,6},{6,7},{8,9},{9,10},{10,11},{11... | collective-permute-start | bytes 393224 | tf_op jit(solution)/shard_map/ppermute | solution.py:27
  5.6 6.7 %collective-permute-start.1 = (f32[2,128,128]{2,1,0:T(8,128)S(1)}, f32[2,128,128]{2,1,0:T(8,128)S(1)}, u32[]{:S(2)}, u32[]{:S(2)}) collective-permute-start(f32[2,128,128]{2,1,0:T(8,128)S(1)} %add.34), channel_id=1, source_target_pairs={{0,2},{1,3},{2,4},{3,5},{4,6},{5,7},{8,10},{9,11},{10,12},{11,13},... | collective-permute-start | bytes 393224 | tf_op jit(solution)/shard_map/ppermute | solution.py:27
  12.3 8.0 %collective-permute-start.2 = (f32[2,128,128]{2,1,0:T(8,128)S(1)}, f32[2,128,128]{2,1,0:T(8,128)S(1)}, u32[]{:S(2)}, u32[]{:S(2)}) collective-permute-start(f32[2,128,128]{2,1,0:T(8,128)S(1)} %add.36), channel_id=1, source_target_pairs={{0,4},{1,5},{2,6},{3,7},{8,12},{9,13},{10,14},{11,15},{16,20},{17,... | collective-permute-start | bytes 393224 | tf_op jit(solution)/shard_map/ppermute | solution.py:27
  23.3 27.4 %copy-start.2 = (s32[2,16,18]{2,1,0:T(8,128)S(1)}, s32[2,16,18]{2,1,0:T(8,128)}, u32[]{:S(2)}) copy-start(s32[2,16,18]{2,1,0:T(8,128)} %param.22) | copy-start | bytes 6916
  33.5 6.5 %collective-permute-start.4 = (bf16[2,128,256]{2,1,0:T(8,128)(2,1)S(1)}, bf16[2,128,256]{2,1,0:T(8,128)(2,1)S(1)}, u32[]{:S(2)}, u32[]{:S(2)}) collective-permute-start(bf16[2,128,256]{2,1,0:T(8,128)(2,1)S(1)} %get-tuple-element.14), channel_id=1, source_target_pairs={{0,2},{1,3},{2,4},{3,5},{4,6},{5,7},{8,10},{9,11},{10,12},{11,13},... | collective-permute-start | bytes 393224 | tf_op jit(solution)/shard_map/ppermute | solution.py:242
  34.8 14.6 %collective-permute-start.5 = (bf16[2,128,256]{2,1,0:T(8,128)(2,1)S(1)}, bf16[2,128,256]{2,1,0:T(8,128)(2,1)S(1)}, u32[]{:S(2)}, u32[]{:S(2)}) collective-permute-start(bf16[2,128,256]{2,1,0:T(8,128)(2,1)S(1)} %get-tuple-element.13), channel_id=1, source_target_pairs={{0,3},{1,4},{2,5},{3,6},{4,7},{8,11},{9,12},{10,13},{11,14},{12,15... | collective-permute-start | bytes 393224 | tf_op jit(solution)/shard_map/ppermute | solution.py:242
  36.1 28.9 %collective-permute-start.3 = (bf16[2,256,256]{2,1,0:T(8,128)(2,1)}, bf16[2,256,256]{2,1,0:T(8,128)(2,1)S(1)}, u32[]{:S(2)}, u32[]{:S(2)}) collective-permute-start(bf16[2,256,256]{2,1,0:T(8,128)(2,1)} %get-tuple-element.8.refs_0_), channel_id=1, source_target_pairs={{0,1},{1,2},{2,3},{3,4},{4,5},{5,6},{6,7},{8,9},{9,10},{10,11},{11... | collective-permute-start | bytes 786440 | tf_op jit(solution)/shard_map/ppermute | solution.py:226
  37.4 27.6 %collective-permute-start.6 = (bf16[2,128,256]{2,1,0:T(8,128)(2,1)S(1)}, bf16[2,128,256]{2,1,0:T(8,128)(2,1)S(1)}, u32[]{:S(2)}, u32[]{:S(2)}) collective-permute-start(bf16[2,128,256]{2,1,0:T(8,128)(2,1)S(1)} %get-tuple-element.12), channel_id=1, source_target_pairs={{0,4},{1,5},{2,6},{3,7},{8,12},{9,13},{10,14},{11,15},{16,20},{17,... | collective-permute-start | bytes 393224 | tf_op jit(solution)/shard_map/ppermute | solution.py:242
  38.7 26.3 %collective-permute-start.7 = (bf16[2,128,256]{2,1,0:T(8,128)(2,1)S(1)}, bf16[2,128,256]{2,1,0:T(8,128)(2,1)S(1)}, u32[]{:S(2)}, u32[]{:S(2)}) collective-permute-start(bf16[2,128,256]{2,1,0:T(8,128)(2,1)S(1)} %get-tuple-element.11), channel_id=1, source_target_pairs={{0,5},{1,6},{2,7},{8,13},{9,14},{10,15},{16,21},{17,22},{18,23},{2... | collective-permute-start | bytes 393224 | tf_op jit(solution)/shard_map/ppermute | solution.py:242
  40.0 25.0 %collective-permute-start.8 = (bf16[2,128,256]{2,1,0:T(8,128)(2,1)S(1)}, bf16[2,128,256]{2,1,0:T(8,128)(2,1)S(1)}, u32[]{:S(2)}, u32[]{:S(2)}) collective-permute-start(bf16[2,128,256]{2,1,0:T(8,128)(2,1)S(1)} %get-tuple-element.10), channel_id=1, source_target_pairs={{0,6},{1,7},{8,14},{9,15},{16,22},{17,23},{24,30},{25,31}} | collective-permute-start | bytes 393224 | tf_op jit(solution)/shard_map/ppermute | solution.py:242
  49.4 15.6 %collective-permute-start.9 = (bf16[2,128,256]{2,1,0:T(8,128)(2,1)S(1)}, bf16[2,128,256]{2,1,0:T(8,128)(2,1)S(1)}, u32[]{:S(2)}, u32[]{:S(2)}) collective-permute-start(bf16[2,128,256]{2,1,0:T(8,128)(2,1)S(1)} %get-tuple-element.9), channel_id=1, source_target_pairs={{0,7},{8,15},{16,23},{24,31}} | collective-permute-start | bytes 393224 | tf_op jit(solution)/shard_map/ppermute | solution.py:242
  65.0 1.0 %copy-start = (bf16[2,256,256]{2,1,0:T(8,128)(2,1)S(1)}, bf16[2,256,256]{2,1,0:T(8,128)(2,1)}, u32[]{:S(2)}) copy-start(bf16[2,256,256]{2,1,0:T(8,128)(2,1)} %get-tuple-element.8.refs_0_) | copy-start | bytes 786436
  65.9 1.0 %copy-start.1 = (bf16[256,1024]{1,0:T(8,128)(2,1)S(1)}, bf16[256,1024]{1,0:T(8,128)(2,1)}, u32[]{:S(2)}) copy-start(bf16[256,1024]{1,0:T(8,128)(2,1)} %get-tuple-element.7.q_ref) | copy-start | bytes 1572868
